TPU v7x, 512 devices: a whole 4x4x16 slice. The times are simulated.
512 devices in a mesh: expert: 32 (over x, y, core), replica: 16 (over z).
Axes of the slice: x: 4, y: 4, z: 16, core: 2. Of those that a mesh axis runs over, the one named last changes fastest.
Arguments:
- tokens: bfloat16 [65536, 2560], P(('expert', 'replica')), may hold values from -6 to 6
- cotangent: bfloat16 [65536, 2560], P(('expert', 'replica')), may hold values from -4 to 4
- partner: int32 [65536, 1], P(('expert', 'replica')), may hold values from 0 to 31; in each aligned block of 128 rows (0 to 127, 128 to 255, ...) at most 5 rows name the same one
- combine: int32 [65536, 2], P(('expert', 'replica')), may hold values from 1 to 8
- counts: int32 [512], P(('expert', 'replica')), may hold values from 32 to 128, as said below
- w_gate: bfloat16 [32, 2560, 768], P('expert', 'replica'), may hold values from -0.125 to 0.125
- w_up: bfloat16 [32, 2560, 768], P('expert', 'replica'), may hold values from -0.125 to 0.125
- w_down: bfloat16 [32, 768, 2560], P('expert', 'replica'), may hold values from -0.21875 to 0.21875
Outputs:
- token_grad: bfloat16 [65536, 2560], P(('expert', 'replica'))
- grad_down: bfloat16 [32, 768, 2560], P('expert', 'replica')
Inputs may be any that keep to these rules, and one draw needn't show every extreme that they name: `partner`: within the 128 rows of one device no expert index is named by more than 5 rows, and some device names one exactly 5 times. `counts`: some device has all 128 slots real.
All inputs are finite; a program needn't handle non-finite values.
Results may differ from a plain program's by a relative error of at most 0.017.
Values may be sent and summed in bfloat16 or wider, within the bound.
No kernel may reach another device: no remote copies, remote signals or barrier semaphores. Data moves between devices by JAX's collectives and lax.ppermute only.
A program may use at most 64 MiB of HBM per device.

v0:
```python
import jax
import jax.numpy as jnp
from jax import lax
from jax.sharding import PartitionSpec as P


def against_rows(left, matrix):
    return lax.dot_general(
        left, matrix, (((1,), (1,)), ((), ())), preferred_element_type=jnp.float32
    )


def expert_backward(inputs, upstream, gate_w, up_w, down_w):
    gate_act = jnp.dot(inputs, gate_w, preferred_element_type=jnp.float32)
    up_act = jnp.dot(inputs, up_w, preferred_element_type=jnp.float32)
    sigmoid_gate = jax.nn.sigmoid(gate_act)
    swish_gate = gate_act * sigmoid_gate
    hidden = (swish_gate * up_act).astype(jnp.bfloat16)
    hidden_grad = against_rows(upstream, down_w)
    gate_grad = (
        hidden_grad * up_act * sigmoid_gate * (1.0 + gate_act * (1.0 - sigmoid_gate))
    ).astype(jnp.bfloat16)
    up_grad = (hidden_grad * swish_gate).astype(jnp.bfloat16)
    input_grad = against_rows(gate_grad, gate_w) + against_rows(up_grad, up_w)
    return (hidden, input_grad)


def local(tokens, cotangent, partner, combine, counts, w_gate, w_up, w_down):
    tok_rows = tokens.shape[0]
    width = tokens.shape[1]
    expert_count = lax.axis_size("expert")
    capacity = max(2, (5 * tok_rows // 4 + expert_count - 1) // expert_count)
    positions = jnp.arange(tok_rows, dtype=jnp.int32)
    valid_rows = positions < counts[0]
    weights = combine.astype(jnp.float32)
    weight_sum = weights[:, 0] + weights[:, 1]
    share_home = jnp.where(valid_rows, weights[:, 0] / weight_sum, 0.0)
    share_away = jnp.where(valid_rows, weights[:, 1] / weight_sum, 0.0)
    upstream = cotangent.astype(jnp.float32)
    q_home = (upstream * share_home[:, None]).astype(jnp.bfloat16)
    q_away = (upstream * share_away[:, None]).astype(jnp.bfloat16)
    gate_full, up_full, down_full = (
        lax.all_gather(w_gate, "replica", axis=1, tiled=True),
        lax.all_gather(w_up, "replica", axis=1, tiled=True),
        lax.all_gather(w_down, "replica", axis=1, tiled=True),
    )
    gate_w = gate_full.reshape(gate_full.shape[1], gate_full.shape[2])
    up_w = up_full.reshape(up_full.shape[1], up_full.shape[2])
    down_w = down_full.reshape(down_full.shape[1], down_full.shape[2])
    target = partner[:, 0]
    onehot_rows = (target[:, None] == jnp.arange(expert_count, dtype=jnp.int32)[None, :]).astype(
        jnp.int32
    )
    rank_within = jnp.sum((jnp.cumsum(onehot_rows, axis=0) - onehot_rows) * onehot_rows, axis=1)
    destination = target * capacity + rank_within
    placing = (
        jnp.arange(expert_count * capacity, dtype=jnp.int32)[:, None] == destination[None, :]
    ).astype(jnp.bfloat16)
    send_x = (
        jnp.dot(placing, tokens, preferred_element_type=jnp.float32)
        .astype(jnp.bfloat16)
        .reshape(expert_count, capacity, width)
    )
    send_q = (
        jnp.dot(placing, q_away, preferred_element_type=jnp.float32)
        .astype(jnp.bfloat16)
        .reshape(expert_count, capacity, width)
    )
    hidden_home, grad_home = expert_backward(tokens, q_home, gate_w, up_w, down_w)
    x_there = lax.all_to_all(send_x, "expert", split_axis=0, concat_axis=0, tiled=True)
    q_there = lax.all_to_all(send_q, "expert", split_axis=0, concat_axis=0, tiled=True)
    item_count = x_there.shape[1]
    hidden_there, grad_there = expert_backward(
        x_there.reshape(-1, width), q_there.reshape(-1, width), gate_w, up_w, down_w
    )
    returned = lax.all_to_all(
        grad_there.astype(jnp.bfloat16).reshape(expert_count, item_count, width),
        "expert",
        split_axis=0,
        concat_axis=0,
        tiled=True,
    )
    returned, hidden_away, q_there = (
        returned,
        hidden_there.reshape(expert_count, item_count, -1),
        q_there,
    )
    contract = (((0,), (0,)), ((), ()))
    flat_returned = returned.reshape(expert_count * capacity, width)
    grad_away = lax.dot_general(
        placing, flat_returned, contract, preferred_element_type=jnp.float32
    )
    token_grad = (grad_home + grad_away).astype(jnp.bfloat16)
    flat_hidden = hidden_away.reshape(expert_count * capacity, -1)
    flat_q = q_there.reshape(expert_count * capacity, width)
    grad_down = lax.psum_scatter(
        (
            lax.dot_general(hidden_home, q_home, contract, preferred_element_type=jnp.float32)
            + lax.dot_general(flat_hidden, flat_q, contract, preferred_element_type=jnp.float32)
        ).astype(jnp.bfloat16),
        "replica",
        scatter_dimension=0,
        tiled=True,
    )
    return (token_grad, grad_down[None])


def solution(mesh):
    placed = (
        P(("expert", "replica"), None),
        P(("expert", "replica"), None),
        P(("expert", "replica"), None),
        P(("expert", "replica"), None),
        P(("expert", "replica")),
        P("expert", "replica", None),
        P("expert", "replica", None),
        P("expert", "replica", None),
    )
    return jax.shard_map(
        local,
        mesh=mesh,
        in_specs=placed,
        out_specs=(P(("expert", "replica"), None), P("expert", "replica", None)),
        check_vma=False,
    )
```

profile of v0, /device:TPU:6, one launch (start us, length us, event | category | flops | bytes accessed | tf_op | source)
XLA Modules:
  0.0 331.7 jit_solution(12413700207397267182)
XLA Ops:
  13.1 1.5 convolution_convert_fusion.1
  15.9 9.6 %all-to-all-start = ((bf16[32,5,2560]{2,1,0:T(8,128)(2,1)}), bf16[32,5,2560]{2,1,0:T(8,128)(2,1)S(1)}, u32[]{:S(2)}, u32[]{:S(2)}) async-start(bf16[32,5,2560]{2,1,0:T(8,128)(2,1)} %reshape.51), calls=%async_computation | async-start | bytes 2621440 | tf_op jit(solution)/shard_map/all_to_all | solution.py:71
  25.9 1.3 reshape.53
  27.2 16.3 %all-to-all-done = bf16[32,5,2560]{2,1,0:T(8,128)(2,1)S(1)} async-done(((bf16[32,5,2560]{2,1,0:T(8,128)(2,1)}), bf16[32,5,2560]{2,1,0:T(8,128)(2,1)S(1)}, u32[]{:S(2)}, u32[]{:S(2)}) %all-to-all-start) | async-done | bytes 819232 | tf_op jit(solution)/shard_map/all_to_all | solution.py:71
  43.5 6.4 %all-to-all-start.1 = ((bf16[32,5,2560]{2,1,0:T(8,128)(2,1)}), bf16[32,5,2560]{2,1,0:T(8,128)(2,1)}, u32[]{:S(2)}, u32[]{:S(2)}) async-start(bf16[32,5,2560]{2,1,0:T(8,128)(2,1)} %reshape.53), calls=%async_computation.1 | async-start | bytes 2621440 | tf_op jit(solution)/shard_map/all_to_all | solution.py:70
  50.3 17.6 %all-to-all-done.1 = bf16[32,5,2560]{2,1,0:T(8,128)(2,1)} async-done(((bf16[32,5,2560]{2,1,0:T(8,128)(2,1)}), bf16[32,5,2560]{2,1,0:T(8,128)(2,1)}, u32[]{:S(2)}, u32[]{:S(2)}) %all-to-all-start.1) | async-done | bytes 819232 | tf_op jit(solution)/shard_map/all_to_all | solution.py:70
  68.0 1.5 reshape.54
  69.4 22.6 %all-gather.8.cloned.1.call-done = bf16[1,2560,768]{2,1,0:T(8,128)(2,1)} async-done(((bf16[1,160,768]{2,1,0:T(8,128)(2,1)}), bf16[1,2560,768]{2,1,0:T(8,128)(2,1)}) %all-gather.8.cloned.1.call-update) | async-done | bytes 3932176 | tf_op jit(solution)/shard_map/all_gather | solution.py:43
  92.0 2.8 fusion.6
  94.8 73.8 %all-gather.6.cloned.1.call-done = bf16[1,2560,768]{2,1,0:T(8,128)(2,1)} async-done(((bf16[1,160,768]{2,1,0:T(8,128)(2,1)}), bf16[1,2560,768]{2,1,0:T(8,128)(2,1)}) %all-gather.6.cloned.1.call-update) | async-done | bytes 3932176 | tf_op jit(solution)/shard_map/all_gather | solution.py:44
  168.6 2.9 fusion.14
  171.6 3.1 fusion.2
  177.0 3.2 add_convert_fusion
  180.3 64.9 %all-gather.4.cloned.1.call-done = bf16[1,768,2560]{2,1,0:T(8,128)(2,1)} async-done(((bf16[1,48,2560]{2,1,0:T(8,128)(2,1)}), bf16[1,768,2560]{2,1,0:T(8,128)(2,1)}) %all-gather.4.cloned.1.call-update) | async-done | bytes 3932176 | tf_op jit(solution)/shard_map/all_gather | solution.py:45
  245.2 3.7 %fusion.16 = f32[160,768]{1,0:T(8,128)S(1)} fusion(bf16[160,2560]{1,0:T(8,128)(2,1)S(1)} %reshape.52, bf16[1,768,2560]{2,1,0:T(8,128)(2,1)} %all-gather.4.cloned.1.call-done), kind=kOutput, calls=%fused_computation.17 | convolution fusion | flops 629145600 | bytes 5242880 | tf_op jit(solution)/shard_map/dot_general | solution.py:8
  248.9 1.4 fusion
  251.0 1.4 fusion.26
  253.7 7.6 %all-to-all-start.2 = ((bf16[32,5,2560]{2,1,0:T(8,128)(2,1)}), bf16[32,5,2560]{2,1,0:T(8,128)(2,1)}, u32[]{:S(2)}, u32[]{:S(2)}) async-start(bf16[32,5,2560]{2,1,0:T(8,128)(2,1)} %reshape.55), calls=%async_computation.2 | async-start | bytes 2621440 | tf_op jit(solution)/shard_map/all_to_all | solution.py:76
  261.4 3.7 %fusion.18 = f32[128,768]{1,0:T(8,128)S(1)} fusion(bf16[1,768,2560]{2,1,0:T(8,128)(2,1)} %all-gather.4.cloned.1.call-done, bf16[128,2560]{1,0:T(8,128)(2,1)S(1)} %copy-done.7, f32[128]{0:T(128)S(1)} %get-tuple-element.3), kind=kOutput, calls=%fused_computation.19 | convolution fusion | flops 504299520 | bytes 4981248 | tf_op jit(solution)/shard_map/dot_general | solution.py:8
  265.1 1.4 fusion.4
  267.2 1.4 fusion.23
  268.6 10.9 %all-to-all-done.2 = bf16[32,5,2560]{2,1,0:T(8,128)(2,1)} async-done(((bf16[32,5,2560]{2,1,0:T(8,128)(2,1)}), bf16[32,5,2560]{2,1,0:T(8,128)(2,1)}, u32[]{:S(2)}, u32[]{:S(2)}) %all-to-all-start.2) | async-done | bytes 819232 | tf_op jit(solution)/shard_map/all_to_all | solution.py:76
  279.5 1.5 reshape.56
  282.2 42.9 %reduce-scatter.2.cloned.1.call-done = bf16[48,2560]{1,0:T(8,128)(2,1)} async-done(((bf16[768,2560]{1,0:T(8,128)(2,1)}), bf16[48,2560]{1,0:T(8,128)(2,1)}) %reduce-scatter.2.cloned.1.call-update) | async-done | bytes 245776 | tf_op jit(solution)/shard_map/reduce_scatter | solution.py:96
  (45 shorter events, 13.5 us)
Async XLA Ops:
  7.2 18.4 %copy-start = (bf16[128,2560]{1,0:T(8,128)(2,1)S(1)}, bf16[128,2560]{1,0:T(8,128)(2,1)}, u32[]{:S(2)}) copy-start(bf16[128,2560]{1,0:T(8,128)(2,1)} %param.8) | copy-start | bytes 1966084
  7.2 84.9 %all-gather.8.cloned.1.call-start = ((), (), s32[]{:S(2)}) async-start(), calls=%async_computation.6 | async-start | bytes 4177920 | tf_op jit(solution)/shard_map/all_gather | solution.py:43
  7.9 160.7 %all-gather.6.cloned.1.call-start = ((), (), s32[]{:S(2)}) async-start(), calls=%async_computation.5 | async-start | bytes 4177920 | tf_op jit(solution)/shard_map/all_gather | solution.py:44
  8.7 236.5 %all-gather.4.cloned.1.call-start = ((), (), s32[]{:S(2)}) async-start(), calls=%async_computation.4 | async-start | bytes 4177920 | tf_op jit(solution)/shard_map/all_gather | solution.py:45
  15.9 27.6 %all-to-all-start = ((bf16[32,5,2560]{2,1,0:T(8,128)(2,1)}), bf16[32,5,2560]{2,1,0:T(8,128)(2,1)S(1)}, u32[]{:S(2)}, u32[]{:S(2)}) async-start(bf16[32,5,2560]{2,1,0:T(8,128)(2,1)} %reshape.51), calls=%async_computation | async-start | bytes 2621440 | tf_op jit(solution)/shard_map/all_to_all | solution.py:71
  43.5 24.4 %all-to-all-start.1 = ((bf16[32,5,2560]{2,1,0:T(8,128)(2,1)}), bf16[32,5,2560]{2,1,0:T(8,128)(2,1)}, u32[]{:S(2)}, u32[]{:S(2)}) async-start(bf16[32,5,2560]{2,1,0:T(8,128)(2,1)} %reshape.53), calls=%async_computation.1 | async-start | bytes 2621440 | tf_op jit(solution)/shard_map/all_to_all | solution.py:70
  49.9 275.3 %reduce-scatter.2.cloned.1.call-start = ((), (), s32[]{:S(2)}) async-start(), calls=%async_computation.7 | async-start | bytes 4177920 | tf_op jit(solution)/shard_map/reduce_scatter | solution.py:96
  168.6 6.0 %copy-start.1 = (bf16[1,2560,768]{2,1,0:T(8,128)(2,1)S(1)}, bf16[1,2560,768]{2,1,0:T(8,128)(2,1)}, u32[]{:S(2)}) copy-start(bf16[1,2560,768]{2,1,0:T(8,128)(2,1)} %all-gather.6.cloned.1.call-done) | copy-start | bytes 11796484
  171.6 3.9 %copy-start.10 = (f32[128,768]{1,0:T(8,128)}, f32[128,768]{1,0:T(8,128)S(1)}, u32[]{:S(2)}) copy-start(f32[128,768]{1,0:T(8,128)S(1)} %fusion.14) | copy-start | bytes 1179652
  174.7 1.1 copy-start.6
  175.5 1.6 copy-start.8
  180.2 68.6 %copy-start.9 = (f32[160,768]{1,0:T(8,128)S(1)}, f32[160,768]{1,0:T(8,128)}, u32[]{:S(2)}) copy-start(f32[160,768]{1,0:T(8,128)} %copy-done.8) | copy-start | bytes 1474564
  245.2 3.7 %copy-start.4 = (bf16[1,2560,768]{2,1,0:T(8,128)(2,1)S(1)}, bf16[1,2560,768]{2,1,0:T(8,128)(2,1)}, u32[]{:S(2)}) copy-start(bf16[1,2560,768]{2,1,0:T(8,128)(2,1)} %all-gather.8.cloned.1.call-done) | copy-start | bytes 11796484
  248.9 2.1 copy-start.2
  252.4 8.9 %copy-start.7 = (bf16[128,2560]{1,0:T(8,128)(2,1)S(1)}, bf16[128,2560]{1,0:T(8,128)(2,1)}, u32[]{:S(2)}) copy-start(bf16[128,2560]{1,0:T(8,128)(2,1)} %param.9) | copy-start | bytes 1966084
  253.7 11.4 %copy-start.11 = (f32[128,768]{1,0:T(8,128)S(1)}, f32[128,768]{1,0:T(8,128)}, u32[]{:S(2)}) copy-start(f32[128,768]{1,0:T(8,128)} %copy-done.10) | copy-start | bytes 1179652
  253.7 25.8 %all-to-all-start.2 = ((bf16[32,5,2560]{2,1,0:T(8,128)(2,1)}), bf16[32,5,2560]{2,1,0:T(8,128)(2,1)}, u32[]{:S(2)}, u32[]{:S(2)}) async-start(bf16[32,5,2560]{2,1,0:T(8,128)(2,1)} %reshape.55), calls=%async_computation.2 | async-start | bytes 2621440 | tf_op jit(solution)/shard_map/all_to_all | solution.py:76
  261.4 3.7 %copy-start.5 = (bf16[1,2560,768]{2,1,0:T(8,128)(2,1)S(1)}, bf16[1,2560,768]{2,1,0:T(8,128)(2,1)}, u32[]{:S(2)}) copy-start(bf16[1,2560,768]{2,1,0:T(8,128)(2,1)} %all-gather.8.cloned.1.call-done) | copy-start | bytes 11796484
  265.1 2.1 copy-start.3
Sparse Core Ops, SparseCore 0:
  10.1 81.9 all-gather.7
  94.1 74.4 all-gather.5
  170.7 74.4 all-gather.3
  248.5 76.6 reduce-scatter.1
where the time goes:
time: 333 us; the launch traced here: 332 us
  waiting for transfers between devices  251 us (75%)
  matrix products  30.2 us (9%)
  starting transfers between devices  23.7 us (7%)
  between operations  14.7 us (4%)
  local copies, waits for them, and re-layouts  8.85 us (3%)
    all_gather x1, waiting for transfers between devices, local(): lax.all_gather(w_up, 'replica', axis=1, tiled=True)  73.8 us
    all_gather x1, waiting for transfers between devices, local(): lax.all_gather(w_down, 'replica', axis=1, tiled=True)  64.9 us
    reduce_scatter x1, waiting for transfers between devices, local(): lax.psum_scatter((lax.dot_general(hidden_home, q_home, contract, preferre...  42.9 us
    all_gather x1, waiting for transfers between devices, local(): lax.all_gather(w_gate, 'replica', axis=1, tiled=True)  22.6 us
    all_to_all x1, waiting for transfers between devices, local(): lax.all_to_all(send_x, 'expert', split_axis=0, concat_axis=0, tiled=True)  17.6 us
    all_to_all x1, waiting for transfers between devices, local(): lax.all_to_all(send_q, 'expert', split_axis=0, concat_axis=0, tiled=True)  16.3 us
    dot_general x6, matrix products, against_rows(): lax.dot_general(left, matrix, (((1,), (1,)), ((), ())), preferred_element...  13 us
    all_to_all x1, waiting for transfers between devices, local(): lax.all_to_all(grad_there.astype(jnp.bfloat16).reshape(expert_count, item...  10.9 us
  transfers between devices with their start and end apart: 7, of which 7 were waited for; matrix products, arithmetic and copies ran while one was open for 12% of the time, Pallas kernels for 0%

commit v1 on v0

--- a/solution.py
+++ b/solution.py
@@ -25,6 +25,64 @@
     return (hidden, input_grad)
 
 
+def ring_gather(parts, axis):
+    n = lax.axis_size(axis)
+    idx = lax.axis_index(axis)
+    right = [(i, (i + 1) % n) for i in range(n)]
+    left = [(i, (i - 1) % n) for i in range(n)]
+    fulls = [jnp.zeros((n,) + p.shape, p.dtype) for p in parts]
+
+    def put(fulls, pieces, d):
+        pos = (idx + d) % n
+        return [lax.dynamic_update_index_in_dim(f, p, pos, 0) for f, p in zip(fulls, pieces)]
+
+    fulls = put(fulls, parts, 0)
+    r, l = list(parts), list(parts)
+    half = n // 2
+    steps = half if n % 2 == 1 else half - 1
+    for k in range(1, steps + 1):
+        r = [lax.ppermute(p, axis, right) for p in r]
+        l = [lax.ppermute(p, axis, left) for p in l]
+        fulls = put(fulls, r, -k)
+        fulls = put(fulls, l, k)
+    if n % 2 == 0 and n > 1:
+        cut = [p.shape[-1] // 2 for p in parts]
+        rh = [lax.ppermute(p[..., :c], axis, right) for p, c in zip(r, cut)]
+        lh = [lax.ppermute(p[..., c:], axis, left) for p, c in zip(l, cut)]
+        last = [jnp.concatenate([a, b], axis=-1) for a, b in zip(rh, lh)]
+        fulls = put(fulls, last, half)
+    return fulls
+
+
+def ring_reduce_scatter(blocks, axis):
+    n = lax.axis_size(axis)
+    idx = lax.axis_index(axis)
+    right = [(i, (i + 1) % n) for i in range(n)]
+    left = [(i, (i - 1) % n) for i in range(n)]
+
+    def blk(k):
+        return lax.dynamic_index_in_dim(blocks, (idx + k) % n, 0, keepdims=False)
+
+    n_right = n // 2
+    n_left = n - 1 - n_right
+    out = blk(0)
+    recv_r = recv_l = None
+    for s in range(1, max(n_right, n_left) + 1):
+        if s <= n_right:
+            mine = blk(n_right + 1 - s)
+            acc = mine if recv_r is None else recv_r.astype(jnp.float32) + mine
+            recv_r = lax.ppermute(acc.astype(jnp.bfloat16), axis, right)
+        if s <= n_left:
+            mine = blk(-(n_left + 1 - s))
+            acc = mine if recv_l is None else recv_l.astype(jnp.float32) + mine
+            recv_l = lax.ppermute(acc.astype(jnp.bfloat16), axis, left)
+    if recv_r is not None:
+        out = out + recv_r.astype(jnp.float32)
+    if recv_l is not None:
+        out = out + recv_l.astype(jnp.float32)
+    return out
+
+
 def local(tokens, cotangent, partner, combine, counts, w_gate, w_up, w_down):
     tok_rows = tokens.shape[0]
     width = tokens.shape[1]
@@ -39,14 +97,10 @@
     upstream = cotangent.astype(jnp.float32)
     q_home = (upstream * share_home[:, None]).astype(jnp.bfloat16)
     q_away = (upstream * share_away[:, None]).astype(jnp.bfloat16)
-    gate_full, up_full, down_full = (
-        lax.all_gather(w_gate, "replica", axis=1, tiled=True),
-        lax.all_gather(w_up, "replica", axis=1, tiled=True),
-        lax.all_gather(w_down, "replica", axis=1, tiled=True),
-    )
-    gate_w = gate_full.reshape(gate_full.shape[1], gate_full.shape[2])
-    up_w = up_full.reshape(up_full.shape[1], up_full.shape[2])
-    down_w = down_full.reshape(down_full.shape[1], down_full.shape[2])
+    gate_full, up_full, down_full = ring_gather([w_gate[0], w_up[0], w_down[0]], "replica")
+    gate_w = gate_full.reshape(-1, gate_full.shape[2])
+    up_w = up_full.reshape(-1, up_full.shape[2])
+    down_w = down_full.reshape(-1, down_full.shape[2])
     target = partner[:, 0]
     onehot_rows = (target[:, None] == jnp.arange(expert_count, dtype=jnp.int32)[None, :]).astype(
         jnp.int32
@@ -93,15 +147,13 @@
     token_grad = (grad_home + grad_away).astype(jnp.bfloat16)
     flat_hidden = hidden_away.reshape(expert_count * capacity, -1)
     flat_q = q_there.reshape(expert_count * capacity, width)
-    grad_down = lax.psum_scatter(
-        (
-            lax.dot_general(hidden_home, q_home, contract, preferred_element_type=jnp.float32)
-            + lax.dot_general(flat_hidden, flat_q, contract, preferred_element_type=jnp.float32)
-        ).astype(jnp.bfloat16),
-        "replica",
-        scatter_dimension=0,
-        tiled=True,
-    )
+    partial = lax.dot_general(
+        hidden_home, q_home, contract, preferred_element_type=jnp.float32
+    ) + lax.dot_general(flat_hidden, flat_q, contract, preferred_element_type=jnp.float32)
+    n_rep = lax.axis_size("replica")
+    grad_down = ring_reduce_scatter(
+        partial.reshape(n_rep, -1, partial.shape[1]), "replica"
+    ).astype(jnp.bfloat16)
     return (token_grad, grad_down[None])
 
 

time: 333 us -> 380 us (1.14)
  waiting for transfers between devices: 251 us -> 27 us
  starting transfers between devices: 23.7 us -> 236 us
  local copies, waits for them, and re-layouts: 8.85 us -> 56.4 us
  between operations: 14.7 us -> 2.6 us
  other arithmetic: 3.09 us -> 14 us
  matrix products: 30.2 us -> 40.6 us
    ppermute x0 -> x63, starting transfers between devices: none -> 215 us  [the longest x21 104 us: ring_gather(): l = [lax.ppermute(p, axis, left) for p in l]]
    all_gather x3 -> x0, waiting for transfers between devices: 161 us -> none  [the longest x1 73.8 us: local(): lax.all_gather(w_up, 'replica', axis=1, tiled=True)]
    reduce_scatter x1 -> x0, waiting for transfers between devices: 42.9 us -> none  [local(): lax.psum_scatter((lax.dot_general(hidden_home, q_home, contract, preferre...]
    dynamic_update_slice x0 -> x45, local copies, waits for them, and re-layouts: none -> 42.7 us  [put(): lax.dynamic_update_index_in_dim(f, p, pos, 0)]
    ppermute x0 -> x63, waiting for transfers between devices: none -> 18.9 us  [the longest x8 15.8 us: ring_reduce_scatter(): recv_r = lax.ppermute(acc.astype(jnp.bfloat16), axis, right)]
    all_to_all x1, waiting for transfers between devices: 16.3 us -> 0.01 us  [local(): lax.all_to_all(send_q, 'expert', split_axis=0, concat_axis=0, tiled=True)]
    all_to_all x1, waiting for transfers between devices: 10.9 us -> 0.01 us  [local(): lax.all_to_all(grad_there.astype(jnp.bfloat16).reshape(expert_count, item...]
    all_to_all x1, waiting for transfers between devices: 17.6 us -> 8.09 us  [local(): lax.all_to_all(send_x, 'expert', split_axis=0, concat_axis=0, tiled=True)]
  transfers between devices with their start and end apart: 7 -> 66, of which waited for: 7 -> 9; matrix products, arithmetic and copies ran while one was open for 12% -> 28% of each run, Pallas kernels for 0% -> 0%
where the time goes in v1:
time: 380 us; the launch traced here: 376 us
  starting transfers between devices  236 us (62%)
  local copies, waits for them, and re-layouts  56.4 us (15%)
  matrix products  40.6 us (11%)
  waiting for transfers between devices  27 us (7%)
  other arithmetic  14 us (4%)
    ppermute x21, starting transfers between devices, ring_gather(): l = [lax.ppermute(p, axis, left) for p in l]  104 us
    dynamic_update_slice x45, local copies, waits for them, and re-layouts, put(): lax.dynamic_update_index_in_dim(f, p, pos, 0)  42.7 us
    ppermute x21, starting transfers between devices, ring_gather(): r = [lax.ppermute(p, axis, right) for p in r]  42.3 us
    ppermute x7, starting transfers between devices, ring_reduce_scatter(): recv_l = lax.ppermute(acc.astype(jnp.bfloat16), axis, left)  35.8 us
    dot_general x6, matrix products, against_rows(): lax.dot_general(left, matrix, (((1,), (1,)), ((), ())), preferred_element...  22.2 us
    ppermute x8, starting transfers between devices, ring_reduce_scatter(): recv_r = lax.ppermute(acc.astype(jnp.bfloat16), axis, right)  15.8 us
    ppermute x8, waiting for transfers between devices, ring_reduce_scatter(): recv_r = lax.ppermute(acc.astype(jnp.bfloat16), axis, right)  15.8 us
    ppermute x3, starting transfers between devices, ring_gather(): rh = [lax.ppermute(p[..., :c], axis, right) for p, c in zip(r, cut)]  10.7 us
  transfers between devices with their start and end apart: 66, of which 9 were waited for; matrix products, arithmetic and copies ran while one was open for 28% of the time, Pallas kernels for 0%

profile of v1, /device:TPU:6, one launch (start us, length us, event | category | flops | bytes accessed | tf_op | source)
XLA Modules:
  0.0 376.5 jit_solution(6867340027013302831)
XLA Ops:
  4.6 9.5 %collective-permute-start.17 = (bf16[160,768]{1,0:T(8,128)(2,1)}, bf16[160,768]{1,0:T(8,128)(2,1)}, u32[]{:S(2)}, u32[]{:S(2)}) collective-permute-start(bf16[160,768]{1,0:T(8,128)(2,1)} %bitcast.209), channel_id=1, source_target_pairs={{0,15},{1,0},{2,1},{3,2},{4,3},{5,4},{6,5},{7,6},{8,7},{9,8},{10,9... | collective-permute-start | bytes 737288 | tf_op jit(solution)/shard_map/ppermute | solution.py:45
  16.1 5.1 %collective-permute-start.1 = (bf16[48,2560]{1,0:T(8,128)(2,1)}, bf16[48,2560]{1,0:T(8,128)(2,1)}, u32[]{:S(2)}, u32[]{:S(2)}) collective-permute-start(bf16[48,2560]{1,0:T(8,128)(2,1)} %bitcast.211), channel_id=1, source_target_pairs={{0,15},{1,0},{2,1},{3,2},{4,3},{5,4},{6,5},{7,6},{8,7},{9,8},{10,9... | collective-permute-start | bytes 737288 | tf_op jit(solution)/shard_map/ppermute | solution.py:45
  29.7 7.7 %all-to-all-start = ((bf16[32,5,2560]{2,1,0:T(8,128)(2,1)}), bf16[32,5,2560]{2,1,0:T(8,128)(2,1)S(1)}, u32[]{:S(2)}, u32[]{:S(2)}) async-start(bf16[32,5,2560]{2,1,0:T(8,128)(2,1)} %reshape.56), calls=%async_computation | async-start | bytes 2621440 | tf_op jit(solution)/shard_map/all_to_all | solution.py:125
  58.9 5.1 %collective-permute-start.19 = (bf16[160,768]{1,0:T(8,128)(2,1)}, bf16[160,768]{1,0:T(8,128)(2,1)S(1)}, u32[]{:S(2)}, u32[]{:S(2)}) collective-permute-start(bf16[160,768]{1,0:T(8,128)(2,1)} %collective-permute-done.17), channel_id=1, source_target_pairs={{0,15},{1,0},{2,1},{3,2},{4,3},{5,4},{6,5},{7,6},{8,7},{9,8},{10,9... | collective-permute-start | bytes 737288 | tf_op jit(solution)/shard_map/ppermute | solution.py:45
  76.3 5.1 %collective-permute-start.35 = (bf16[160,768]{1,0:T(8,128)(2,1)S(1)}, bf16[160,768]{1,0:T(8,128)(2,1)S(1)}, u32[]{:S(2)}, u32[]{:S(2)}) collective-permute-start(bf16[160,768]{1,0:T(8,128)(2,1)S(1)} %collective-permute-done.33), channel_id=1, source_target_pairs={{0,15},{1,0},{2,1},{3,2},{4,3},{5,4},{6,5},{7,6},{8,7},{9,8},{10,9... | collective-permute-start | bytes 737288 | tf_op jit(solution)/shard_map/ppermute | solution.py:45
  86.1 5.1 %collective-permute-start.21 = (bf16[160,768]{1,0:T(8,128)(2,1)S(1)}, bf16[160,768]{1,0:T(8,128)(2,1)S(1)}, u32[]{:S(2)}, u32[]{:S(2)}) collective-permute-start(bf16[160,768]{1,0:T(8,128)(2,1)S(1)} %collective-permute-done.19), channel_id=1, source_target_pairs={{0,15},{1,0},{2,1},{3,2},{4,3},{5,4},{6,5},{7,6},{8,7},{9,8},{10,9... | collective-permute-start | bytes 737288 | tf_op jit(solution)/shard_map/ppermute | solution.py:45
  100.6 5.1 %collective-permute-start.37 = (bf16[160,768]{1,0:T(8,128)(2,1)S(1)}, bf16[160,768]{1,0:T(8,128)(2,1)S(1)}, u32[]{:S(2)}, u32[]{:S(2)}) collective-permute-start(bf16[160,768]{1,0:T(8,128)(2,1)S(1)} %collective-permute-done.35), channel_id=1, source_target_pairs={{0,15},{1,0},{2,1},{3,2},{4,3},{5,4},{6,5},{7,6},{8,7},{9,8},{10,9... | collective-permute-start | bytes 737288 | tf_op jit(solution)/shard_map/ppermute | solution.py:45
  111.3 5.1 %collective-permute-start.23 = (bf16[160,768]{1,0:T(8,128)(2,1)S(1)}, bf16[160,768]{1,0:T(8,128)(2,1)}, u32[]{:S(2)}, u32[]{:S(2)}) collective-permute-start(bf16[160,768]{1,0:T(8,128)(2,1)S(1)} %collective-permute-done.21), channel_id=1, source_target_pairs={{0,15},{1,0},{2,1},{3,2},{4,3},{5,4},{6,5},{7,6},{8,7},{9,8},{10,9... | collective-permute-start | bytes 737288 | tf_op jit(solution)/shard_map/ppermute | solution.py:45
  118.1 7.4 %all-to-all-start.1 = ((bf16[32,5,2560]{2,1,0:T(8,128)(2,1)}), bf16[32,5,2560]{2,1,0:T(8,128)(2,1)}, u32[]{:S(2)}, u32[]{:S(2)}) async-start(bf16[32,5,2560]{2,1,0:T(8,128)(2,1)} %reshape.58), calls=%async_computation.1 | async-start | bytes 2621440 | tf_op jit(solution)/shard_map/all_to_all | solution.py:124
  135.6 8.1 %all-to-all-done.1 = bf16[32,5,2560]{2,1,0:T(8,128)(2,1)} async-done(((bf16[32,5,2560]{2,1,0:T(8,128)(2,1)}), bf16[32,5,2560]{2,1,0:T(8,128)(2,1)}, u32[]{:S(2)}, u32[]{:S(2)}) %all-to-all-start.1) | async-done | bytes 819232 | tf_op jit(solution)/shard_map/all_to_all | solution.py:124
  154.6 5.1 %collective-permute-start.25 = (bf16[160,768]{1,0:T(8,128)(2,1)}, bf16[160,768]{1,0:T(8,128)(2,1)S(1)}, u32[]{:S(2)}, u32[]{:S(2)}) collective-permute-start(bf16[160,768]{1,0:T(8,128)(2,1)} %collective-permute-done.23), channel_id=1, source_target_pairs={{0,15},{1,0},{2,1},{3,2},{4,3},{5,4},{6,5},{7,6},{8,7},{9,8},{10,9... | collective-permute-start | bytes 737288 | tf_op jit(solution)/shard_map/ppermute | solution.py:45
  172.0 5.1 %collective-permute-start.41 = (bf16[160,768]{1,0:T(8,128)(2,1)S(1)}, bf16[160,768]{1,0:T(8,128)(2,1)S(1)}, u32[]{:S(2)}, u32[]{:S(2)}) collective-permute-start(bf16[160,768]{1,0:T(8,128)(2,1)S(1)} %collective-permute-done.39), channel_id=1, source_target_pairs={{0,15},{1,0},{2,1},{3,2},{4,3},{5,4},{6,5},{7,6},{8,7},{9,8},{10,9... | collective-permute-start | bytes 737288 | tf_op jit(solution)/shard_map/ppermute | solution.py:45
  181.7 5.1 %collective-permute-start.27 = (bf16[160,768]{1,0:T(8,128)(2,1)S(1)}, bf16[160,768]{1,0:T(8,128)(2,1)S(1)}, u32[]{:S(2)}, u32[]{:S(2)}) collective-permute-start(bf16[160,768]{1,0:T(8,128)(2,1)S(1)} %collective-permute-done.25), channel_id=1, source_target_pairs={{0,15},{1,0},{2,1},{3,2},{4,3},{5,4},{6,5},{7,6},{8,7},{9,8},{10,9... | collective-permute-start | bytes 737288 | tf_op jit(solution)/shard_map/ppermute | solution.py:45
  196.3 5.1 %collective-permute-start.43 = (bf16[160,768]{1,0:T(8,128)(2,1)S(1)}, bf16[160,768]{1,0:T(8,128)(2,1)S(1)}, u32[]{:S(2)}, u32[]{:S(2)}) collective-permute-start(bf16[160,768]{1,0:T(8,128)(2,1)S(1)} %collective-permute-done.41), channel_id=1, source_target_pairs={{0,15},{1,0},{2,1},{3,2},{4,3},{5,4},{6,5},{7,6},{8,7},{9,8},{10,9... | collective-permute-start | bytes 737288 | tf_op jit(solution)/shard_map/ppermute | solution.py:45
  206.0 5.1 %collective-permute-start.29 = (bf16[160,768]{1,0:T(8,128)(2,1)S(1)}, bf16[160,768]{1,0:T(8,128)(2,1)S(1)}, u32[]{:S(2)}, u32[]{:S(2)}) collective-permute-start(bf16[160,768]{1,0:T(8,128)(2,1)S(1)} %collective-permute-done.27), channel_id=1, source_target_pairs={{0,15},{1,0},{2,1},{3,2},{4,3},{5,4},{6,5},{7,6},{8,7},{9,8},{10,9... | collective-permute-start | bytes 737288 | tf_op jit(solution)/shard_map/ppermute | solution.py:45
  219.2 5.1 %collective-permute-start.45 = (bf16[160,768]{1,0:T(8,128)(2,1)S(1)}, bf16[160,768]{1,0:T(8,128)(2,1)S(1)}, u32[]{:S(2)}, u32[]{:S(2)}) collective-permute-start(bf16[160,768]{1,0:T(8,128)(2,1)S(1)} %collective-permute-done.43), channel_id=1, source_target_pairs={{0,15},{1,0},{2,1},{3,2},{4,3},{5,4},{6,5},{7,6},{8,7},{9,8},{10,9... | collective-permute-start | bytes 737288 | tf_op jit(solution)/shard_map/ppermute | solution.py:45
  265.7 5.1 %collective-permute-start.56 = (bf16[48,2560]{1,0:T(8,128)(2,1)S(1)}, bf16[48,2560]{1,0:T(8,128)(2,1)S(1)}, u32[]{:S(2)}, u32[]{:S(2)}) collective-permute-start(bf16[48,2560]{1,0:T(8,128)(2,1)S(1)} %get-tuple-element.15), channel_id=1, source_target_pairs={{0,15},{1,0},{2,1},{3,2},{4,3},{5,4},{6,5},{7,6},{8,7},{9,8},{10,9... | collective-permute-start | bytes 737288 | tf_op jit(solution)/shard_map/ppermute | solution.py:78
  281.2 5.7 %collective-permute-done.49 = bf16[48,2560]{1,0:T(8,128)(2,1)S(1)} collective-permute-done((bf16[48,2560]{1,0:T(8,128)(2,1)S(1)}, bf16[48,2560]{1,0:T(8,128)(2,1)S(1)}, u32[]{:S(2)}, u32[]{:S(2)}) %collective-permute-start.49) | collective-permute-done | bytes 245792 | tf_op jit(solution)/shard_map/ppermute | solution.py:74
  288.9 5.1 %collective-permute-start.57 = (bf16[48,2560]{1,0:T(8,128)(2,1)S(1)}, bf16[48,2560]{1,0:T(8,128)(2,1)S(1)}, u32[]{:S(2)}, u32[]{:S(2)}) collective-permute-start(bf16[48,2560]{1,0:T(8,128)(2,1)S(1)} %get-tuple-element.13), channel_id=1, source_target_pairs={{0,15},{1,0},{2,1},{3,2},{4,3},{5,4},{6,5},{7,6},{8,7},{9,8},{10,9... | collective-permute-start | bytes 737288 | tf_op jit(solution)/shard_map/ppermute | solution.py:78
  301.8 5.6 %collective-permute-start.58 = (bf16[48,2560]{1,0:T(8,128)(2,1)S(1)}, bf16[48,2560]{1,0:T(8,128)(2,1)}, u32[]{:S(2)}, u32[]{:S(2)}) collective-permute-start(bf16[48,2560]{1,0:T(8,128)(2,1)S(1)} %get-tuple-element.11), channel_id=1, source_target_pairs={{0,15},{1,0},{2,1},{3,2},{4,3},{5,4},{6,5},{7,6},{8,7},{9,8},{10,9... | collective-permute-start | bytes 737288 | tf_op jit(solution)/shard_map/ppermute | solution.py:78
  312.2 5.6 %all-to-all-start.2 = ((bf16[32,5,2560]{2,1,0:T(8,128)(2,1)}), bf16[32,5,2560]{2,1,0:T(8,128)(2,1)S(1)}, u32[]{:S(2)}, u32[]{:S(2)}) async-start(bf16[32,5,2560]{2,1,0:T(8,128)(2,1)} %reshape.60), calls=%async_computation.2 | async-start | bytes 2621440 | tf_op jit(solution)/shard_map/all_to_all | solution.py:130
  321.1 5.1 %collective-permute-start.59 = (bf16[48,2560]{1,0:T(8,128)(2,1)S(1)}, bf16[48,2560]{1,0:T(8,128)(2,1)S(1)}, u32[]{:S(2)}, u32[]{:S(2)}) collective-permute-start(bf16[48,2560]{1,0:T(8,128)(2,1)S(1)} %get-tuple-element.9), channel_id=1, source_target_pairs={{0,15},{1,0},{2,1},{3,2},{4,3},{5,4},{6,5},{7,6},{8,7},{9,8},{10,9... | collective-permute-start | bytes 737288 | tf_op jit(solution)/shard_map/ppermute | solution.py:78
  334.7 5.7 %collective-permute-start.60 = (bf16[48,2560]{1,0:T(8,128)(2,1)S(1)}, bf16[48,2560]{1,0:T(8,128)(2,1)S(1)}, u32[]{:S(2)}, u32[]{:S(2)}) collective-permute-start(bf16[48,2560]{1,0:T(8,128)(2,1)S(1)} %get-tuple-element.7), channel_id=1, source_target_pairs={{0,15},{1,0},{2,1},{3,2},{4,3},{5,4},{6,5},{7,6},{8,7},{9,8},{10,9... | collective-permute-start | bytes 737288 | tf_op jit(solution)/shard_map/ppermute | solution.py:78
  349.2 5.1 %collective-permute-start.61 = (bf16[48,2560]{1,0:T(8,128)(2,1)}, bf16[48,2560]{1,0:T(8,128)(2,1)}, u32[]{:S(2)}, u32[]{:S(2)}) collective-permute-start(bf16[48,2560]{1,0:T(8,128)(2,1)} %get-tuple-element.5), channel_id=1, source_target_pairs={{0,15},{1,0},{2,1},{3,2},{4,3},{5,4},{6,5},{7,6},{8,7},{9,8},{10,9... | collective-permute-start | bytes 737288 | tf_op jit(solution)/shard_map/ppermute | solution.py:78
  (223 shorter events, 236.5 us)
Async XLA Ops:
  0.6 54.4 %collective-permute-start.16 = (bf16[160,768]{1,0:T(8,128)(2,1)}, bf16[160,768]{1,0:T(8,128)(2,1)}, u32[]{:S(2)}, u32[]{:S(2)}) collective-permute-start(bf16[160,768]{1,0:T(8,128)(2,1)} %bitcast.208), channel_id=1, source_target_pairs={{0,1},{1,2},{2,3},{3,4},{4,5},{5,6},{6,7},{7,8},{8,9},{9,10},{10,1... | collective-permute-start | bytes 737288 | tf_op jit(solution)/shard_map/ppermute | solution.py:44
  4.6 52.3 %collective-permute-start.17 = (bf16[160,768]{1,0:T(8,128)(2,1)}, bf16[160,768]{1,0:T(8,128)(2,1)}, u32[]{:S(2)}, u32[]{:S(2)}) collective-permute-start(bf16[160,768]{1,0:T(8,128)(2,1)} %bitcast.209), channel_id=1, source_target_pairs={{0,15},{1,0},{2,1},{3,2},{4,3},{5,4},{6,5},{7,6},{8,7},{9,8},{10,9... | collective-permute-start | bytes 737288 | tf_op jit(solution)/shard_map/ppermute | solution.py:45
  14.1 34.1 %collective-permute-start = (bf16[48,2560]{1,0:T(8,128)(2,1)}, bf16[48,2560]{1,0:T(8,128)(2,1)}, u32[]{:S(2)}, u32[]{:S(2)}) collective-permute-start(bf16[48,2560]{1,0:T(8,128)(2,1)} %bitcast.210), channel_id=1, source_target_pairs={{0,1},{1,2},{2,3},{3,4},{4,5},{5,6},{6,7},{7,8},{8,9},{9,10},{10,1... | collective-permute-start | bytes 737288 | tf_op jit(solution)/shard_map/ppermute | solution.py:44
  16.1 42.8 %collective-permute-start.1 = (bf16[48,2560]{1,0:T(8,128)(2,1)}, bf16[48,2560]{1,0:T(8,128)(2,1)}, u32[]{:S(2)}, u32[]{:S(2)}) collective-permute-start(bf16[48,2560]{1,0:T(8,128)(2,1)} %bitcast.211), channel_id=1, source_target_pairs={{0,15},{1,0},{2,1},{3,2},{4,3},{5,4},{6,5},{7,6},{8,7},{9,8},{10,9... | collective-permute-start | bytes 737288 | tf_op jit(solution)/shard_map/ppermute | solution.py:45
  21.2 47.8 %collective-permute-start.32 = (bf16[160,768]{1,0:T(8,128)(2,1)}, bf16[160,768]{1,0:T(8,128)(2,1)S(1)}, u32[]{:S(2)}, u32[]{:S(2)}) collective-permute-start(bf16[160,768]{1,0:T(8,128)(2,1)} %bitcast.212), channel_id=1, source_target_pairs={{0,1},{1,2},{2,3},{3,4},{4,5},{5,6},{6,7},{7,8},{8,9},{9,10},{10,1... | collective-permute-start | bytes 737288 | tf_op jit(solution)/shard_map/ppermute | solution.py:44
  29.7 88.4 %all-to-all-start = ((bf16[32,5,2560]{2,1,0:T(8,128)(2,1)}), bf16[32,5,2560]{2,1,0:T(8,128)(2,1)S(1)}, u32[]{:S(2)}, u32[]{:S(2)}) async-start(bf16[32,5,2560]{2,1,0:T(8,128)(2,1)} %reshape.56), calls=%async_computation | async-start | bytes 2621440 | tf_op jit(solution)/shard_map/all_to_all | solution.py:125
  48.3 25.4 %collective-permute-start.33 = (bf16[160,768]{1,0:T(8,128)(2,1)S(1)}, bf16[160,768]{1,0:T(8,128)(2,1)S(1)}, u32[]{:S(2)}, u32[]{:S(2)}) collective-permute-start(bf16[160,768]{1,0:T(8,128)(2,1)S(1)} %bitcast.213), channel_id=1, source_target_pairs={{0,15},{1,0},{2,1},{3,2},{4,3},{5,4},{6,5},{7,6},{8,7},{9,8},{10,9... | collective-permute-start | bytes 737288 | tf_op jit(solution)/shard_map/ppermute | solution.py:45
  57.0 25.2 %collective-permute-start.18 = (bf16[160,768]{1,0:T(8,128)(2,1)}, bf16[160,768]{1,0:T(8,128)(2,1)S(1)}, u32[]{:S(2)}, u32[]{:S(2)}) collective-permute-start(bf16[160,768]{1,0:T(8,128)(2,1)} %collective-permute-done.16), channel_id=1, source_target_pairs={{0,1},{1,2},{2,3},{3,4},{4,5},{5,6},{6,7},{7,8},{8,9},{9,10},{10,1... | collective-permute-start | bytes 737288 | tf_op jit(solution)/shard_map/ppermute | solution.py:44
  58.9 25.2 %collective-permute-start.19 = (bf16[160,768]{1,0:T(8,128)(2,1)}, bf16[160,768]{1,0:T(8,128)(2,1)S(1)}, u32[]{:S(2)}, u32[]{:S(2)}) collective-permute-start(bf16[160,768]{1,0:T(8,128)(2,1)} %collective-permute-done.17), channel_id=1, source_target_pairs={{0,15},{1,0},{2,1},{3,2},{4,3},{5,4},{6,5},{7,6},{8,7},{9,8},{10,9... | collective-permute-start | bytes 737288 | tf_op jit(solution)/shard_map/ppermute | solution.py:45
  98.0 28.9 %collective-permute-start.36 = (bf16[160,768]{1,0:T(8,128)(2,1)S(1)}, bf16[160,768]{1,0:T(8,128)(2,1)}, u32[]{:S(2)}, u32[]{:S(2)}) collective-permute-start(bf16[160,768]{1,0:T(8,128)(2,1)S(1)} %collective-permute-done.34), channel_id=1, source_target_pairs={{0,1},{1,2},{2,3},{3,4},{4,5},{5,6},{6,7},{7,8},{8,9},{9,10},{10,1... | collective-permute-start | bytes 737288 | tf_op jit(solution)/shard_map/ppermute | solution.py:44
  100.6 31.9 %collective-permute-start.37 = (bf16[160,768]{1,0:T(8,128)(2,1)S(1)}, bf16[160,768]{1,0:T(8,128)(2,1)S(1)}, u32[]{:S(2)}, u32[]{:S(2)}) collective-permute-start(bf16[160,768]{1,0:T(8,128)(2,1)S(1)} %collective-permute-done.35), channel_id=1, source_target_pairs={{0,15},{1,0},{2,1},{3,2},{4,3},{5,4},{6,5},{7,6},{8,7},{9,8},{10,9... | collective-permute-start | bytes 737288 | tf_op jit(solution)/shard_map/ppermute | solution.py:45
  107.4 37.7 %collective-permute-start.6 = (bf16[48,2560]{1,0:T(8,128)(2,1)}, bf16[48,2560]{1,0:T(8,128)(2,1)}, u32[]{:S(2)}, u32[]{:S(2)}) collective-permute-start(bf16[48,2560]{1,0:T(8,128)(2,1)} %collective-permute-done.4), channel_id=1, source_target_pairs={{0,1},{1,2},{2,3},{3,4},{4,5},{5,6},{6,7},{7,8},{8,9},{9,10},{10,1... | collective-permute-start | bytes 737288 | tf_op jit(solution)/shard_map/ppermute | solution.py:44
  109.3 41.4 %collective-permute-start.22 = (bf16[160,768]{1,0:T(8,128)(2,1)S(1)}, bf16[160,768]{1,0:T(8,128)(2,1)S(1)}, u32[]{:S(2)}, u32[]{:S(2)}) collective-permute-start(bf16[160,768]{1,0:T(8,128)(2,1)S(1)} %collective-permute-done.20), channel_id=1, source_target_pairs={{0,1},{1,2},{2,3},{3,4},{4,5},{5,6},{6,7},{7,8},{8,9},{9,10},{10,1... | collective-permute-start | bytes 737288 | tf_op jit(solution)/shard_map/ppermute | solution.py:44
  111.3 41.4 %collective-permute-start.23 = (bf16[160,768]{1,0:T(8,128)(2,1)S(1)}, bf16[160,768]{1,0:T(8,128)(2,1)}, u32[]{:S(2)}, u32[]{:S(2)}) collective-permute-start(bf16[160,768]{1,0:T(8,128)(2,1)S(1)} %collective-permute-done.21), channel_id=1, source_target_pairs={{0,15},{1,0},{2,1},{3,2},{4,3},{5,4},{6,5},{7,6},{8,7},{9,8},{10,9... | collective-permute-start | bytes 737288 | tf_op jit(solution)/shard_map/ppermute | solution.py:45
  118.1 25.6 %all-to-all-start.1 = ((bf16[32,5,2560]{2,1,0:T(8,128)(2,1)}), bf16[32,5,2560]{2,1,0:T(8,128)(2,1)}, u32[]{:S(2)}, u32[]{:S(2)}) async-start(bf16[32,5,2560]{2,1,0:T(8,128)(2,1)} %reshape.58), calls=%async_computation.1 | async-start | bytes 2621440 | tf_op jit(solution)/shard_map/all_to_all | solution.py:124
  126.9 27.7 %collective-permute-start.7 = (bf16[48,2560]{1,0:T(8,128)(2,1)}, bf16[48,2560]{1,0:T(8,128)(2,1)}, u32[]{:S(2)}, u32[]{:S(2)}) collective-permute-start(bf16[48,2560]{1,0:T(8,128)(2,1)} %collective-permute-done.5), channel_id=1, source_target_pairs={{0,15},{1,0},{2,1},{3,2},{4,3},{5,4},{6,5},{7,6},{8,7},{9,8},{10,9... | collective-permute-start | bytes 737288 | tf_op jit(solution)/shard_map/ppermute | solution.py:45
  132.5 31.2 %collective-permute-start.38 = (bf16[160,768]{1,0:T(8,128)(2,1)}, bf16[160,768]{1,0:T(8,128)(2,1)}, u32[]{:S(2)}, u32[]{:S(2)}) collective-permute-start(bf16[160,768]{1,0:T(8,128)(2,1)} %collective-permute-done.36), channel_id=1, source_target_pairs={{0,1},{1,2},{2,3},{3,4},{4,5},{5,6},{6,7},{7,8},{8,9},{9,10},{10,1... | collective-permute-start | bytes 737288 | tf_op jit(solution)/shard_map/ppermute | solution.py:44
  152.7 25.2 %collective-permute-start.24 = (bf16[160,768]{1,0:T(8,128)(2,1)S(1)}, bf16[160,768]{1,0:T(8,128)(2,1)S(1)}, u32[]{:S(2)}, u32[]{:S(2)}) collective-permute-start(bf16[160,768]{1,0:T(8,128)(2,1)S(1)} %collective-permute-done.22), channel_id=1, source_target_pairs={{0,1},{1,2},{2,3},{3,4},{4,5},{5,6},{6,7},{7,8},{8,9},{9,10},{10,1... | collective-permute-start | bytes 737288 | tf_op jit(solution)/shard_map/ppermute | solution.py:44
  154.6 25.2 %collective-permute-start.25 = (bf16[160,768]{1,0:T(8,128)(2,1)}, bf16[160,768]{1,0:T(8,128)(2,1)S(1)}, u32[]{:S(2)}, u32[]{:S(2)}) collective-permute-start(bf16[160,768]{1,0:T(8,128)(2,1)} %collective-permute-done.23), channel_id=1, source_target_pairs={{0,15},{1,0},{2,1},{3,2},{4,3},{5,4},{6,5},{7,6},{8,7},{9,8},{10,9... | collective-permute-start | bytes 737288 | tf_op jit(solution)/shard_map/ppermute | solution.py:45
  202.2 34.7 %collective-permute-start.12 = (bf16[48,2560]{1,0:T(8,128)(2,1)S(1)}, bf16[48,2560]{1,0:T(8,128)(2,1)S(1)}, u32[]{:S(2)}, u32[]{:S(2)}) collective-permute-start(bf16[48,2560]{1,0:T(8,128)(2,1)S(1)} %collective-permute-done.10), channel_id=1, source_target_pairs={{0,1},{1,2},{2,3},{3,4},{4,5},{5,6},{6,7},{7,8},{8,9},{9,10},{10,1... | collective-permute-start | bytes 737288 | tf_op jit(solution)/shard_map/ppermute | solution.py:44
  225.8 25.7 %collective-permute-start.31 = (bf16[160,384]{1,0:T(8,128)(2,1)S(1)}, bf16[160,384]{1,0:T(8,128)(2,1)S(1)}, u32[]{:S(2)}, u32[]{:S(2)}) collective-permute-start(bf16[160,384]{1,0:T(8,128)(2,1)S(1)} %slice.37), channel_id=1, source_target_pairs={{0,15},{1,0},{2,1},{3,2},{4,3},{5,4},{6,5},{7,6},{8,7},{9,8},{10,9... | collective-permute-start | bytes 368648 | tf_op jit(solution)/shard_map/ppermute | solution.py:51
  231.7 39.1 %collective-permute-start.15 = (bf16[48,1280]{1,0:T(8,128)(2,1)S(1)}, bf16[48,1280]{1,0:T(8,128)(2,1)S(1)}, u32[]{:S(2)}, u32[]{:S(2)}) collective-permute-start(bf16[48,1280]{1,0:T(8,128)(2,1)S(1)} %slice.35), channel_id=1, source_target_pairs={{0,15},{1,0},{2,1},{3,2},{4,3},{5,4},{6,5},{7,6},{8,7},{9,8},{10,9... | collective-permute-start | bytes 368648 | tf_op jit(solution)/shard_map/ppermute | solution.py:51
  245.1 25.7 %collective-permute-start.14 = (bf16[48,1280]{1,0:T(8,128)(2,1)S(1)}, bf16[48,1280]{1,0:T(8,128)(2,1)S(1)}, u32[]{:S(2)}, u32[]{:S(2)}) collective-permute-start(bf16[48,1280]{1,0:T(8,128)(2,1)S(1)} %slice.34), channel_id=1, source_target_pairs={{0,1},{1,2},{2,3},{3,4},{4,5},{5,6},{6,7},{7,8},{8,9},{9,10},{10,1... | collective-permute-start | bytes 368648 | tf_op jit(solution)/shard_map/ppermute | solution.py:50
  312.2 46.8 %all-to-all-start.2 = ((bf16[32,5,2560]{2,1,0:T(8,128)(2,1)}), bf16[32,5,2560]{2,1,0:T(8,128)(2,1)S(1)}, u32[]{:S(2)}, u32[]{:S(2)}) async-start(bf16[32,5,2560]{2,1,0:T(8,128)(2,1)} %reshape.60), calls=%async_computation.2 | async-start | bytes 2621440 | tf_op jit(solution)/shard_map/all_to_all | solution.py:130
  (53 other events, 850.6 us)

commit v2 on v0

--- a/solution.py
+++ b/solution.py
@@ -25,6 +25,45 @@
     return (hidden, input_grad)
 
 
+def ring_plan():
+    n_exp = lax.axis_size("expert")
+    n = lax.axis_size("replica")
+    perm = []
+    for e in range(n_exp):
+        step = 1 if e % 2 == 0 else n - 1
+        perm += [(e * n + r, e * n + (r + step) % n) for r in range(n)]
+    r = lax.axis_index("replica")
+    toward = 1 - 2 * (lax.axis_index("expert") % 2)
+    return n, r, toward, perm
+
+
+def ring_gather(piece):
+    n, r, toward, perm = ring_plan()
+    pieces = [piece]
+    for _ in range(n - 1):
+        pieces.append(lax.ppermute(pieces[-1], ("expert", "replica"), perm))
+    stacked = jnp.stack(pieces)
+    order = (toward * (r - jnp.arange(n, dtype=jnp.int32))) % n
+    return jnp.take(stacked, order, axis=0)
+
+
+def ring_reduce_scatter(blocks):
+    n, r, toward, perm = ring_plan()
+
+    def blk(k):
+        return lax.dynamic_index_in_dim(blocks, k % n, 0, keepdims=False)
+
+    recv = None
+    for s in range(1, n):
+        mine = blk(r - s * toward)
+        acc = mine if recv is None else recv.astype(jnp.float32) + mine
+        recv = lax.ppermute(acc.astype(jnp.bfloat16), ("expert", "replica"), perm)
+    out = blk(r)
+    if recv is not None:
+        out = out + recv.astype(jnp.float32)
+    return out
+
+
 def local(tokens, cotangent, partner, combine, counts, w_gate, w_up, w_down):
     tok_rows = tokens.shape[0]
     width = tokens.shape[1]
@@ -39,14 +78,13 @@
     upstream = cotangent.astype(jnp.float32)
     q_home = (upstream * share_home[:, None]).astype(jnp.bfloat16)
     q_away = (upstream * share_away[:, None]).astype(jnp.bfloat16)
-    gate_full, up_full, down_full = (
-        lax.all_gather(w_gate, "replica", axis=1, tiled=True),
-        lax.all_gather(w_up, "replica", axis=1, tiled=True),
-        lax.all_gather(w_down, "replica", axis=1, tiled=True),
+    shard_rows, hidden_units = w_gate.shape[1], w_gate.shape[2]
+    full = ring_gather(
+        jnp.stack([w_gate[0], w_up[0], w_down[0].reshape(shard_rows, hidden_units)])
     )
-    gate_w = gate_full.reshape(gate_full.shape[1], gate_full.shape[2])
-    up_w = up_full.reshape(up_full.shape[1], up_full.shape[2])
-    down_w = down_full.reshape(down_full.shape[1], down_full.shape[2])
+    gate_w = full[:, 0].reshape(-1, hidden_units)
+    up_w = full[:, 1].reshape(-1, hidden_units)
+    down_w = full[:, 2].reshape(-1, w_down.shape[1], w_down.shape[2]).reshape(-1, w_down.shape[2])
     target = partner[:, 0]
     onehot_rows = (target[:, None] == jnp.arange(expert_count, dtype=jnp.int32)[None, :]).astype(
         jnp.int32
@@ -93,14 +131,12 @@
     token_grad = (grad_home + grad_away).astype(jnp.bfloat16)
     flat_hidden = hidden_away.reshape(expert_count * capacity, -1)
     flat_q = q_there.reshape(expert_count * capacity, width)
-    grad_down = lax.psum_scatter(
-        (
-            lax.dot_general(hidden_home, q_home, contract, preferred_element_type=jnp.float32)
-            + lax.dot_general(flat_hidden, flat_q, contract, preferred_element_type=jnp.float32)
-        ).astype(jnp.bfloat16),
-        "replica",
-        scatter_dimension=0,
-        tiled=True,
+    partial = lax.dot_general(
+        hidden_home, q_home, contract, preferred_element_type=jnp.float32
+    ) + lax.dot_general(flat_hidden, flat_q, contract, preferred_element_type=jnp.float32)
+    n_rep = lax.axis_size("replica")
+    grad_down = ring_reduce_scatter(partial.reshape(n_rep, -1, partial.shape[1])).astype(
+        jnp.bfloat16
     )
     return (token_grad, grad_down[None])
 

time: 333 us -> 438 us (1.32)
  local copies, waits for them, and re-layouts: 8.85 us -> 66.8 us
  starting transfers between devices: 23.7 us -> 80.4 us
  other arithmetic: 3.09 us -> 25.9 us
  waiting for transfers between devices: 251 us -> 233 us
  between operations: 14.7 us -> 2.36 us
    ppermute x0 -> x30, waiting for transfers between devices: none -> 213 us  [the longest x15 136 us: ring_gather(): pieces.append(lax.ppermute(pieces[-1], ('expert', 'replica'), perm))]
    all_gather x3 -> x0, waiting for transfers between devices: 161 us -> none  [the longest x1 73.8 us: local(): lax.all_gather(w_up, 'replica', axis=1, tiled=True)]
    ppermute x0 -> x30, starting transfers between devices: none -> 60 us  [the longest x15 30.7 us: ring_gather(): pieces.append(lax.ppermute(pieces[-1], ('expert', 'replica'), perm))]
    reduce_scatter x1 -> x0, waiting for transfers between devices: 42.9 us -> none  [local(): lax.psum_scatter((lax.dot_general(hidden_home, q_home, contract, preferre...]
    unnamed x24 -> x57, local copies, waits for them, and re-layouts: 1.68 us -> 33.6 us
    convert_element_type x0 -> x14, other arithmetic: none -> 15.4 us  [ring_reduce_scatter(): recv = lax.ppermute(acc.astype(jnp.bfloat16), ('expert', 'replica'), perm)]
    all_to_all x1, waiting for transfers between devices: 10.9 us -> 0.01 us  [local(): lax.all_to_all(grad_there.astype(jnp.bfloat16).reshape(expert_count, item...]
    gather x0 -> x1, local copies, waits for them, and re-layouts: none -> 10.5 us  [ring_gather(): return jnp.take(stacked, order, axis=0)]
  transfers between devices with their start and end apart: 7 -> 33, of which waited for: 7 -> 28; matrix products, arithmetic and copies ran while one was open for 12% -> 17% of each run, Pallas kernels for 0% -> 0%
where the time goes in v2:
time: 438 us; the launch traced here: 435 us
  waiting for transfers between devices  233 us (53%)
  starting transfers between devices  80.4 us (18%)
  local copies, waits for them, and re-layouts  66.8 us (15%)
  matrix products  26.5 us (6%)
  other arithmetic  25.9 us (6%)
    ppermute x15, waiting for transfers between devices, ring_gather(): pieces.append(lax.ppermute(pieces[-1], ('expert', 'replica'), perm))  136 us
    ppermute x15, waiting for transfers between devices, ring_reduce_scatter(): recv = lax.ppermute(acc.astype(jnp.bfloat16), ('expert', 'replica'), perm)  77.3 us
    unnamed x57, local copies, waits for them, and re-layouts  33.6 us
    ppermute x15, starting transfers between devices, ring_gather(): pieces.append(lax.ppermute(pieces[-1], ('expert', 'replica'), perm))  30.7 us
    ppermute x15, starting transfers between devices, ring_reduce_scatter(): recv = lax.ppermute(acc.astype(jnp.bfloat16), ('expert', 'replica'), perm)  29.2 us
    dot_general x6, matrix products, against_rows(): lax.dot_general(left, matrix, (((1,), (1,)), ((), ())), preferred_element...  18.1 us
    convert_element_type x14, other arithmetic, ring_reduce_scatter(): recv = lax.ppermute(acc.astype(jnp.bfloat16), ('expert', 'replica'), perm)  15.4 us
    gather x1, local copies, waits for them, and re-layouts, ring_gather(): return jnp.take(stacked, order, axis=0)  10.5 us
  transfers between devices with their start and end apart: 33, of which 28 were waited for; matrix products, arithmetic and copies ran while one was open for 17% of the time, Pallas kernels for 0%

profile of v2, /device:TPU:6, one launch (start us, length us, event | category | flops | bytes accessed | tf_op | source)
XLA Modules:
  0.0 435.1 jit_solution(13580630350366776687)
XLA Ops:
  7.8 17.0 %collective-permute-done = bf16[3,160,768]{2,1,0:T(8,128)(2,1)S(1)} collective-permute-done((bf16[3,160,768]{2,1,0:T(8,128)(2,1)S(1)}, bf16[3,160,768]{2,1,0:T(8,128)(2,1)S(1)}, u32[]{:S(2)}, u32[]{:S(2)}) %collective-permute-start) | collective-permute-done | bytes 737312 | tf_op jit(solution)/shard_map/ppermute | solution.py:44
  26.8 12.6 %collective-permute-done.1 = bf16[3,160,768]{2,1,0:T(8,128)(2,1)S(1)} collective-permute-done((bf16[3,160,768]{2,1,0:T(8,128)(2,1)S(1)}, bf16[3,160,768]{2,1,0:T(8,128)(2,1)S(1)}, u32[]{:S(2)}, u32[]{:S(2)}) %collective-permute-start.1) | collective-permute-done | bytes 737312 | tf_op jit(solution)/shard_map/ppermute | solution.py:44
  41.3 12.6 %collective-permute-done.2 = bf16[3,160,768]{2,1,0:T(8,128)(2,1)S(1)} collective-permute-done((bf16[3,160,768]{2,1,0:T(8,128)(2,1)S(1)}, bf16[3,160,768]{2,1,0:T(8,128)(2,1)S(1)}, u32[]{:S(2)}, u32[]{:S(2)}) %collective-permute-start.2) | collective-permute-done | bytes 737312 | tf_op jit(solution)/shard_map/ppermute | solution.py:44
  55.9 12.6 %collective-permute-done.3 = bf16[3,160,768]{2,1,0:T(8,128)(2,1)S(1)} collective-permute-done((bf16[3,160,768]{2,1,0:T(8,128)(2,1)S(1)}, bf16[3,160,768]{2,1,0:T(8,128)(2,1)S(1)}, u32[]{:S(2)}, u32[]{:S(2)}) %collective-permute-start.3) | collective-permute-done | bytes 737312 | tf_op jit(solution)/shard_map/ppermute | solution.py:44
  70.4 12.6 %collective-permute-done.4 = bf16[3,160,768]{2,1,0:T(8,128)(2,1)S(1)} collective-permute-done((bf16[3,160,768]{2,1,0:T(8,128)(2,1)S(1)}, bf16[3,160,768]{2,1,0:T(8,128)(2,1)S(1)}, u32[]{:S(2)}, u32[]{:S(2)}) %collective-permute-start.4) | collective-permute-done | bytes 737312 | tf_op jit(solution)/shard_map/ppermute | solution.py:44
  85.0 12.6 %collective-permute-done.5 = bf16[3,160,768]{2,1,0:T(8,128)(2,1)S(1)} collective-permute-done((bf16[3,160,768]{2,1,0:T(8,128)(2,1)S(1)}, bf16[3,160,768]{2,1,0:T(8,128)(2,1)S(1)}, u32[]{:S(2)}, u32[]{:S(2)}) %collective-permute-start.5) | collective-permute-done | bytes 737312 | tf_op jit(solution)/shard_map/ppermute | solution.py:44
  100.4 12.7 %collective-permute-done.6 = bf16[3,160,768]{2,1,0:T(8,128)(2,1)} collective-permute-done((bf16[3,160,768]{2,1,0:T(8,128)(2,1)S(1)}, bf16[3,160,768]{2,1,0:T(8,128)(2,1)}, u32[]{:S(2)}, u32[]{:S(2)}) %collective-permute-start.6) | collective-permute-done | bytes 737312 | tf_op jit(solution)/shard_map/ppermute | solution.py:44
  116.8 11.2 %collective-permute-done.7 = bf16[3,160,768]{2,1,0:T(8,128)(2,1)} collective-permute-done((bf16[3,160,768]{2,1,0:T(8,128)(2,1)}, bf16[3,160,768]{2,1,0:T(8,128)(2,1)}, u32[]{:S(2)}, u32[]{:S(2)}) %collective-permute-start.7) | collective-permute-done | bytes 737312 | tf_op jit(solution)/shard_map/ppermute | solution.py:44
  132.3 7.6 %all-to-all-start.1 = ((bf16[32,5,2560]{2,1,0:T(8,128)(2,1)}), bf16[32,5,2560]{2,1,0:T(8,128)(2,1)S(1)}, u32[]{:S(2)}, u32[]{:S(2)}) async-start(bf16[32,5,2560]{2,1,0:T(8,128)(2,1)} %reshape.102), calls=%async_computation.1 | async-start | bytes 2621440 | tf_op jit(solution)/shard_map/all_to_all | solution.py:108
  148.5 9.5 %all-to-all-done.1 = bf16[32,5,2560]{2,1,0:T(8,128)(2,1)S(1)} async-done(((bf16[32,5,2560]{2,1,0:T(8,128)(2,1)}), bf16[32,5,2560]{2,1,0:T(8,128)(2,1)S(1)}, u32[]{:S(2)}, u32[]{:S(2)}) %all-to-all-start.1) | async-done | bytes 819232 | tf_op jit(solution)/shard_map/all_to_all | solution.py:108
  171.9 10.5 %all-to-all-done = bf16[32,5,2560]{2,1,0:T(8,128)(2,1)} async-done(((bf16[32,5,2560]{2,1,0:T(8,128)(2,1)}), bf16[32,5,2560]{2,1,0:T(8,128)(2,1)}, u32[]{:S(2)}, u32[]{:S(2)}) %all-to-all-start) | async-done | bytes 819232 | tf_op jit(solution)/shard_map/all_to_all | solution.py:109
  193.9 6.7 %collective-permute-done.11 = bf16[3,160,768]{2,1,0:T(8,128)(2,1)S(1)} collective-permute-done((bf16[3,160,768]{2,1,0:T(8,128)(2,1)}, bf16[3,160,768]{2,1,0:T(8,128)(2,1)S(1)}, u32[]{:S(2)}, u32[]{:S(2)}) %collective-permute-start.11) | collective-permute-done | bytes 737312 | tf_op jit(solution)/shard_map/ppermute | solution.py:44
  208.7 6.5 %collective-permute-done.12 = bf16[3,160,768]{2,1,0:T(8,128)(2,1)S(1)} collective-permute-done((bf16[3,160,768]{2,1,0:T(8,128)(2,1)S(1)}, bf16[3,160,768]{2,1,0:T(8,128)(2,1)S(1)}, u32[]{:S(2)}, u32[]{:S(2)}) %collective-permute-start.12) | collective-permute-done | bytes 737312 | tf_op jit(solution)/shard_map/ppermute | solution.py:44
  234.6 9.7 %collective-permute-done.14 = bf16[3,160,768]{2,1,0:T(8,128)(2,1)S(1)} collective-permute-done((bf16[3,160,768]{2,1,0:T(8,128)(2,1)S(1)}, bf16[3,160,768]{2,1,0:T(8,128)(2,1)S(1)}, u32[]{:S(2)}, u32[]{:S(2)}) %collective-permute-start.14) | collective-permute-done | bytes 737312 | tf_op jit(solution)/shard_map/ppermute | solution.py:44
  245.2 10.5 %gather_fusion = bf16[16,3,160,768]{3,2,1,0:T(8,128)(2,1)} fusion(bf16[16,3,160,768]{3,2,1,0:T(8,128)(2,1)} %bitcast_dynamic-update-slice_fusion, s32[1024]{0:T(1024)S(1)} %pad_clamp_fusion), kind=kCustom, calls=%fused_computation | custom fusion | bytes 23593024 | tf_op jit(solution)/shard_map/jit(_take)/gather | solution.py:47
  275.2 7.3 %collective-permute-done.15 = bf16[48,2560]{1,0:T(8,128)(2,1)S(1)} collective-permute-done((bf16[48,2560]{1,0:T(8,128)(2,1)S(1)}, bf16[48,2560]{1,0:T(8,128)(2,1)S(1)}, u32[]{:S(2)}, u32[]{:S(2)}) %collective-permute-start.15) | collective-permute-done | bytes 245792 | tf_op jit(solution)/shard_map/ppermute | solution.py:60
  285.6 7.3 %collective-permute-done.16 = bf16[48,2560]{1,0:T(8,128)(2,1)S(1)} collective-permute-done((bf16[48,2560]{1,0:T(8,128)(2,1)S(1)}, bf16[48,2560]{1,0:T(8,128)(2,1)S(1)}, u32[]{:S(2)}, u32[]{:S(2)}) %collective-permute-start.16) | collective-permute-done | bytes 245792 | tf_op jit(solution)/shard_map/ppermute | solution.py:60
  296.0 7.3 %collective-permute-done.17 = bf16[48,2560]{1,0:T(8,128)(2,1)S(1)} collective-permute-done((bf16[48,2560]{1,0:T(8,128)(2,1)S(1)}, bf16[48,2560]{1,0:T(8,128)(2,1)S(1)}, u32[]{:S(2)}, u32[]{:S(2)}) %collective-permute-start.17) | collective-permute-done | bytes 245792 | tf_op jit(solution)/shard_map/ppermute | solution.py:60
  306.3 7.3 %collective-permute-done.18 = bf16[48,2560]{1,0:T(8,128)(2,1)S(1)} collective-permute-done((bf16[48,2560]{1,0:T(8,128)(2,1)S(1)}, bf16[48,2560]{1,0:T(8,128)(2,1)S(1)}, u32[]{:S(2)}, u32[]{:S(2)}) %collective-permute-start.18) | collective-permute-done | bytes 245792 | tf_op jit(solution)/shard_map/ppermute | solution.py:60
  316.7 7.3 %collective-permute-done.19 = bf16[48,2560]{1,0:T(8,128)(2,1)S(1)} collective-permute-done((bf16[48,2560]{1,0:T(8,128)(2,1)S(1)}, bf16[48,2560]{1,0:T(8,128)(2,1)S(1)}, u32[]{:S(2)}, u32[]{:S(2)}) %collective-permute-start.19) | collective-permute-done | bytes 245792 | tf_op jit(solution)/shard_map/ppermute | solution.py:60
  327.1 7.3 %collective-permute-done.20 = bf16[48,2560]{1,0:T(8,128)(2,1)S(1)} collective-permute-done((bf16[48,2560]{1,0:T(8,128)(2,1)S(1)}, bf16[48,2560]{1,0:T(8,128)(2,1)S(1)}, u32[]{:S(2)}, u32[]{:S(2)}) %collective-permute-start.20) | collective-permute-done | bytes 245792 | tf_op jit(solution)/shard_map/ppermute | solution.py:60
  337.5 7.3 %collective-permute-done.21 = bf16[48,2560]{1,0:T(8,128)(2,1)S(1)} collective-permute-done((bf16[48,2560]{1,0:T(8,128)(2,1)S(1)}, bf16[48,2560]{1,0:T(8,128)(2,1)S(1)}, u32[]{:S(2)}, u32[]{:S(2)}) %collective-permute-start.21) | collective-permute-done | bytes 245792 | tf_op jit(solution)/shard_map/ppermute | solution.py:60
  348.0 8.0 %reshape_reshape_squeeze.3 = bf16[768,2560]{1,0:T(8,128)(2,1)} reshape(bf16[16,1,160,768]{3,2,1,0:T(8,128)(2,1)} %get-tuple-element.4) | data formatting | bytes 7864320 | tf_op jit(solution)/shard_map/reshape;reshape;squeeze | solution.py:87
  384.8 6.6 %all-to-all-start.2 = ((bf16[32,5,2560]{2,1,0:T(8,128)(2,1)}), bf16[32,5,2560]{2,1,0:T(8,128)(2,1)}, u32[]{:S(2)}, u32[]{:S(2)}) async-start(bf16[32,5,2560]{2,1,0:T(8,128)(2,1)} %reshape.104), calls=%async_computation.2 | async-start | bytes 2621440 | tf_op jit(solution)/shard_map/all_to_all | solution.py:114
  (152 shorter events, 201.6 us)
Async XLA Ops:
  4.0 20.8 %collective-permute-start = (bf16[3,160,768]{2,1,0:T(8,128)(2,1)S(1)}, bf16[3,160,768]{2,1,0:T(8,128)(2,1)S(1)}, u32[]{:S(2)}, u32[]{:S(2)}) collective-permute-start(bf16[3,160,768]{2,1,0:T(8,128)(2,1)S(1)} %constant_dynamic-update-slice_fusion), channel_id=1, source_target_pairs={{0,1},{1,2},{2,3},{3,4},{4,5},{5,6},{6,7},{7,8},{8,9},{9,10},{10,1... | collective-permute-start | bytes 2211848 | tf_op jit(solution)/shard_map/ppermute | solution.py:44
  24.8 14.6 %collective-permute-start.1 = (bf16[3,160,768]{2,1,0:T(8,128)(2,1)S(1)}, bf16[3,160,768]{2,1,0:T(8,128)(2,1)S(1)}, u32[]{:S(2)}, u32[]{:S(2)}) collective-permute-start(bf16[3,160,768]{2,1,0:T(8,128)(2,1)S(1)} %collective-permute-done), channel_id=1, source_target_pairs={{0,1},{1,2},{2,3},{3,4},{4,5},{5,6},{6,7},{7,8},{8,9},{9,10},{10,1... | collective-permute-start | bytes 2211848 | tf_op jit(solution)/shard_map/ppermute | solution.py:44
  39.4 14.6 %collective-permute-start.2 = (bf16[3,160,768]{2,1,0:T(8,128)(2,1)S(1)}, bf16[3,160,768]{2,1,0:T(8,128)(2,1)S(1)}, u32[]{:S(2)}, u32[]{:S(2)}) collective-permute-start(bf16[3,160,768]{2,1,0:T(8,128)(2,1)S(1)} %collective-permute-done.1), channel_id=1, source_target_pairs={{0,1},{1,2},{2,3},{3,4},{4,5},{5,6},{6,7},{7,8},{8,9},{9,10},{10,1... | collective-permute-start | bytes 2211848 | tf_op jit(solution)/shard_map/ppermute | solution.py:44
  53.9 14.6 %collective-permute-start.3 = (bf16[3,160,768]{2,1,0:T(8,128)(2,1)S(1)}, bf16[3,160,768]{2,1,0:T(8,128)(2,1)S(1)}, u32[]{:S(2)}, u32[]{:S(2)}) collective-permute-start(bf16[3,160,768]{2,1,0:T(8,128)(2,1)S(1)} %collective-permute-done.2), channel_id=1, source_target_pairs={{0,1},{1,2},{2,3},{3,4},{4,5},{5,6},{6,7},{7,8},{8,9},{9,10},{10,1... | collective-permute-start | bytes 2211848 | tf_op jit(solution)/shard_map/ppermute | solution.py:44
  68.5 14.6 %collective-permute-start.4 = (bf16[3,160,768]{2,1,0:T(8,128)(2,1)S(1)}, bf16[3,160,768]{2,1,0:T(8,128)(2,1)S(1)}, u32[]{:S(2)}, u32[]{:S(2)}) collective-permute-start(bf16[3,160,768]{2,1,0:T(8,128)(2,1)S(1)} %collective-permute-done.3), channel_id=1, source_target_pairs={{0,1},{1,2},{2,3},{3,4},{4,5},{5,6},{6,7},{7,8},{8,9},{9,10},{10,1... | collective-permute-start | bytes 2211848 | tf_op jit(solution)/shard_map/ppermute | solution.py:44
  83.1 14.6 %collective-permute-start.5 = (bf16[3,160,768]{2,1,0:T(8,128)(2,1)S(1)}, bf16[3,160,768]{2,1,0:T(8,128)(2,1)S(1)}, u32[]{:S(2)}, u32[]{:S(2)}) collective-permute-start(bf16[3,160,768]{2,1,0:T(8,128)(2,1)S(1)} %collective-permute-done.4), channel_id=1, source_target_pairs={{0,1},{1,2},{2,3},{3,4},{4,5},{5,6},{6,7},{7,8},{8,9},{9,10},{10,1... | collective-permute-start | bytes 2211848 | tf_op jit(solution)/shard_map/ppermute | solution.py:44
  98.5 14.7 %collective-permute-start.6 = (bf16[3,160,768]{2,1,0:T(8,128)(2,1)S(1)}, bf16[3,160,768]{2,1,0:T(8,128)(2,1)}, u32[]{:S(2)}, u32[]{:S(2)}) collective-permute-start(bf16[3,160,768]{2,1,0:T(8,128)(2,1)S(1)} %collective-permute-done.5), channel_id=1, source_target_pairs={{0,1},{1,2},{2,3},{3,4},{4,5},{5,6},{6,7},{7,8},{8,9},{9,10},{10,1... | collective-permute-start | bytes 2211848 | tf_op jit(solution)/shard_map/ppermute | solution.py:44
  113.2 14.9 %collective-permute-start.7 = (bf16[3,160,768]{2,1,0:T(8,128)(2,1)}, bf16[3,160,768]{2,1,0:T(8,128)(2,1)}, u32[]{:S(2)}, u32[]{:S(2)}) collective-permute-start(bf16[3,160,768]{2,1,0:T(8,128)(2,1)} %collective-permute-done.6), channel_id=1, source_target_pairs={{0,1},{1,2},{2,3},{3,4},{4,5},{5,6},{6,7},{7,8},{8,9},{9,10},{10,1... | collective-permute-start | bytes 2211848 | tf_op jit(solution)/shard_map/ppermute | solution.py:44
  128.0 14.9 %collective-permute-start.8 = (bf16[3,160,768]{2,1,0:T(8,128)(2,1)}, bf16[3,160,768]{2,1,0:T(8,128)(2,1)}, u32[]{:S(2)}, u32[]{:S(2)}) collective-permute-start(bf16[3,160,768]{2,1,0:T(8,128)(2,1)} %collective-permute-done.7), channel_id=1, source_target_pairs={{0,1},{1,2},{2,3},{3,4},{4,5},{5,6},{6,7},{7,8},{8,9},{9,10},{10,1... | collective-permute-start | bytes 2211848 | tf_op jit(solution)/shard_map/ppermute | solution.py:44
  132.3 25.7 %all-to-all-start.1 = ((bf16[32,5,2560]{2,1,0:T(8,128)(2,1)}), bf16[32,5,2560]{2,1,0:T(8,128)(2,1)S(1)}, u32[]{:S(2)}, u32[]{:S(2)}) async-start(bf16[32,5,2560]{2,1,0:T(8,128)(2,1)} %reshape.102), calls=%async_computation.1 | async-start | bytes 2621440 | tf_op jit(solution)/shard_map/all_to_all | solution.py:108
  142.9 21.5 %collective-permute-start.9 = (bf16[3,160,768]{2,1,0:T(8,128)(2,1)}, bf16[3,160,768]{2,1,0:T(8,128)(2,1)}, u32[]{:S(2)}, u32[]{:S(2)}) collective-permute-start(bf16[3,160,768]{2,1,0:T(8,128)(2,1)} %collective-permute-done.8), channel_id=1, source_target_pairs={{0,1},{1,2},{2,3},{3,4},{4,5},{5,6},{6,7},{7,8},{8,9},{9,10},{10,1... | collective-permute-start | bytes 2211848 | tf_op jit(solution)/shard_map/ppermute | solution.py:44
  158.0 24.4 %all-to-all-start = ((bf16[32,5,2560]{2,1,0:T(8,128)(2,1)}), bf16[32,5,2560]{2,1,0:T(8,128)(2,1)}, u32[]{:S(2)}, u32[]{:S(2)}) async-start(bf16[32,5,2560]{2,1,0:T(8,128)(2,1)} %reshape.100), calls=%async_computation | async-start | bytes 2621440 | tf_op jit(solution)/shard_map/all_to_all | solution.py:109
  164.4 21.5 %collective-permute-start.10 = (bf16[3,160,768]{2,1,0:T(8,128)(2,1)}, bf16[3,160,768]{2,1,0:T(8,128)(2,1)}, u32[]{:S(2)}, u32[]{:S(2)}) collective-permute-start(bf16[3,160,768]{2,1,0:T(8,128)(2,1)} %collective-permute-done.9), channel_id=1, source_target_pairs={{0,1},{1,2},{2,3},{3,4},{4,5},{5,6},{6,7},{7,8},{8,9},{9,10},{10,1... | collective-permute-start | bytes 2211848 | tf_op jit(solution)/shard_map/ppermute | solution.py:44
  185.9 14.8 %collective-permute-start.11 = (bf16[3,160,768]{2,1,0:T(8,128)(2,1)}, bf16[3,160,768]{2,1,0:T(8,128)(2,1)S(1)}, u32[]{:S(2)}, u32[]{:S(2)}) collective-permute-start(bf16[3,160,768]{2,1,0:T(8,128)(2,1)} %collective-permute-done.10), channel_id=1, source_target_pairs={{0,1},{1,2},{2,3},{3,4},{4,5},{5,6},{6,7},{7,8},{8,9},{9,10},{10,1... | collective-permute-start | bytes 2211848 | tf_op jit(solution)/shard_map/ppermute | solution.py:44
  200.6 14.6 %collective-permute-start.12 = (bf16[3,160,768]{2,1,0:T(8,128)(2,1)S(1)}, bf16[3,160,768]{2,1,0:T(8,128)(2,1)S(1)}, u32[]{:S(2)}, u32[]{:S(2)}) collective-permute-start(bf16[3,160,768]{2,1,0:T(8,128)(2,1)S(1)} %collective-permute-done.11), channel_id=1, source_target_pairs={{0,1},{1,2},{2,3},{3,4},{4,5},{5,6},{6,7},{7,8},{8,9},{9,10},{10,1... | collective-permute-start | bytes 2211848 | tf_op jit(solution)/shard_map/ppermute | solution.py:44
  215.2 14.6 %collective-permute-start.13 = (bf16[3,160,768]{2,1,0:T(8,128)(2,1)S(1)}, bf16[3,160,768]{2,1,0:T(8,128)(2,1)S(1)}, u32[]{:S(2)}, u32[]{:S(2)}) collective-permute-start(bf16[3,160,768]{2,1,0:T(8,128)(2,1)S(1)} %collective-permute-done.12), channel_id=1, source_target_pairs={{0,1},{1,2},{2,3},{3,4},{4,5},{5,6},{6,7},{7,8},{8,9},{9,10},{10,1... | collective-permute-start | bytes 2211848 | tf_op jit(solution)/shard_map/ppermute | solution.py:44
  229.8 14.6 %collective-permute-start.14 = (bf16[3,160,768]{2,1,0:T(8,128)(2,1)S(1)}, bf16[3,160,768]{2,1,0:T(8,128)(2,1)S(1)}, u32[]{:S(2)}, u32[]{:S(2)}) collective-permute-start(bf16[3,160,768]{2,1,0:T(8,128)(2,1)S(1)} %collective-permute-done.13), channel_id=1, source_target_pairs={{0,1},{1,2},{2,3},{3,4},{4,5},{5,6},{6,7},{7,8},{8,9},{9,10},{10,1... | collective-permute-start | bytes 2211848 | tf_op jit(solution)/shard_map/ppermute | solution.py:44
  273.3 9.3 %collective-permute-start.15 = (bf16[48,2560]{1,0:T(8,128)(2,1)S(1)}, bf16[48,2560]{1,0:T(8,128)(2,1)S(1)}, u32[]{:S(2)}, u32[]{:S(2)}) collective-permute-start(bf16[48,2560]{1,0:T(8,128)(2,1)S(1)} %fusion.28), channel_id=1, source_target_pairs={{0,1},{1,2},{2,3},{3,4},{4,5},{5,6},{6,7},{7,8},{8,9},{9,10},{10,1... | collective-permute-start | bytes 737288 | tf_op jit(solution)/shard_map/ppermute | solution.py:60
  345.9 10.1 %collective-permute-start.22 = (bf16[48,2560]{1,0:T(8,128)(2,1)S(1)}, bf16[48,2560]{1,0:T(8,128)(2,1)S(1)}, u32[]{:S(2)}, u32[]{:S(2)}) collective-permute-start(bf16[48,2560]{1,0:T(8,128)(2,1)S(1)} %fusion.13), channel_id=1, source_target_pairs={{0,1},{1,2},{2,3},{3,4},{4,5},{5,6},{6,7},{7,8},{8,9},{9,10},{10,1... | collective-permute-start | bytes 737288 | tf_op jit(solution)/shard_map/ppermute | solution.py:60
  357.2 9.4 %collective-permute-start.23 = (bf16[48,2560]{1,0:T(8,128)(2,1)S(1)}, bf16[48,2560]{1,0:T(8,128)(2,1)S(1)}, u32[]{:S(2)}, u32[]{:S(2)}) collective-permute-start(bf16[48,2560]{1,0:T(8,128)(2,1)S(1)} %fusion.12), channel_id=1, source_target_pairs={{0,1},{1,2},{2,3},{3,4},{4,5},{5,6},{6,7},{7,8},{8,9},{9,10},{10,1... | collective-permute-start | bytes 737288 | tf_op jit(solution)/shard_map/ppermute | solution.py:60
  378.1 13.3 %collective-permute-start.25 = (bf16[48,2560]{1,0:T(8,128)(2,1)S(1)}, bf16[48,2560]{1,0:T(8,128)(2,1)S(1)}, u32[]{:S(2)}, u32[]{:S(2)}) collective-permute-start(bf16[48,2560]{1,0:T(8,128)(2,1)S(1)} %fusion.10), channel_id=1, source_target_pairs={{0,1},{1,2},{2,3},{3,4},{4,5},{5,6},{6,7},{7,8},{8,9},{9,10},{10,1... | collective-permute-start | bytes 737288 | tf_op jit(solution)/shard_map/ppermute | solution.py:60
  384.8 32.1 %all-to-all-start.2 = ((bf16[32,5,2560]{2,1,0:T(8,128)(2,1)}), bf16[32,5,2560]{2,1,0:T(8,128)(2,1)}, u32[]{:S(2)}, u32[]{:S(2)}) async-start(bf16[32,5,2560]{2,1,0:T(8,128)(2,1)} %reshape.104), calls=%async_computation.2 | async-start | bytes 2621440 | tf_op jit(solution)/shard_map/all_to_all | solution.py:114
  392.6 9.4 %collective-permute-start.26 = (bf16[48,2560]{1,0:T(8,128)(2,1)S(1)}, bf16[48,2560]{1,0:T(8,128)(2,1)S(1)}, u32[]{:S(2)}, u32[]{:S(2)}) collective-permute-start(bf16[48,2560]{1,0:T(8,128)(2,1)S(1)} %fusion.9), channel_id=1, source_target_pairs={{0,1},{1,2},{2,3},{3,4},{4,5},{5,6},{6,7},{7,8},{8,9},{9,10},{10,1... | collective-permute-start | bytes 737288 | tf_op jit(solution)/shard_map/ppermute | solution.py:60
  413.5 9.4 %collective-permute-start.28 = (bf16[48,2560]{1,0:T(8,128)(2,1)S(1)}, bf16[48,2560]{1,0:T(8,128)(2,1)}, u32[]{:S(2)}, u32[]{:S(2)}) collective-permute-start(bf16[48,2560]{1,0:T(8,128)(2,1)S(1)} %fusion.7), channel_id=1, source_target_pairs={{0,1},{1,2},{2,3},{3,4},{4,5},{5,6},{6,7},{7,8},{8,9},{9,10},{10,1... | collective-permute-start | bytes 737288 | tf_op jit(solution)/shard_map/ppermute | solution.py:60
  (29 other events, 892.5 us)

commit v3 on v0

--- a/solution.py
+++ b/solution.py
@@ -25,6 +25,30 @@
     return (hidden, input_grad)
 
 
+def ring_gather(piece, axis):
+    n = lax.axis_size(axis)
+    idx = lax.axis_index(axis)
+    right = [(i, (i + 1) % n) for i in range(n)]
+    left = [(i, (i - 1) % n) for i in range(n)]
+    ahead = {0: piece}
+    r = l = piece
+    half = n // 2
+    steps = half if n % 2 == 1 else half - 1
+    for k in range(1, steps + 1):
+        r = lax.ppermute(r, axis, right)
+        l = lax.ppermute(l, axis, left)
+        ahead[n - k] = r
+        ahead[k] = l
+    if n % 2 == 0 and n > 1:
+        cut = piece.shape[-1] // 2
+        rh = lax.ppermute(r[..., :cut], axis, right)
+        lh = lax.ppermute(l[..., cut:], axis, left)
+        ahead[half] = jnp.concatenate([rh, lh], axis=-1)
+    stacked = jnp.stack([ahead[m] for m in range(n)])
+    order = (jnp.arange(n, dtype=jnp.int32) - idx) % n
+    return jnp.take(stacked, order, axis=0)
+
+
 def local(tokens, cotangent, partner, combine, counts, w_gate, w_up, w_down):
     tok_rows = tokens.shape[0]
     width = tokens.shape[1]
@@ -39,14 +63,14 @@
     upstream = cotangent.astype(jnp.float32)
     q_home = (upstream * share_home[:, None]).astype(jnp.bfloat16)
     q_away = (upstream * share_away[:, None]).astype(jnp.bfloat16)
-    gate_full, up_full, down_full = (
+    gate_full, up_full = (
         lax.all_gather(w_gate, "replica", axis=1, tiled=True),
         lax.all_gather(w_up, "replica", axis=1, tiled=True),
-        lax.all_gather(w_down, "replica", axis=1, tiled=True),
     )
+    down_full = ring_gather(w_down[0], "replica")
     gate_w = gate_full.reshape(gate_full.shape[1], gate_full.shape[2])
     up_w = up_full.reshape(up_full.shape[1], up_full.shape[2])
-    down_w = down_full.reshape(down_full.shape[1], down_full.shape[2])
+    down_w = down_full.reshape(-1, down_full.shape[2])
     target = partner[:, 0]
     onehot_rows = (target[:, None] == jnp.arange(expert_count, dtype=jnp.int32)[None, :]).astype(
         jnp.int32

time: 333 us -> 277 us (0.83)
  waiting for transfers between devices: 251 us -> 102 us
  starting transfers between devices: 23.7 us -> 87.3 us
  local copies, waits for them, and re-layouts: 8.85 us -> 37.9 us
    ppermute x0 -> x16, starting transfers between devices: none -> 64.9 us  [the longest x7 43.8 us: ring_gather(): l = lax.ppermute(l, axis, left)]
    all_gather x1 -> x0, waiting for transfers between devices: 64.9 us -> none  [local(): lax.all_gather(w_down, 'replica', axis=1, tiled=True)]
    all_gather x1, waiting for transfers between devices: 73.8 us -> 31.7 us  [local(): lax.all_gather(w_up, 'replica', axis=1, tiled=True)]
    ppermute x0 -> x16, waiting for transfers between devices: none -> 28 us  [the longest x7 17.3 us: ring_gather(): l = lax.ppermute(l, axis, left)]
    all_gather x1, waiting for transfers between devices: 22.6 us -> 0.01 us  [local(): lax.all_gather(w_gate, 'replica', axis=1, tiled=True)]
    reduce_scatter x1, waiting for transfers between devices: 42.9 us -> 21.8 us  [local(): lax.psum_scatter((lax.dot_general(hidden_home, q_home, contract, preferre...]
    unnamed x24 -> x60, local copies, waits for them, and re-layouts: 1.68 us -> 21.9 us
    all_to_all x1, waiting for transfers between devices: 17.6 us -> 0.01 us  [local(): lax.all_to_all(send_x, 'expert', split_axis=0, concat_axis=0, tiled=True)]
  transfers between devices with their start and end apart: 7 -> 22, of which waited for: 7 -> 10; matrix products, arithmetic and copies ran while one was open for 12% -> 20% of each run, Pallas kernels for 0% -> 0%
where the time goes in v3:
time: 277 us; the launch traced here: 275 us
  waiting for transfers between devices  102 us (37%)
  starting transfers between devices  87.3 us (32%)
  local copies, waits for them, and re-layouts  37.9 us (14%)
  matrix products  27 us (10%)
  between operations  15 us (5%)
  other arithmetic  6.36 us (2%)
    ppermute x7, starting transfers between devices, ring_gather(): l = lax.ppermute(l, axis, left)  43.8 us
    all_gather x1, waiting for transfers between devices, local(): lax.all_gather(w_up, 'replica', axis=1, tiled=True)  31.7 us
    unnamed x60, local copies, waits for them, and re-layouts  21.9 us
    reduce_scatter x1, waiting for transfers between devices, local(): lax.psum_scatter((lax.dot_general(hidden_home, q_home, contract, preferre...  21.8 us
    ppermute x7, waiting for transfers between devices, ring_gather(): l = lax.ppermute(l, axis, left)  17.3 us
    ppermute x7, starting transfers between devices, ring_gather(): r = lax.ppermute(r, axis, right)  13.4 us
    all_to_all x1, waiting for transfers between devices, local(): lax.all_to_all(grad_there.astype(jnp.bfloat16).reshape(expert_count, item...  13 us
    dot_general x6, matrix products, against_rows(): lax.dot_general(left, matrix, (((1,), (1,)), ((), ())), preferred_element...  12.5 us
  transfers between devices with their start and end apart: 22, of which 10 were waited for; matrix products, arithmetic and copies ran while one was open for 20% of the time, Pallas kernels for 0%

profile of v3, /device:TPU:6, one launch (start us, length us, event | category | flops | bytes accessed | tf_op | source)
XLA Modules:
  0.0 275.4 jit_solution(17153805396383461517)
XLA Ops:
  7.9 11.4 %collective-permute-start = (bf16[48,2560]{1,0:T(8,128)(2,1)}, bf16[48,2560]{1,0:T(8,128)(2,1)}, u32[]{:S(2)}, u32[]{:S(2)}) collective-permute-start(bf16[48,2560]{1,0:T(8,128)(2,1)} %bitcast.82), channel_id=1, source_target_pairs={{0,15},{1,0},{2,1},{3,2},{4,3},{5,4},{6,5},{7,6},{8,7},{9,8},{10,9... | collective-permute-start | bytes 737288 | tf_op jit(solution)/shard_map/ppermute | solution.py:39
  25.3 7.6 %all-to-all-start.1 = ((bf16[32,5,2560]{2,1,0:T(8,128)(2,1)}), bf16[32,5,2560]{2,1,0:T(8,128)(2,1)S(1)}, u32[]{:S(2)}, u32[]{:S(2)}) async-start(bf16[32,5,2560]{2,1,0:T(8,128)(2,1)} %reshape.136), calls=%async_computation.1 | async-start | bytes 2621440 | tf_op jit(solution)/shard_map/all_to_all | solution.py:94
  39.0 5.1 %collective-permute-start.1 = (bf16[48,2560]{1,0:T(8,128)(2,1)}, bf16[48,2560]{1,0:T(8,128)(2,1)}, u32[]{:S(2)}, u32[]{:S(2)}) collective-permute-start(bf16[48,2560]{1,0:T(8,128)(2,1)} %collective-permute-done), channel_id=1, source_target_pairs={{0,15},{1,0},{2,1},{3,2},{4,3},{5,4},{6,5},{7,6},{8,7},{9,8},{10,9... | collective-permute-start | bytes 737288 | tf_op jit(solution)/shard_map/ppermute | solution.py:39
  47.7 7.5 %collective-permute-done.1 = bf16[48,2560]{1,0:T(8,128)(2,1)} collective-permute-done((bf16[48,2560]{1,0:T(8,128)(2,1)}, bf16[48,2560]{1,0:T(8,128)(2,1)}, u32[]{:S(2)}, u32[]{:S(2)}) %collective-permute-start.1) | collective-permute-done | bytes 245792 | tf_op jit(solution)/shard_map/ppermute | solution.py:39
  55.2 5.6 %collective-permute-start.2 = (bf16[48,2560]{1,0:T(8,128)(2,1)}, bf16[48,2560]{1,0:T(8,128)(2,1)}, u32[]{:S(2)}, u32[]{:S(2)}) collective-permute-start(bf16[48,2560]{1,0:T(8,128)(2,1)} %collective-permute-done.1), channel_id=1, source_target_pairs={{0,15},{1,0},{2,1},{3,2},{4,3},{5,4},{6,5},{7,6},{8,7},{9,8},{10,9... | collective-permute-start | bytes 737288 | tf_op jit(solution)/shard_map/ppermute | solution.py:39
  62.8 7.4 %all-to-all-start = ((bf16[32,5,2560]{2,1,0:T(8,128)(2,1)}), bf16[32,5,2560]{2,1,0:T(8,128)(2,1)}, u32[]{:S(2)}, u32[]{:S(2)}) async-start(bf16[32,5,2560]{2,1,0:T(8,128)(2,1)} %reshape.134), calls=%async_computation | async-start | bytes 2621440 | tf_op jit(solution)/shard_map/all_to_all | solution.py:95
  71.9 5.4 %collective-permute-start.3 = (bf16[48,2560]{1,0:T(8,128)(2,1)}, bf16[48,2560]{1,0:T(8,128)(2,1)}, u32[]{:S(2)}, u32[]{:S(2)}) collective-permute-start(bf16[48,2560]{1,0:T(8,128)(2,1)} %collective-permute-done.2), channel_id=1, source_target_pairs={{0,15},{1,0},{2,1},{3,2},{4,3},{5,4},{6,5},{7,6},{8,7},{9,8},{10,9... | collective-permute-start | bytes 737288 | tf_op jit(solution)/shard_map/ppermute | solution.py:39
  82.5 5.9 %all-to-all-done = bf16[32,5,2560]{2,1,0:T(8,128)(2,1)} async-done(((bf16[32,5,2560]{2,1,0:T(8,128)(2,1)}), bf16[32,5,2560]{2,1,0:T(8,128)(2,1)}, u32[]{:S(2)}, u32[]{:S(2)}) %all-to-all-start) | async-done | bytes 819232 | tf_op jit(solution)/shard_map/all_to_all | solution.py:95
  89.8 5.1 %collective-permute-start.4 = (bf16[48,2560]{1,0:T(8,128)(2,1)}, bf16[48,2560]{1,0:T(8,128)(2,1)S(1)}, u32[]{:S(2)}, u32[]{:S(2)}) collective-permute-start(bf16[48,2560]{1,0:T(8,128)(2,1)} %collective-permute-done.3), channel_id=1, source_target_pairs={{0,15},{1,0},{2,1},{3,2},{4,3},{5,4},{6,5},{7,6},{8,7},{9,8},{10,9... | collective-permute-start | bytes 737288 | tf_op jit(solution)/shard_map/ppermute | solution.py:39
  98.6 3.3 %collective-permute-done.4 = bf16[48,2560]{1,0:T(8,128)(2,1)S(1)} collective-permute-done((bf16[48,2560]{1,0:T(8,128)(2,1)}, bf16[48,2560]{1,0:T(8,128)(2,1)S(1)}, u32[]{:S(2)}, u32[]{:S(2)}) %collective-permute-start.4) | collective-permute-done | bytes 245792 | tf_op jit(solution)/shard_map/ppermute | solution.py:39
  101.8 5.5 %collective-permute-start.5 = (bf16[48,2560]{1,0:T(8,128)(2,1)S(1)}, bf16[48,2560]{1,0:T(8,128)(2,1)S(1)}, u32[]{:S(2)}, u32[]{:S(2)}) collective-permute-start(bf16[48,2560]{1,0:T(8,128)(2,1)S(1)} %collective-permute-done.4), channel_id=1, source_target_pairs={{0,15},{1,0},{2,1},{3,2},{4,3},{5,4},{6,5},{7,6},{8,7},{9,8},{10,9... | collective-permute-start | bytes 737288 | tf_op jit(solution)/shard_map/ppermute | solution.py:39
  112.0 5.6 %collective-permute-start.6 = (bf16[48,2560]{1,0:T(8,128)(2,1)S(1)}, bf16[48,2560]{1,0:T(8,128)(2,1)S(1)}, u32[]{:S(2)}, u32[]{:S(2)}) collective-permute-start(bf16[48,2560]{1,0:T(8,128)(2,1)S(1)} %collective-permute-done.5), channel_id=1, source_target_pairs={{0,15},{1,0},{2,1},{3,2},{4,3},{5,4},{6,5},{7,6},{8,7},{9,8},{10,9... | collective-permute-start | bytes 737288 | tf_op jit(solution)/shard_map/ppermute | solution.py:39
  120.3 4.5 %collective-permute-done.6 = bf16[48,2560]{1,0:T(8,128)(2,1)S(1)} collective-permute-done((bf16[48,2560]{1,0:T(8,128)(2,1)S(1)}, bf16[48,2560]{1,0:T(8,128)(2,1)S(1)}, u32[]{:S(2)}, u32[]{:S(2)}) %collective-permute-start.6) | collective-permute-done | bytes 245792 | tf_op jit(solution)/shard_map/ppermute | solution.py:39
  124.8 5.6 %collective-permute-start.15 = (bf16[48,1280]{1,0:T(8,128)(2,1)S(1)}, bf16[48,1280]{1,0:T(8,128)(2,1)S(1)}, u32[]{:S(2)}, u32[]{:S(2)}) collective-permute-start(bf16[48,1280]{1,0:T(8,128)(2,1)S(1)} %slice.21), channel_id=1, source_target_pairs={{0,15},{1,0},{2,1},{3,2},{4,3},{5,4},{6,5},{7,6},{8,7},{9,8},{10,9... | collective-permute-start | bytes 368648 | tf_op jit(solution)/shard_map/ppermute | solution.py:45
  130.4 3.4 %collective-permute-done.13 = bf16[48,2560]{1,0:T(8,128)(2,1)S(1)} collective-permute-done((bf16[48,2560]{1,0:T(8,128)(2,1)S(1)}, bf16[48,2560]{1,0:T(8,128)(2,1)S(1)}, u32[]{:S(2)}, u32[]{:S(2)}) %collective-permute-start.13) | collective-permute-done | bytes 245792 | tf_op jit(solution)/shard_map/ppermute | solution.py:38
  136.7 7.2 %collective-permute-done.14 = bf16[48,1280]{1,0:T(8,128)(2,1)S(1)} collective-permute-done((bf16[48,1280]{1,0:T(8,128)(2,1)S(1)}, bf16[48,1280]{1,0:T(8,128)(2,1)S(1)}, u32[]{:S(2)}, u32[]{:S(2)}) %collective-permute-start.14) | collective-permute-done | bytes 122912 | tf_op jit(solution)/shard_map/ppermute | solution.py:44
  146.1 2.8 %fusion.6 = f32[128,768]{1,0:T(8,128)S(1)} fusion(bf16[128,2560]{1,0:T(8,128)(2,1)S(1)} %copy-done, bf16[1,2560,768]{2,1,0:T(8,128)(2,1)} %all-gather.5.cloned.1.call-done), kind=kOutput, calls=%fused_computation.8 | convolution fusion | flops 503316480 | bytes 4980736 | tf_op jit(solution)/shard_map/dot_general | solution.py:14
  148.9 31.7 %all-gather.3.cloned.1.call-done = bf16[1,2560,768]{2,1,0:T(8,128)(2,1)} async-done(((bf16[1,160,768]{2,1,0:T(8,128)(2,1)}), bf16[1,2560,768]{2,1,0:T(8,128)(2,1)}) %all-gather.3.cloned.1.call-update) | async-done | bytes 3932176 | tf_op jit(solution)/shard_map/all_gather | solution.py:68
  190.0 3.2 %add_convert_fusion = bf16[768,2560]{1,0:T(8,128)(2,1)} fusion(f32[768,2560]{1,0:T(8,128)S(1)} %fusion.32, bf16[160,2560]{1,0:T(8,128)(2,1)S(1)} %reshape.135, f32[160,768]{1,0:T(8,128)S(1)} %fusion.10, f32[160,768]{1,0:T(8,128)S(1)} %fusion.2), kind=kOutput, calls=%fused_computation.1 | convolution fusion | flops 633815040 | bytes 13598720 | tf_op jit(solution)/shard_map/dot_general | solution.py:123
  199.6 4.8 %gather_fusion = bf16[16,48,2560]{2,1,0:T(8,128)(2,1)} fusion(bf16[16,48,2560]{2,1,0:T(8,128)(2,1)} %bitcast_dynamic-update-slice_fusion, s32[1024]{0:T(1024)S(1)} %pad_clamp_fusion), kind=kCustom, calls=%fused_computation | custom fusion | bytes 7864384 | tf_op jit(solution)/shard_map/jit(_take)/gather | solution.py:49
  218.9 7.2 %all-to-all-start.2 = ((bf16[32,5,2560]{2,1,0:T(8,128)(2,1)}), bf16[32,5,2560]{2,1,0:T(8,128)(2,1)}, u32[]{:S(2)}, u32[]{:S(2)}) async-start(bf16[32,5,2560]{2,1,0:T(8,128)(2,1)} %reshape.138), calls=%async_computation.2 | async-start | bytes 2621440 | tf_op jit(solution)/shard_map/all_to_all | solution.py:100
  226.2 3.7 %fusion.4 = f32[128,2560]{1,0:T(8,128)S(1)} fusion(bf16[1,2560,768]{2,1,0:T(8,128)(2,1)} %all-gather.5.cloned.1.call-done, f32[128,768]{1,0:T(8,128)S(1)} %fusion.6, f32[128,768]{1,0:T(8,128)S(1)} %copy-done.14, f32[128,768]{1,0:T(8,128)S(1)} %copy-done.13), kind=kOutput, calls=%fused_computation.6 | convolution fusion | flops 504299520 | bytes 6422528 | tf_op jit(solution)/shard_map/dot_general | solution.py:8
  231.3 13.0 %all-to-all-done.2 = bf16[32,5,2560]{2,1,0:T(8,128)(2,1)} async-done(((bf16[32,5,2560]{2,1,0:T(8,128)(2,1)}), bf16[32,5,2560]{2,1,0:T(8,128)(2,1)}, u32[]{:S(2)}, u32[]{:S(2)}) %all-to-all-start.2) | async-done | bytes 819232 | tf_op jit(solution)/shard_map/all_to_all | solution.py:100
  247.0 21.8 %reduce-scatter.2.cloned.1.call-done = bf16[48,2560]{1,0:T(8,128)(2,1)} async-done(((bf16[768,2560]{1,0:T(8,128)(2,1)}), bf16[48,2560]{1,0:T(8,128)(2,1)}) %reduce-scatter.2.cloned.1.call-update) | async-done | bytes 245776 | tf_op jit(solution)/shard_map/reduce_scatter | solution.py:120
  (122 shorter events, 76.0 us)
Async XLA Ops:
  7.2 27.9 %copy-start.7 = (bf16[128,2560]{1,0:T(8,128)(2,1)S(1)}, bf16[128,2560]{1,0:T(8,128)(2,1)}, u32[]{:S(2)}) copy-start(bf16[128,2560]{1,0:T(8,128)(2,1)} %param.9) | copy-start | bytes 1966084
  7.2 138.9 %all-gather.5.cloned.1.call-start = ((), (), s32[]{:S(2)}) async-start(), calls=%async_computation.5 | async-start | bytes 4177920 | tf_op jit(solution)/shard_map/all_gather | solution.py:67
  7.9 31.0 %collective-permute-start = (bf16[48,2560]{1,0:T(8,128)(2,1)}, bf16[48,2560]{1,0:T(8,128)(2,1)}, u32[]{:S(2)}, u32[]{:S(2)}) collective-permute-start(bf16[48,2560]{1,0:T(8,128)(2,1)} %bitcast.82), channel_id=1, source_target_pairs={{0,15},{1,0},{2,1},{3,2},{4,3},{5,4},{6,5},{7,6},{8,7},{9,8},{10,9... | collective-permute-start | bytes 737288 | tf_op jit(solution)/shard_map/ppermute | solution.py:39
  19.4 24.8 %collective-permute-start.7 = (bf16[48,2560]{1,0:T(8,128)(2,1)}, bf16[48,2560]{1,0:T(8,128)(2,1)S(1)}, u32[]{:S(2)}, u32[]{:S(2)}) collective-permute-start(bf16[48,2560]{1,0:T(8,128)(2,1)} %bitcast.83), channel_id=1, source_target_pairs={{0,1},{1,2},{2,3},{3,4},{4,5},{5,6},{6,7},{7,8},{8,9},{9,10},{10,1... | collective-permute-start | bytes 737288 | tf_op jit(solution)/shard_map/ppermute | solution.py:38
  25.3 37.5 %all-to-all-start.1 = ((bf16[32,5,2560]{2,1,0:T(8,128)(2,1)}), bf16[32,5,2560]{2,1,0:T(8,128)(2,1)S(1)}, u32[]{:S(2)}, u32[]{:S(2)}) async-start(bf16[32,5,2560]{2,1,0:T(8,128)(2,1)} %reshape.136), calls=%async_computation.1 | async-start | bytes 2621440 | tf_op jit(solution)/shard_map/all_to_all | solution.py:94
  32.9 147.7 %all-gather.3.cloned.1.call-start = ((), (), s32[]{:S(2)}) async-start(), calls=%async_computation.4 | async-start | bytes 4177920 | tf_op jit(solution)/shard_map/all_gather | solution.py:68
  39.0 16.2 %collective-permute-start.1 = (bf16[48,2560]{1,0:T(8,128)(2,1)}, bf16[48,2560]{1,0:T(8,128)(2,1)}, u32[]{:S(2)}, u32[]{:S(2)}) collective-permute-start(bf16[48,2560]{1,0:T(8,128)(2,1)} %collective-permute-done), channel_id=1, source_target_pairs={{0,15},{1,0},{2,1},{3,2},{4,3},{5,4},{6,5},{7,6},{8,7},{9,8},{10,9... | collective-permute-start | bytes 737288 | tf_op jit(solution)/shard_map/ppermute | solution.py:39
  44.1 35.2 %copy-start.16 = (bf16[48,2560]{1,0:T(8,128)(2,1)}, bf16[48,2560]{1,0:T(8,128)(2,1)S(1)}, u32[]{:S(2)}) copy-start(bf16[48,2560]{1,0:T(8,128)(2,1)S(1)} %collective-permute-done.7) | copy-start | bytes 737284
  44.1 16.7 %collective-permute-start.8 = (bf16[48,2560]{1,0:T(8,128)(2,1)S(1)}, bf16[48,2560]{1,0:T(8,128)(2,1)S(1)}, u32[]{:S(2)}, u32[]{:S(2)}) collective-permute-start(bf16[48,2560]{1,0:T(8,128)(2,1)S(1)} %collective-permute-done.7), channel_id=1, source_target_pairs={{0,1},{1,2},{2,3},{3,4},{4,5},{5,6},{6,7},{7,8},{8,9},{9,10},{10,1... | collective-permute-start | bytes 737288 | tf_op jit(solution)/shard_map/ppermute | solution.py:38
  55.2 16.7 %collective-permute-start.2 = (bf16[48,2560]{1,0:T(8,128)(2,1)}, bf16[48,2560]{1,0:T(8,128)(2,1)}, u32[]{:S(2)}, u32[]{:S(2)}) collective-permute-start(bf16[48,2560]{1,0:T(8,128)(2,1)} %collective-permute-done.1), channel_id=1, source_target_pairs={{0,15},{1,0},{2,1},{3,2},{4,3},{5,4},{6,5},{7,6},{8,7},{9,8},{10,9... | collective-permute-start | bytes 737288 | tf_op jit(solution)/shard_map/ppermute | solution.py:39
  60.8 16.5 %collective-permute-start.9 = (bf16[48,2560]{1,0:T(8,128)(2,1)S(1)}, bf16[48,2560]{1,0:T(8,128)(2,1)}, u32[]{:S(2)}, u32[]{:S(2)}) collective-permute-start(bf16[48,2560]{1,0:T(8,128)(2,1)S(1)} %collective-permute-done.8), channel_id=1, source_target_pairs={{0,1},{1,2},{2,3},{3,4},{4,5},{5,6},{6,7},{7,8},{8,9},{9,10},{10,1... | collective-permute-start | bytes 737288 | tf_op jit(solution)/shard_map/ppermute | solution.py:38
  62.8 25.6 %all-to-all-start = ((bf16[32,5,2560]{2,1,0:T(8,128)(2,1)}), bf16[32,5,2560]{2,1,0:T(8,128)(2,1)}, u32[]{:S(2)}, u32[]{:S(2)}) async-start(bf16[32,5,2560]{2,1,0:T(8,128)(2,1)} %reshape.134), calls=%async_computation | async-start | bytes 2621440 | tf_op jit(solution)/shard_map/all_to_all | solution.py:95
  70.2 198.7 %reduce-scatter.2.cloned.1.call-start = ((), (), s32[]{:S(2)}) async-start(), calls=%async_computation.6 | async-start | bytes 4177920 | tf_op jit(solution)/shard_map/reduce_scatter | solution.py:120
  71.9 17.9 %collective-permute-start.3 = (bf16[48,2560]{1,0:T(8,128)(2,1)}, bf16[48,2560]{1,0:T(8,128)(2,1)}, u32[]{:S(2)}, u32[]{:S(2)}) collective-permute-start(bf16[48,2560]{1,0:T(8,128)(2,1)} %collective-permute-done.2), channel_id=1, source_target_pairs={{0,15},{1,0},{2,1},{3,2},{4,3},{5,4},{6,5},{7,6},{8,7},{9,8},{10,9... | collective-permute-start | bytes 737288 | tf_op jit(solution)/shard_map/ppermute | solution.py:39
  77.4 17.6 %collective-permute-start.10 = (bf16[48,2560]{1,0:T(8,128)(2,1)}, bf16[48,2560]{1,0:T(8,128)(2,1)}, u32[]{:S(2)}, u32[]{:S(2)}) collective-permute-start(bf16[48,2560]{1,0:T(8,128)(2,1)} %collective-permute-done.9), channel_id=1, source_target_pairs={{0,1},{1,2},{2,3},{3,4},{4,5},{5,6},{6,7},{7,8},{8,9},{9,10},{10,1... | collective-permute-start | bytes 737288 | tf_op jit(solution)/shard_map/ppermute | solution.py:38
  89.8 12.0 %collective-permute-start.4 = (bf16[48,2560]{1,0:T(8,128)(2,1)}, bf16[48,2560]{1,0:T(8,128)(2,1)S(1)}, u32[]{:S(2)}, u32[]{:S(2)}) collective-permute-start(bf16[48,2560]{1,0:T(8,128)(2,1)} %collective-permute-done.3), channel_id=1, source_target_pairs={{0,15},{1,0},{2,1},{3,2},{4,3},{5,4},{6,5},{7,6},{8,7},{9,8},{10,9... | collective-permute-start | bytes 737288 | tf_op jit(solution)/shard_map/ppermute | solution.py:39
  95.0 12.4 %collective-permute-start.11 = (bf16[48,2560]{1,0:T(8,128)(2,1)}, bf16[48,2560]{1,0:T(8,128)(2,1)S(1)}, u32[]{:S(2)}, u32[]{:S(2)}) collective-permute-start(bf16[48,2560]{1,0:T(8,128)(2,1)} %collective-permute-done.10), channel_id=1, source_target_pairs={{0,1},{1,2},{2,3},{3,4},{4,5},{5,6},{6,7},{7,8},{8,9},{9,10},{10,1... | collective-permute-start | bytes 737288 | tf_op jit(solution)/shard_map/ppermute | solution.py:38
  101.8 10.2 %collective-permute-start.5 = (bf16[48,2560]{1,0:T(8,128)(2,1)S(1)}, bf16[48,2560]{1,0:T(8,128)(2,1)S(1)}, u32[]{:S(2)}, u32[]{:S(2)}) collective-permute-start(bf16[48,2560]{1,0:T(8,128)(2,1)S(1)} %collective-permute-done.4), channel_id=1, source_target_pairs={{0,15},{1,0},{2,1},{3,2},{4,3},{5,4},{6,5},{7,6},{8,7},{9,8},{10,9... | collective-permute-start | bytes 737288 | tf_op jit(solution)/shard_map/ppermute | solution.py:39
  107.4 10.3 %collective-permute-start.12 = (bf16[48,2560]{1,0:T(8,128)(2,1)S(1)}, bf16[48,2560]{1,0:T(8,128)(2,1)S(1)}, u32[]{:S(2)}, u32[]{:S(2)}) collective-permute-start(bf16[48,2560]{1,0:T(8,128)(2,1)S(1)} %collective-permute-done.11), channel_id=1, source_target_pairs={{0,1},{1,2},{2,3},{3,4},{4,5},{5,6},{6,7},{7,8},{8,9},{9,10},{10,1... | collective-permute-start | bytes 737288 | tf_op jit(solution)/shard_map/ppermute | solution.py:38
  112.0 12.8 %collective-permute-start.6 = (bf16[48,2560]{1,0:T(8,128)(2,1)S(1)}, bf16[48,2560]{1,0:T(8,128)(2,1)S(1)}, u32[]{:S(2)}, u32[]{:S(2)}) collective-permute-start(bf16[48,2560]{1,0:T(8,128)(2,1)S(1)} %collective-permute-done.5), channel_id=1, source_target_pairs={{0,15},{1,0},{2,1},{3,2},{4,3},{5,4},{6,5},{7,6},{8,7},{9,8},{10,9... | collective-permute-start | bytes 737288 | tf_op jit(solution)/shard_map/ppermute | solution.py:39
  117.7 16.2 %collective-permute-start.13 = (bf16[48,2560]{1,0:T(8,128)(2,1)S(1)}, bf16[48,2560]{1,0:T(8,128)(2,1)S(1)}, u32[]{:S(2)}, u32[]{:S(2)}) collective-permute-start(bf16[48,2560]{1,0:T(8,128)(2,1)S(1)} %collective-permute-done.12), channel_id=1, source_target_pairs={{0,1},{1,2},{2,3},{3,4},{4,5},{5,6},{6,7},{7,8},{8,9},{9,10},{10,1... | collective-permute-start | bytes 737288 | tf_op jit(solution)/shard_map/ppermute | solution.py:38
  124.8 11.9 %collective-permute-start.15 = (bf16[48,1280]{1,0:T(8,128)(2,1)S(1)}, bf16[48,1280]{1,0:T(8,128)(2,1)S(1)}, u32[]{:S(2)}, u32[]{:S(2)}) collective-permute-start(bf16[48,1280]{1,0:T(8,128)(2,1)S(1)} %slice.21), channel_id=1, source_target_pairs={{0,15},{1,0},{2,1},{3,2},{4,3},{5,4},{6,5},{7,6},{8,7},{9,8},{10,9... | collective-permute-start | bytes 368648 | tf_op jit(solution)/shard_map/ppermute | solution.py:45
  133.9 10.1 %collective-permute-start.14 = (bf16[48,1280]{1,0:T(8,128)(2,1)S(1)}, bf16[48,1280]{1,0:T(8,128)(2,1)S(1)}, u32[]{:S(2)}, u32[]{:S(2)}) collective-permute-start(bf16[48,1280]{1,0:T(8,128)(2,1)S(1)} %slice.20), channel_id=1, source_target_pairs={{0,1},{1,2},{2,3},{3,4},{4,5},{5,6},{6,7},{7,8},{8,9},{9,10},{10,1... | collective-permute-start | bytes 368648 | tf_op jit(solution)/shard_map/ppermute | solution.py:44
  218.9 25.4 %all-to-all-start.2 = ((bf16[32,5,2560]{2,1,0:T(8,128)(2,1)}), bf16[32,5,2560]{2,1,0:T(8,128)(2,1)}, u32[]{:S(2)}, u32[]{:S(2)}) async-start(bf16[32,5,2560]{2,1,0:T(8,128)(2,1)} %reshape.138), calls=%async_computation.2 | async-start | bytes 2621440 | tf_op jit(solution)/shard_map/all_to_all | solution.py:100
  (21 other events, 167.4 us)
Sparse Core Ops, SparseCore 0:
  10.1 93.8 all-gather.4
  106.1 74.4 all-gather.2
  193.3 75.5 reduce-scatter.1

commit v4 on v0

--- a/solution.py
+++ b/solution.py
@@ -25,6 +25,31 @@
     return (hidden, input_grad)
 
 
+def ring_gather(pieces, axis):
+    n = lax.axis_size(axis)
+    idx = lax.axis_index(axis)
+    right = [(i, (i + 1) % n) for i in range(n)]
+    left = [(i, (i - 1) % n) for i in range(n)]
+    ahead = [{0: p} for p in pieces]
+    r, l = list(pieces), list(pieces)
+    half = n // 2
+    steps = half if n % 2 == 1 else half - 1
+    for k in range(1, steps + 1):
+        r = [lax.ppermute(p, axis, right) for p in r]
+        l = [lax.ppermute(p, axis, left) for p in l]
+        for a, rp, lp in zip(ahead, r, l):
+            a[n - k] = rp
+            a[k] = lp
+    if n % 2 == 0 and n > 1:
+        for a, rp, lp in zip(ahead, r, l):
+            cut = rp.shape[-1] // 2
+            rh = lax.ppermute(rp[..., :cut], axis, right)
+            lh = lax.ppermute(lp[..., cut:], axis, left)
+            a[half] = jnp.concatenate([rh, lh], axis=-1)
+    order = (jnp.arange(n, dtype=jnp.int32) - idx) % n
+    return [jnp.take(jnp.stack([a[m] for m in range(n)]), order, axis=0) for a in ahead]
+
+
 def local(tokens, cotangent, partner, combine, counts, w_gate, w_up, w_down):
     tok_rows = tokens.shape[0]
     width = tokens.shape[1]
@@ -39,14 +64,18 @@
     upstream = cotangent.astype(jnp.float32)
     q_home = (upstream * share_home[:, None]).astype(jnp.bfloat16)
     q_away = (upstream * share_away[:, None]).astype(jnp.bfloat16)
-    gate_full, up_full, down_full = (
+    split = w_up.shape[2] // 2
+    gate_full, up_first = (
         lax.all_gather(w_gate, "replica", axis=1, tiled=True),
-        lax.all_gather(w_up, "replica", axis=1, tiled=True),
-        lax.all_gather(w_down, "replica", axis=1, tiled=True),
+        lax.all_gather(w_up[..., :split], "replica", axis=1, tiled=True),
     )
+    down_full, up_second = ring_gather([w_down[0], w_up[0, :, split:]], "replica")
     gate_w = gate_full.reshape(gate_full.shape[1], gate_full.shape[2])
-    up_w = up_full.reshape(up_full.shape[1], up_full.shape[2])
-    down_w = down_full.reshape(down_full.shape[1], down_full.shape[2])
+    up_w = jnp.concatenate(
+        [up_first.reshape(up_first.shape[1], split), up_second.reshape(-1, w_up.shape[2] - split)],
+        axis=1,
+    )
+    down_w = down_full.reshape(-1, down_full.shape[2])
     target = partner[:, 0]
     onehot_rows = (target[:, None] == jnp.arange(expert_count, dtype=jnp.int32)[None, :]).astype(
         jnp.int32

time: 333 us -> 314 us (0.943)
  waiting for transfers between devices: 251 us -> 65.9 us
  starting transfers between devices: 23.7 us -> 140 us
  local copies, waits for them, and re-layouts: 8.85 us -> 51.9 us
  other arithmetic: 3.09 us -> 12.1 us
    all_gather x2 -> x1, waiting for transfers between devices: 139 us -> 0.01 us  [local(): lax.all_gather(w_up[..., :split], 'replica', axis=1, tiled=True)]
    ppermute x0 -> x32, starting transfers between devices: none -> 118 us  [the longest x14 73.6 us: ring_gather(): l = [lax.ppermute(p, axis, left) for p in l]]
    unnamed x24 -> x93, local copies, waits for them, and re-layouts: 1.68 us -> 32.6 us
    all_gather x1, waiting for transfers between devices: 22.6 us -> 0.01 us  [local(): lax.all_gather(w_gate, 'replica', axis=1, tiled=True)]
    reduce_scatter x1, waiting for transfers between devices: 42.9 us -> 22 us  [local(): lax.psum_scatter((lax.dot_general(hidden_home, q_home, contract, preferre...]
    ppermute x0 -> x32, waiting for transfers between devices: none -> 18 us  [the longest x2 10.5 us: ring_gather(): rh = lax.ppermute(rp[..., :cut], axis, right)]
    all_to_all x1, waiting for transfers between devices: 16.3 us -> 0.01 us  [local(): lax.all_to_all(send_q, 'expert', split_axis=0, concat_axis=0, tiled=True)]
    select_n x0 -> x4, other arithmetic: none -> 7.56 us  [ring_gather(): jnp.take(jnp.stack([a[m] for m in range(n)]), order, axis=0)]
  transfers between devices with their start and end apart: 7 -> 38, of which waited for: 7 -> 11; matrix products, arithmetic and copies ran while one was open for 12% -> 24% of each run, Pallas kernels for 0% -> 0%
where the time goes in v4:
time: 314 us; the launch traced here: 312 us
  starting transfers between devices  140 us (45%)
  waiting for transfers between devices  65.9 us (21%)
  local copies, waits for them, and re-layouts  51.9 us (17%)
  matrix products  27.7 us (9%)
  between operations  15.2 us (5%)
  other arithmetic  12.1 us (4%)
    ppermute x14, starting transfers between devices, ring_gather(): l = [lax.ppermute(p, axis, left) for p in l]  73.6 us
    unnamed x93, local copies, waits for them, and re-layouts  32.6 us
    ppermute x14, starting transfers between devices, ring_gather(): r = [lax.ppermute(p, axis, right) for p in r]  29.4 us
    reduce_scatter x1, waiting for transfers between devices, local(): lax.psum_scatter((lax.dot_general(hidden_home, q_home, contract, preferre...  22 us
    all_to_all x1, waiting for transfers between devices, local(): lax.all_to_all(send_x, 'expert', split_axis=0, concat_axis=0, tiled=True)  14.5 us
    ppermute x2, starting transfers between devices, ring_gather(): lh = lax.ppermute(lp[..., cut:], axis, left)  10.7 us
    dot_general x6, matrix products, against_rows(): lax.dot_general(left, matrix, (((1,), (1,)), ((), ())), preferred_element...  10.7 us
    all_to_all x1, waiting for transfers between devices, local(): lax.all_to_all(grad_there.astype(jnp.bfloat16).reshape(expert_count, item...  10.7 us
  transfers between devices with their start and end apart: 38, of which 11 were waited for; matrix products, arithmetic and copies ran while one was open for 24% of the time, Pallas kernels for 0%

profile of v4, /device:TPU:6, one launch (start us, length us, event | category | flops | bytes accessed | tf_op | source)
XLA Modules:
  0.0 312.4 jit_solution(6111199786200745196)
XLA Ops:
  9.1 11.4 %collective-permute-start = (bf16[48,2560]{1,0:T(8,128)(2,1)}, bf16[48,2560]{1,0:T(8,128)(2,1)S(1)}, u32[]{:S(2)}, u32[]{:S(2)}) collective-permute-start(bf16[48,2560]{1,0:T(8,128)(2,1)} %bitcast.112), channel_id=1, source_target_pairs={{0,15},{1,0},{2,1},{3,2},{4,3},{5,4},{6,5},{7,6},{8,7},{9,8},{10,9... | collective-permute-start | bytes 737288 | tf_op jit(solution)/shard_map/ppermute | solution.py:39
  22.4 5.1 %collective-permute-start.16 = (bf16[160,384]{1,0:T(8,128)(2,1)}, bf16[160,384]{1,0:T(8,128)(2,1)}, u32[]{:S(2)}, u32[]{:S(2)}) collective-permute-start(bf16[160,384]{1,0:T(8,128)(2,1)} %get-tuple-element.4), channel_id=1, source_target_pairs={{0,15},{1,0},{2,1},{3,2},{4,3},{5,4},{6,5},{7,6},{8,7},{9,8},{10,9... | collective-permute-start | bytes 368648 | tf_op jit(solution)/shard_map/ppermute | solution.py:39
  36.1 7.6 %all-to-all-start = ((bf16[32,5,2560]{2,1,0:T(8,128)(2,1)}), bf16[32,5,2560]{2,1,0:T(8,128)(2,1)S(1)}, u32[]{:S(2)}, u32[]{:S(2)}) async-start(bf16[32,5,2560]{2,1,0:T(8,128)(2,1)} %reshape.137), calls=%async_computation | async-start | bytes 2621440 | tf_op jit(solution)/shard_map/all_to_all | solution.py:100
  47.2 5.1 %collective-permute-start.17 = (bf16[160,384]{1,0:T(8,128)(2,1)}, bf16[160,384]{1,0:T(8,128)(2,1)S(1)}, u32[]{:S(2)}, u32[]{:S(2)}) collective-permute-start(bf16[160,384]{1,0:T(8,128)(2,1)} %collective-permute-done.16), channel_id=1, source_target_pairs={{0,15},{1,0},{2,1},{3,2},{4,3},{5,4},{6,5},{7,6},{8,7},{9,8},{10,9... | collective-permute-start | bytes 368648 | tf_op jit(solution)/shard_map/ppermute | solution.py:39
  55.8 5.1 %collective-permute-start.1 = (bf16[48,2560]{1,0:T(8,128)(2,1)S(1)}, bf16[48,2560]{1,0:T(8,128)(2,1)S(1)}, u32[]{:S(2)}, u32[]{:S(2)}) collective-permute-start(bf16[48,2560]{1,0:T(8,128)(2,1)S(1)} %collective-permute-done), channel_id=1, source_target_pairs={{0,15},{1,0},{2,1},{3,2},{4,3},{5,4},{6,5},{7,6},{8,7},{9,8},{10,9... | collective-permute-start | bytes 737288 | tf_op jit(solution)/shard_map/ppermute | solution.py:39
  63.6 5.1 %collective-permute-start.18 = (bf16[160,384]{1,0:T(8,128)(2,1)S(1)}, bf16[160,384]{1,0:T(8,128)(2,1)S(1)}, u32[]{:S(2)}, u32[]{:S(2)}) collective-permute-start(bf16[160,384]{1,0:T(8,128)(2,1)S(1)} %collective-permute-done.17), channel_id=1, source_target_pairs={{0,15},{1,0},{2,1},{3,2},{4,3},{5,4},{6,5},{7,6},{8,7},{9,8},{10,9... | collective-permute-start | bytes 368648 | tf_op jit(solution)/shard_map/ppermute | solution.py:39
  73.0 5.6 %collective-permute-start.19 = (bf16[160,384]{1,0:T(8,128)(2,1)S(1)}, bf16[160,384]{1,0:T(8,128)(2,1)S(1)}, u32[]{:S(2)}, u32[]{:S(2)}) collective-permute-start(bf16[160,384]{1,0:T(8,128)(2,1)S(1)} %collective-permute-done.18), channel_id=1, source_target_pairs={{0,15},{1,0},{2,1},{3,2},{4,3},{5,4},{6,5},{7,6},{8,7},{9,8},{10,9... | collective-permute-start | bytes 368648 | tf_op jit(solution)/shard_map/ppermute | solution.py:39
  82.0 5.1 %collective-permute-start.2 = (bf16[48,2560]{1,0:T(8,128)(2,1)S(1)}, bf16[48,2560]{1,0:T(8,128)(2,1)}, u32[]{:S(2)}, u32[]{:S(2)}) collective-permute-start(bf16[48,2560]{1,0:T(8,128)(2,1)S(1)} %collective-permute-done.1), channel_id=1, source_target_pairs={{0,15},{1,0},{2,1},{3,2},{4,3},{5,4},{6,5},{7,6},{8,7},{9,8},{10,9... | collective-permute-start | bytes 737288 | tf_op jit(solution)/shard_map/ppermute | solution.py:39
  89.8 5.1 %collective-permute-start.20 = (bf16[160,384]{1,0:T(8,128)(2,1)S(1)}, bf16[160,384]{1,0:T(8,128)(2,1)S(1)}, u32[]{:S(2)}, u32[]{:S(2)}) collective-permute-start(bf16[160,384]{1,0:T(8,128)(2,1)S(1)} %collective-permute-done.19), channel_id=1, source_target_pairs={{0,15},{1,0},{2,1},{3,2},{4,3},{5,4},{6,5},{7,6},{8,7},{9,8},{10,9... | collective-permute-start | bytes 368648 | tf_op jit(solution)/shard_map/ppermute | solution.py:39
  97.5 5.4 %collective-permute-start.21 = (bf16[160,384]{1,0:T(8,128)(2,1)S(1)}, bf16[160,384]{1,0:T(8,128)(2,1)}, u32[]{:S(2)}, u32[]{:S(2)}) collective-permute-start(bf16[160,384]{1,0:T(8,128)(2,1)S(1)} %collective-permute-done.20), channel_id=1, source_target_pairs={{0,15},{1,0},{2,1},{3,2},{4,3},{5,4},{6,5},{7,6},{8,7},{9,8},{10,9... | collective-permute-start | bytes 368648 | tf_op jit(solution)/shard_map/ppermute | solution.py:39
  105.5 5.1 %collective-permute-start.3 = (bf16[48,2560]{1,0:T(8,128)(2,1)}, bf16[48,2560]{1,0:T(8,128)(2,1)}, u32[]{:S(2)}, u32[]{:S(2)}) collective-permute-start(bf16[48,2560]{1,0:T(8,128)(2,1)} %collective-permute-done.2), channel_id=1, source_target_pairs={{0,15},{1,0},{2,1},{3,2},{4,3},{5,4},{6,5},{7,6},{8,7},{9,8},{10,9... | collective-permute-start | bytes 737288 | tf_op jit(solution)/shard_map/ppermute | solution.py:39
  112.6 5.1 %collective-permute-start.22 = (bf16[160,384]{1,0:T(8,128)(2,1)}, bf16[160,384]{1,0:T(8,128)(2,1)S(1)}, u32[]{:S(2)}, u32[]{:S(2)}) collective-permute-start(bf16[160,384]{1,0:T(8,128)(2,1)} %collective-permute-done.21), channel_id=1, source_target_pairs={{0,15},{1,0},{2,1},{3,2},{4,3},{5,4},{6,5},{7,6},{8,7},{9,8},{10,9... | collective-permute-start | bytes 368648 | tf_op jit(solution)/shard_map/ppermute | solution.py:39
  119.7 7.9 %all-to-all-start.1 = ((bf16[32,5,2560]{2,1,0:T(8,128)(2,1)}), bf16[32,5,2560]{2,1,0:T(8,128)(2,1)}, u32[]{:S(2)}, u32[]{:S(2)}) async-start(bf16[32,5,2560]{2,1,0:T(8,128)(2,1)} %reshape.139), calls=%async_computation.1 | async-start | bytes 2621440 | tf_op jit(solution)/shard_map/all_to_all | solution.py:99
  131.3 14.5 %all-to-all-done.1 = bf16[32,5,2560]{2,1,0:T(8,128)(2,1)} async-done(((bf16[32,5,2560]{2,1,0:T(8,128)(2,1)}), bf16[32,5,2560]{2,1,0:T(8,128)(2,1)}, u32[]{:S(2)}, u32[]{:S(2)}) %all-to-all-start.1) | async-done | bytes 819232 | tf_op jit(solution)/shard_map/all_to_all | solution.py:99
  148.1 5.1 %collective-permute-start.31 = (bf16[160,192]{1,0:T(8,128)(2,1)S(1)}, bf16[160,192]{1,0:T(8,128)(2,1)S(1)}, u32[]{:S(2)}, u32[]{:S(2)}) collective-permute-start(bf16[160,192]{1,0:T(8,128)(2,1)S(1)} %slice.41), channel_id=1, source_target_pairs={{0,15},{1,0},{2,1},{3,2},{4,3},{5,4},{6,5},{7,6},{8,7},{9,8},{10,9... | collective-permute-start | bytes 184328 | tf_op jit(solution)/shard_map/ppermute | solution.py:47
  156.5 5.4 %collective-permute-done.30 = bf16[160,192]{1,0:T(8,128)(2,1)S(1)} collective-permute-done((bf16[160,192]{1,0:T(8,128)(2,1)S(1)}, bf16[160,192]{1,0:T(8,128)(2,1)S(1)}, u32[]{:S(2)}, u32[]{:S(2)}) %collective-permute-start.30) | collective-permute-done | bytes 61472 | tf_op jit(solution)/shard_map/ppermute | solution.py:46
  177.6 3.9 %collective-permute-start.11 = (bf16[48,2560]{1,0:T(8,128)(2,1)}, bf16[48,2560]{1,0:T(8,128)(2,1)S(1)}, u32[]{:S(2)}, u32[]{:S(2)}) collective-permute-start(bf16[48,2560]{1,0:T(8,128)(2,1)} %collective-permute-done.10), channel_id=1, source_target_pairs={{0,1},{1,2},{2,3},{3,4},{4,5},{5,6},{6,7},{7,8},{8,9},{9,10},{10,1... | collective-permute-start | bytes 737288 | tf_op jit(solution)/shard_map/ppermute | solution.py:38
  193.1 4.9 %collective-permute-start.6 = (bf16[48,2560]{1,0:T(8,128)(2,1)S(1)}, bf16[48,2560]{1,0:T(8,128)(2,1)S(1)}, u32[]{:S(2)}, u32[]{:S(2)}) collective-permute-start(bf16[48,2560]{1,0:T(8,128)(2,1)S(1)} %collective-permute-done.5), channel_id=1, source_target_pairs={{0,15},{1,0},{2,1},{3,2},{4,3},{5,4},{6,5},{7,6},{8,7},{9,8},{10,9... | collective-permute-start | bytes 737288 | tf_op jit(solution)/shard_map/ppermute | solution.py:39
  201.7 5.6 %collective-permute-start.15 = (bf16[48,1280]{1,0:T(8,128)(2,1)S(1)}, bf16[48,1280]{1,0:T(8,128)(2,1)S(1)}, u32[]{:S(2)}, u32[]{:S(2)}) collective-permute-start(bf16[48,1280]{1,0:T(8,128)(2,1)S(1)} %slice.39), channel_id=1, source_target_pairs={{0,15},{1,0},{2,1},{3,2},{4,3},{5,4},{6,5},{7,6},{8,7},{9,8},{10,9... | collective-permute-start | bytes 368648 | tf_op jit(solution)/shard_map/ppermute | solution.py:47
  210.2 5.1 %collective-permute-done.14 = bf16[48,1280]{1,0:T(8,128)(2,1)S(1)} collective-permute-done((bf16[48,1280]{1,0:T(8,128)(2,1)S(1)}, bf16[48,1280]{1,0:T(8,128)(2,1)S(1)}, u32[]{:S(2)}, u32[]{:S(2)}) %collective-permute-start.14) | collective-permute-done | bytes 122912 | tf_op jit(solution)/shard_map/ppermute | solution.py:46
  238.5 4.8 %gather_fusion = bf16[16,48,2560]{2,1,0:T(8,128)(2,1)} fusion(bf16[16,48,2560]{2,1,0:T(8,128)(2,1)} %bitcast_dynamic-update-slice_fusion, s32[1024]{0:T(1024)S(1)} %pad_clamp_fusion), kind=kCustom, calls=%fused_computation | custom fusion | bytes 7864384 | tf_op jit(solution)/shard_map/jit(_take)/gather | solution.py:50
  256.0 6.3 %all-to-all-start.2 = ((bf16[32,5,2560]{2,1,0:T(8,128)(2,1)}), bf16[32,5,2560]{2,1,0:T(8,128)(2,1)S(1)}, u32[]{:S(2)}, u32[]{:S(2)}) async-start(bf16[32,5,2560]{2,1,0:T(8,128)(2,1)} %reshape.141), calls=%async_computation.2 | async-start | bytes 2621440 | tf_op jit(solution)/shard_map/all_to_all | solution.py:105
  269.7 10.7 %all-to-all-done.2 = bf16[32,5,2560]{2,1,0:T(8,128)(2,1)S(1)} async-done(((bf16[32,5,2560]{2,1,0:T(8,128)(2,1)}), bf16[32,5,2560]{2,1,0:T(8,128)(2,1)S(1)}, u32[]{:S(2)}, u32[]{:S(2)}) %all-to-all-start.2) | async-done | bytes 819232 | tf_op jit(solution)/shard_map/all_to_all | solution.py:105
  283.9 22.0 %reduce-scatter.2.cloned.1.call-done = bf16[48,2560]{1,0:T(8,128)(2,1)} async-done(((bf16[768,2560]{1,0:T(8,128)(2,1)}), bf16[48,2560]{1,0:T(8,128)(2,1)}) %reduce-scatter.2.cloned.1.call-update) | async-done | bytes 245776 | tf_op jit(solution)/shard_map/reduce_scatter | solution.py:125
  (196 shorter events, 130.2 us)
Async XLA Ops:
  7.2 210.3 %all-gather.3.cloned.1.call-start = ((), (), s32[]{:S(2)}) async-start(), calls=%async_computation.4 | async-start | bytes 2088960 | tf_op jit(solution)/shard_map/all_gather | solution.py:70
  9.1 46.7 %collective-permute-start = (bf16[48,2560]{1,0:T(8,128)(2,1)}, bf16[48,2560]{1,0:T(8,128)(2,1)S(1)}, u32[]{:S(2)}, u32[]{:S(2)}) collective-permute-start(bf16[48,2560]{1,0:T(8,128)(2,1)} %bitcast.112), channel_id=1, source_target_pairs={{0,15},{1,0},{2,1},{3,2},{4,3},{5,4},{6,5},{7,6},{8,7},{9,8},{10,9... | collective-permute-start | bytes 737288 | tf_op jit(solution)/shard_map/ppermute | solution.py:39
  20.5 41.2 %collective-permute-start.7 = (bf16[48,2560]{1,0:T(8,128)(2,1)}, bf16[48,2560]{1,0:T(8,128)(2,1)S(1)}, u32[]{:S(2)}, u32[]{:S(2)}) collective-permute-start(bf16[48,2560]{1,0:T(8,128)(2,1)} %bitcast.113), channel_id=1, source_target_pairs={{0,1},{1,2},{2,3},{3,4},{4,5},{5,6},{6,7},{7,8},{8,9},{9,10},{10,1... | collective-permute-start | bytes 737288 | tf_op jit(solution)/shard_map/ppermute | solution.py:38
  22.4 24.8 %collective-permute-start.16 = (bf16[160,384]{1,0:T(8,128)(2,1)}, bf16[160,384]{1,0:T(8,128)(2,1)}, u32[]{:S(2)}, u32[]{:S(2)}) collective-permute-start(bf16[160,384]{1,0:T(8,128)(2,1)} %get-tuple-element.4), channel_id=1, source_target_pairs={{0,15},{1,0},{2,1},{3,2},{4,3},{5,4},{6,5},{7,6},{8,7},{9,8},{10,9... | collective-permute-start | bytes 368648 | tf_op jit(solution)/shard_map/ppermute | solution.py:39
  27.6 24.8 %collective-permute-start.23 = (bf16[160,384]{1,0:T(8,128)(2,1)}, bf16[160,384]{1,0:T(8,128)(2,1)}, u32[]{:S(2)}, u32[]{:S(2)}) collective-permute-start(bf16[160,384]{1,0:T(8,128)(2,1)} %get-tuple-element.4), channel_id=1, source_target_pairs={{0,1},{1,2},{2,3},{3,4},{4,5},{5,6},{6,7},{7,8},{8,9},{9,10},{10,1... | collective-permute-start | bytes 368648 | tf_op jit(solution)/shard_map/ppermute | solution.py:38
  36.1 83.7 %all-to-all-start = ((bf16[32,5,2560]{2,1,0:T(8,128)(2,1)}), bf16[32,5,2560]{2,1,0:T(8,128)(2,1)S(1)}, u32[]{:S(2)}, u32[]{:S(2)}) async-start(bf16[32,5,2560]{2,1,0:T(8,128)(2,1)} %reshape.137), calls=%async_computation | async-start | bytes 2621440 | tf_op jit(solution)/shard_map/all_to_all | solution.py:100
  43.7 179.0 %all-gather.5.cloned.1.call-start = ((), (), s32[]{:S(2)}) async-start(), calls=%async_computation.5 | async-start | bytes 4177920 | tf_op jit(solution)/shard_map/all_gather | solution.py:69
  47.2 16.4 %collective-permute-start.17 = (bf16[160,384]{1,0:T(8,128)(2,1)}, bf16[160,384]{1,0:T(8,128)(2,1)S(1)}, u32[]{:S(2)}, u32[]{:S(2)}) collective-permute-start(bf16[160,384]{1,0:T(8,128)(2,1)} %collective-permute-done.16), channel_id=1, source_target_pairs={{0,15},{1,0},{2,1},{3,2},{4,3},{5,4},{6,5},{7,6},{8,7},{9,8},{10,9... | collective-permute-start | bytes 368648 | tf_op jit(solution)/shard_map/ppermute | solution.py:39
  52.3 16.4 %collective-permute-start.24 = (bf16[160,384]{1,0:T(8,128)(2,1)}, bf16[160,384]{1,0:T(8,128)(2,1)S(1)}, u32[]{:S(2)}, u32[]{:S(2)}) collective-permute-start(bf16[160,384]{1,0:T(8,128)(2,1)} %collective-permute-done.23), channel_id=1, source_target_pairs={{0,1},{1,2},{2,3},{3,4},{4,5},{5,6},{6,7},{7,8},{8,9},{9,10},{10,1... | collective-permute-start | bytes 368648 | tf_op jit(solution)/shard_map/ppermute | solution.py:38
  55.8 26.2 %collective-permute-start.1 = (bf16[48,2560]{1,0:T(8,128)(2,1)S(1)}, bf16[48,2560]{1,0:T(8,128)(2,1)S(1)}, u32[]{:S(2)}, u32[]{:S(2)}) collective-permute-start(bf16[48,2560]{1,0:T(8,128)(2,1)S(1)} %collective-permute-done), channel_id=1, source_target_pairs={{0,15},{1,0},{2,1},{3,2},{4,3},{5,4},{6,5},{7,6},{8,7},{9,8},{10,9... | collective-permute-start | bytes 737288 | tf_op jit(solution)/shard_map/ppermute | solution.py:39
  61.7 26.2 %collective-permute-start.8 = (bf16[48,2560]{1,0:T(8,128)(2,1)S(1)}, bf16[48,2560]{1,0:T(8,128)(2,1)S(1)}, u32[]{:S(2)}, u32[]{:S(2)}) collective-permute-start(bf16[48,2560]{1,0:T(8,128)(2,1)S(1)} %collective-permute-done.7), channel_id=1, source_target_pairs={{0,1},{1,2},{2,3},{3,4},{4,5},{5,6},{6,7},{7,8},{8,9},{9,10},{10,1... | collective-permute-start | bytes 737288 | tf_op jit(solution)/shard_map/ppermute | solution.py:38
  73.0 16.8 %collective-permute-start.19 = (bf16[160,384]{1,0:T(8,128)(2,1)S(1)}, bf16[160,384]{1,0:T(8,128)(2,1)S(1)}, u32[]{:S(2)}, u32[]{:S(2)}) collective-permute-start(bf16[160,384]{1,0:T(8,128)(2,1)S(1)} %collective-permute-done.18), channel_id=1, source_target_pairs={{0,15},{1,0},{2,1},{3,2},{4,3},{5,4},{6,5},{7,6},{8,7},{9,8},{10,9... | collective-permute-start | bytes 368648 | tf_op jit(solution)/shard_map/ppermute | solution.py:39
  79.4 15.5 %collective-permute-start.26 = (bf16[160,384]{1,0:T(8,128)(2,1)S(1)}, bf16[160,384]{1,0:T(8,128)(2,1)S(1)}, u32[]{:S(2)}, u32[]{:S(2)}) collective-permute-start(bf16[160,384]{1,0:T(8,128)(2,1)S(1)} %collective-permute-done.25), channel_id=1, source_target_pairs={{0,1},{1,2},{2,3},{3,4},{4,5},{5,6},{6,7},{7,8},{8,9},{9,10},{10,1... | collective-permute-start | bytes 368648 | tf_op jit(solution)/shard_map/ppermute | solution.py:38
  82.0 23.5 %collective-permute-start.2 = (bf16[48,2560]{1,0:T(8,128)(2,1)S(1)}, bf16[48,2560]{1,0:T(8,128)(2,1)}, u32[]{:S(2)}, u32[]{:S(2)}) collective-permute-start(bf16[48,2560]{1,0:T(8,128)(2,1)S(1)} %collective-permute-done.1), channel_id=1, source_target_pairs={{0,15},{1,0},{2,1},{3,2},{4,3},{5,4},{6,5},{7,6},{8,7},{9,8},{10,9... | collective-permute-start | bytes 737288 | tf_op jit(solution)/shard_map/ppermute | solution.py:39
  87.8 22.8 %collective-permute-start.9 = (bf16[48,2560]{1,0:T(8,128)(2,1)S(1)}, bf16[48,2560]{1,0:T(8,128)(2,1)}, u32[]{:S(2)}, u32[]{:S(2)}) collective-permute-start(bf16[48,2560]{1,0:T(8,128)(2,1)S(1)} %collective-permute-done.8), channel_id=1, source_target_pairs={{0,1},{1,2},{2,3},{3,4},{4,5},{5,6},{6,7},{7,8},{8,9},{9,10},{10,1... | collective-permute-start | bytes 737288 | tf_op jit(solution)/shard_map/ppermute | solution.py:38
  97.5 15.1 %collective-permute-start.21 = (bf16[160,384]{1,0:T(8,128)(2,1)S(1)}, bf16[160,384]{1,0:T(8,128)(2,1)}, u32[]{:S(2)}, u32[]{:S(2)}) collective-permute-start(bf16[160,384]{1,0:T(8,128)(2,1)S(1)} %collective-permute-done.20), channel_id=1, source_target_pairs={{0,15},{1,0},{2,1},{3,2},{4,3},{5,4},{6,5},{7,6},{8,7},{9,8},{10,9... | collective-permute-start | bytes 368648 | tf_op jit(solution)/shard_map/ppermute | solution.py:39
  102.9 14.8 %collective-permute-start.28 = (bf16[160,384]{1,0:T(8,128)(2,1)S(1)}, bf16[160,384]{1,0:T(8,128)(2,1)}, u32[]{:S(2)}, u32[]{:S(2)}) collective-permute-start(bf16[160,384]{1,0:T(8,128)(2,1)S(1)} %collective-permute-done.27), channel_id=1, source_target_pairs={{0,1},{1,2},{2,3},{3,4},{4,5},{5,6},{6,7},{7,8},{8,9},{9,10},{10,1... | collective-permute-start | bytes 368648 | tf_op jit(solution)/shard_map/ppermute | solution.py:38
  105.5 70.1 %collective-permute-start.3 = (bf16[48,2560]{1,0:T(8,128)(2,1)}, bf16[48,2560]{1,0:T(8,128)(2,1)}, u32[]{:S(2)}, u32[]{:S(2)}) collective-permute-start(bf16[48,2560]{1,0:T(8,128)(2,1)} %collective-permute-done.2), channel_id=1, source_target_pairs={{0,15},{1,0},{2,1},{3,2},{4,3},{5,4},{6,5},{7,6},{8,7},{9,8},{10,9... | collective-permute-start | bytes 737288 | tf_op jit(solution)/shard_map/ppermute | solution.py:39
  110.7 66.9 %collective-permute-start.10 = (bf16[48,2560]{1,0:T(8,128)(2,1)}, bf16[48,2560]{1,0:T(8,128)(2,1)}, u32[]{:S(2)}, u32[]{:S(2)}) collective-permute-start(bf16[48,2560]{1,0:T(8,128)(2,1)} %collective-permute-done.9), channel_id=1, source_target_pairs={{0,1},{1,2},{2,3},{3,4},{4,5},{5,6},{6,7},{7,8},{8,9},{9,10},{10,1... | collective-permute-start | bytes 737288 | tf_op jit(solution)/shard_map/ppermute | solution.py:38
  112.6 35.4 %collective-permute-start.22 = (bf16[160,384]{1,0:T(8,128)(2,1)}, bf16[160,384]{1,0:T(8,128)(2,1)S(1)}, u32[]{:S(2)}, u32[]{:S(2)}) collective-permute-start(bf16[160,384]{1,0:T(8,128)(2,1)} %collective-permute-done.21), channel_id=1, source_target_pairs={{0,15},{1,0},{2,1},{3,2},{4,3},{5,4},{6,5},{7,6},{8,7},{9,8},{10,9... | collective-permute-start | bytes 368648 | tf_op jit(solution)/shard_map/ppermute | solution.py:39
  117.8 35.4 %collective-permute-start.29 = (bf16[160,384]{1,0:T(8,128)(2,1)}, bf16[160,384]{1,0:T(8,128)(2,1)S(1)}, u32[]{:S(2)}, u32[]{:S(2)}) collective-permute-start(bf16[160,384]{1,0:T(8,128)(2,1)} %collective-permute-done.28), channel_id=1, source_target_pairs={{0,1},{1,2},{2,3},{3,4},{4,5},{5,6},{6,7},{7,8},{8,9},{9,10},{10,1... | collective-permute-start | bytes 368648 | tf_op jit(solution)/shard_map/ppermute | solution.py:38
  119.7 26.0 %all-to-all-start.1 = ((bf16[32,5,2560]{2,1,0:T(8,128)(2,1)}), bf16[32,5,2560]{2,1,0:T(8,128)(2,1)}, u32[]{:S(2)}, u32[]{:S(2)}) async-start(bf16[32,5,2560]{2,1,0:T(8,128)(2,1)} %reshape.139), calls=%async_computation.1 | async-start | bytes 2621440 | tf_op jit(solution)/shard_map/all_to_all | solution.py:99
  127.6 178.2 %reduce-scatter.2.cloned.1.call-start = ((), (), s32[]{:S(2)}) async-start(), calls=%async_computation.6 | async-start | bytes 4177920 | tf_op jit(solution)/shard_map/reduce_scatter | solution.py:125
  256.0 24.4 %all-to-all-start.2 = ((bf16[32,5,2560]{2,1,0:T(8,128)(2,1)}), bf16[32,5,2560]{2,1,0:T(8,128)(2,1)S(1)}, u32[]{:S(2)}, u32[]{:S(2)}) async-start(bf16[32,5,2560]{2,1,0:T(8,128)(2,1)} %reshape.141), calls=%async_computation.2 | async-start | bytes 2621440 | tf_op jit(solution)/shard_map/all_to_all | solution.py:105
  (47 other events, 644.4 us)
Sparse Core Ops, SparseCore 0:
  10.7 78.6 all-gather.2
  91.4 78.5 all-gather.4
  232.2 73.6 reduce-scatter.1

commit v5 on v0

--- a/solution.py
+++ b/solution.py
@@ -39,14 +39,12 @@
     upstream = cotangent.astype(jnp.float32)
     q_home = (upstream * share_home[:, None]).astype(jnp.bfloat16)
     q_away = (upstream * share_away[:, None]).astype(jnp.bfloat16)
-    gate_full, up_full, down_full = (
-        lax.all_gather(w_gate, "replica", axis=1, tiled=True),
-        lax.all_gather(w_up, "replica", axis=1, tiled=True),
-        lax.all_gather(w_down, "replica", axis=1, tiled=True),
-    )
-    gate_w = gate_full.reshape(gate_full.shape[1], gate_full.shape[2])
-    up_w = up_full.reshape(up_full.shape[1], up_full.shape[2])
-    down_w = down_full.reshape(down_full.shape[1], down_full.shape[2])
+    shard_rows, hidden_units = w_gate.shape[1], w_gate.shape[2]
+    stacked = jnp.stack([w_gate[0], w_up[0], w_down[0].reshape(shard_rows, hidden_units)])
+    full = lax.all_gather(stacked, "replica", axis=0, tiled=False)
+    gate_w = full[:, 0].reshape(-1, hidden_units)
+    up_w = full[:, 1].reshape(-1, hidden_units)
+    down_w = full[:, 2].reshape(-1, w_down.shape[1], w_down.shape[2]).reshape(-1, w_down.shape[2])
     target = partner[:, 0]
     onehot_rows = (target[:, None] == jnp.arange(expert_count, dtype=jnp.int32)[None, :]).astype(
         jnp.int32

time: 333 us -> 256 us (0.77)
  waiting for transfers between devices: 251 us -> 161 us
  local copies, waits for them, and re-layouts: 8.85 us -> 27.6 us
  matrix products: 30.2 us -> 23.3 us
    all_gather x3 -> x1, waiting for transfers between devices: 161 us -> 87 us  [local(): full = lax.all_gather(stacked, 'replica', axis=0, tiled=False)]
    reduce_scatter x1, waiting for transfers between devices: 42.9 us -> 31.2 us  [local(): lax.psum_scatter((lax.dot_general(hidden_home, q_home, contract, preferre...]
    another operation x0 -> x2, local copies, waits for them, and re-layouts: none -> 9.32 us  [the longest x1 8.02 us: local(): full[:, 2].reshape(-1, w_down.shape[1], w_down.shape[2])]
    slice x0 -> x1, local copies, waits for them, and re-layouts: none -> 6.64 us  [local(): up_w = full[:, 1].reshape(-1, hidden_units)]
    dot_general x2, matrix products: 5.84 us -> 1.48 us  [expert_backward(): gate_act = jnp.dot(inputs, gate_w, preferred_element_type=jnp.float32)]
  transfers between devices with their start and end apart: 7 -> 5, of which waited for: 7 -> 5; matrix products, arithmetic and copies ran while one was open for 12% -> 14% of each run, Pallas kernels for 0% -> 0%
where the time goes in v5:
time: 256 us; the launch traced here: 255 us
  waiting for transfers between devices  161 us (63%)
  local copies, waits for them, and re-layouts  27.6 us (11%)
  starting transfers between devices  23.7 us (9%)
  matrix products  23.3 us (9%)
  between operations  15 us (6%)
  other arithmetic  4.51 us (2%)
    all_gather x1, waiting for transfers between devices, local(): full = lax.all_gather(stacked, 'replica', axis=0, tiled=False)  87 us
    reduce_scatter x1, waiting for transfers between devices, local(): lax.psum_scatter((lax.dot_general(hidden_home, q_home, contract, preferre...  31.2 us
    all_to_all x1, waiting for transfers between devices, local(): lax.all_to_all(send_q, 'expert', split_axis=0, concat_axis=0, tiled=True)  16.3 us
    all_to_all x1, waiting for transfers between devices, local(): lax.all_to_all(send_x, 'expert', split_axis=0, concat_axis=0, tiled=True)  15.5 us
    dot_general x6, matrix products, against_rows(): lax.dot_general(left, matrix, (((1,), (1,)), ((), ())), preferred_element...  13.9 us
    all_to_all x1, waiting for transfers between devices, local(): lax.all_to_all(grad_there.astype(jnp.bfloat16).reshape(expert_count, item...  10.9 us
    all_to_all x1, starting transfers between devices, local(): lax.all_to_all(send_x, 'expert', split_axis=0, concat_axis=0, tiled=True)  9.58 us
    another operation x1, local copies, waits for them, and re-layouts, local(): full[:, 2].reshape(-1, w_down.shape[1], w_down.shape[2])  8.02 us
  transfers between devices with their start and end apart: 5, of which 5 were waited for; matrix products, arithmetic and copies ran while one was open for 14% of the time, Pallas kernels for 0%

profile of v5, /device:TPU:6, one launch (start us, length us, event | category | flops | bytes accessed | tf_op | source)
XLA Modules:
  0.0 255.2 jit_solution(11991757183906421600)
XLA Ops:
  7.2 1.3 stack_reshape_squeeze.3
  8.5 2.0 pad_maximum_fusion
  14.7 9.6 %all-to-all-start.1 = ((bf16[32,5,2560]{2,1,0:T(8,128)(2,1)}), bf16[32,5,2560]{2,1,0:T(8,128)(2,1)S(1)}, u32[]{:S(2)}, u32[]{:S(2)}) async-start(bf16[32,5,2560]{2,1,0:T(8,128)(2,1)} %reshape.41), calls=%async_computation.1 | async-start | bytes 2621440 | tf_op jit(solution)/shard_map/all_to_all | solution.py:68
  25.4 1.3 reshape.39
  26.7 15.5 %all-to-all-done.1 = bf16[32,5,2560]{2,1,0:T(8,128)(2,1)S(1)} async-done(((bf16[32,5,2560]{2,1,0:T(8,128)(2,1)}), bf16[32,5,2560]{2,1,0:T(8,128)(2,1)S(1)}, u32[]{:S(2)}, u32[]{:S(2)}) %all-to-all-start.1) | async-done | bytes 819232 | tf_op jit(solution)/shard_map/all_to_all | solution.py:68
  42.3 6.4 %all-to-all-start = ((bf16[32,5,2560]{2,1,0:T(8,128)(2,1)}), bf16[32,5,2560]{2,1,0:T(8,128)(2,1)}, u32[]{:S(2)}, u32[]{:S(2)}) async-start(bf16[32,5,2560]{2,1,0:T(8,128)(2,1)} %reshape.39), calls=%async_computation | async-start | bytes 2621440 | tf_op jit(solution)/shard_map/all_to_all | solution.py:69
  48.9 1.5 reshape.42
  50.4 16.3 %all-to-all-done = bf16[32,5,2560]{2,1,0:T(8,128)(2,1)} async-done(((bf16[32,5,2560]{2,1,0:T(8,128)(2,1)}), bf16[32,5,2560]{2,1,0:T(8,128)(2,1)}, u32[]{:S(2)}, u32[]{:S(2)}) %all-to-all-start) | async-done | bytes 819232 | tf_op jit(solution)/shard_map/all_to_all | solution.py:69
  66.7 1.5 reshape.40
  68.2 87.0 %all-gather.3.cloned.1.call-done = bf16[48,160,768]{2,1,0:T(8,128)(2,1)} async-done(((bf16[3,160,768]{2,1,0:T(8,128)(2,1)}), bf16[48,160,768]{2,1,0:T(8,128)(2,1)}) %all-gather.3.cloned.1.call-update) | async-done | bytes 11796496 | tf_op jit(solution)/shard_map/all_gather | solution.py:44
  155.3 6.6 %fusion.32 = (bf16[16,1,160,768]{3,2,1,0:T(8,128)(2,1)S(1)}, bf16[16,1,160,768]{3,2,1,0:T(8,128)(2,1)S(1)}, bf16[16,1,160,768]{3,2,1,0:T(8,128)(2,1)}) fusion(bf16[16,3,160,768]{3,2,1,0:T(8,128)(2,1)} %bitcast.44), kind=kLoop, calls=%fused_computation.52 | loop fusion | bytes 23592960 | tf_op jit(solution)/shard_map/slice | solution.py:46
  167.0 3.1 %add_convert_fusion = bf16[768,2560]{1,0:T(8,128)(2,1)} fusion(f32[768,2560]{1,0:T(8,128)S(1)} %fusion.8, bf16[160,2560]{1,0:T(8,128)(2,1)S(1)} %reshape.40, f32[160,768]{1,0:T(8,128)S(1)} %fusion.34, f32[160,768]{1,0:T(8,128)S(1)} %fusion.35), kind=kOutput, calls=%fused_computation | convolution fusion | flops 633815040 | bytes 13598720 | tf_op jit(solution)/shard_map/dot_general | solution.py:97
  170.2 8.0 %reshape_reshape_squeeze.3 = bf16[768,2560]{1,0:T(8,128)(2,1)} reshape(bf16[16,1,160,768]{3,2,1,0:T(8,128)(2,1)} %get-tuple-element.4) | data formatting | bytes 7864320 | tf_op jit(solution)/shard_map/reshape;reshape;squeeze | solution.py:47
  178.2 3.7 %fusion.33 = f32[160,768]{1,0:T(8,128)S(1)} fusion(bf16[160,2560]{1,0:T(8,128)(2,1)S(1)} %reshape.40, bf16[768,2560]{1,0:T(8,128)(2,1)} %reshape_reshape_squeeze.3), kind=kOutput, calls=%fused_computation.53 | convolution fusion | flops 629145600 | bytes 5242880 | tf_op jit(solution)/shard_map/dot_general | solution.py:8
  181.9 1.4 fusion.12
  184.0 2.3 fusion
  186.3 2.4 reshape.43
  188.7 7.5 %all-to-all-start.2 = ((bf16[32,5,2560]{2,1,0:T(8,128)(2,1)}), bf16[32,5,2560]{2,1,0:T(8,128)(2,1)}, u32[]{:S(2)}, u32[]{:S(2)}) async-start(bf16[32,5,2560]{2,1,0:T(8,128)(2,1)} %reshape.43), calls=%async_computation.2 | async-start | bytes 2621440 | tf_op jit(solution)/shard_map/all_to_all | solution.py:74
  196.2 3.7 %fusion.10 = f32[128,768]{1,0:T(8,128)S(1)} fusion(bf16[768,2560]{1,0:T(8,128)(2,1)} %reshape_reshape_squeeze.3, bf16[128,2560]{1,0:T(8,128)(2,1)S(1)} %copy-done.9, f32[128]{0:T(128)S(1)} %get-tuple-element.6), kind=kOutput, calls=%fused_computation.27 | convolution fusion | flops 504299520 | bytes 4981248 | tf_op jit(solution)/shard_map/dot_general | solution.py:8
  199.9 1.4 fusion.14
  202.1 1.4 convolution_add_fusion.2
  203.5 10.9 %all-to-all-done.2 = bf16[32,5,2560]{2,1,0:T(8,128)(2,1)} async-done(((bf16[32,5,2560]{2,1,0:T(8,128)(2,1)}), bf16[32,5,2560]{2,1,0:T(8,128)(2,1)}, u32[]{:S(2)}, u32[]{:S(2)}) %all-to-all-start.2) | async-done | bytes 819232 | tf_op jit(solution)/shard_map/all_to_all | solution.py:74
  214.4 1.5 reshape.44
  217.1 31.2 %reduce-scatter.2.cloned.1.call-done = bf16[48,2560]{1,0:T(8,128)(2,1)} async-done(((bf16[768,2560]{1,0:T(8,128)(2,1)}), bf16[48,2560]{1,0:T(8,128)(2,1)}) %reduce-scatter.2.cloned.1.call-update) | async-done | bytes 245776 | tf_op jit(solution)/shard_map/reduce_scatter | solution.py:94
  (47 shorter events, 12.5 us)
Async XLA Ops:
  7.2 5.9 %copy-start = (bf16[128,2560]{1,0:T(8,128)(2,1)S(1)}, bf16[128,2560]{1,0:T(8,128)(2,1)}, u32[]{:S(2)}) copy-start(bf16[128,2560]{1,0:T(8,128)(2,1)} %param.8) | copy-start | bytes 1966084
  7.2 148.1 %all-gather.3.cloned.1.call-start = ((), (), s32[]{:S(2)}) async-start(), calls=%async_computation.5 | async-start | bytes 12533760 | tf_op jit(solution)/shard_map/all_gather | solution.py:44
  10.6 13.7 %copy-start.13 = (s32[128,2]{0,1:T(2,128)S(1)}, s32[128,2]{0,1:T(2,128)}, u32[]{:S(2)}) copy-start(s32[128,2]{0,1:T(2,128)} %param.11) | copy-start | bytes 3076
  10.6 14.4 %copy-start.7 = (bf16[128,2560]{1,0:T(8,128)(2,1)S(1)}, bf16[128,2560]{1,0:T(8,128)(2,1)}, u32[]{:S(2)}) copy-start(bf16[128,2560]{1,0:T(8,128)(2,1)} %param.9) | copy-start | bytes 1966084
  14.7 27.6 %all-to-all-start.1 = ((bf16[32,5,2560]{2,1,0:T(8,128)(2,1)}), bf16[32,5,2560]{2,1,0:T(8,128)(2,1)S(1)}, u32[]{:S(2)}, u32[]{:S(2)}) async-start(bf16[32,5,2560]{2,1,0:T(8,128)(2,1)} %reshape.41), calls=%async_computation.1 | async-start | bytes 2621440 | tf_op jit(solution)/shard_map/all_to_all | solution.py:68
  42.3 6.4 %copy-start.10 = (bf16[32,5,2560]{2,1,0:T(8,128)(2,1)}, bf16[32,5,2560]{2,1,0:T(8,128)(2,1)S(1)}, u32[]{:S(2)}) copy-start(bf16[32,5,2560]{2,1,0:T(8,128)(2,1)S(1)} %all-to-all-done.1) | copy-start | bytes 2457604
  42.3 24.4 %all-to-all-start = ((bf16[32,5,2560]{2,1,0:T(8,128)(2,1)}), bf16[32,5,2560]{2,1,0:T(8,128)(2,1)}, u32[]{:S(2)}, u32[]{:S(2)}) async-start(bf16[32,5,2560]{2,1,0:T(8,128)(2,1)} %reshape.39), calls=%async_computation | async-start | bytes 2621440 | tf_op jit(solution)/shard_map/all_to_all | solution.py:69
  48.7 199.7 %reduce-scatter.2.cloned.1.call-start = ((), (), s32[]{:S(2)}) async-start(), calls=%async_computation.4 | async-start | bytes 4177920 | tf_op jit(solution)/shard_map/reduce_scatter | solution.py:94
  161.9 1.9 copy-start.4
  161.9 3.1 %copy-start.1 = (bf16[16,1,160,768]{3,2,1,0:T(8,128)(2,1)}, bf16[16,1,160,768]{3,2,1,0:T(8,128)(2,1)S(1)}, u32[]{:S(2)}) copy-start(bf16[16,1,160,768]{3,2,1,0:T(8,128)(2,1)S(1)} %get-tuple-element.2) | copy-start | bytes 11796484
  163.8 2.0 copy-start.8
  165.0 2.0 copy-start.11
  178.2 3.7 %copy-start.5 = (bf16[16,1,160,768]{3,2,1,0:T(8,128)(2,1)S(1)}, bf16[16,1,160,768]{3,2,1,0:T(8,128)(2,1)}, u32[]{:S(2)}) copy-start(bf16[16,1,160,768]{3,2,1,0:T(8,128)(2,1)} %copy-done.4) | copy-start | bytes 11796484
  178.2 3.7 %copy-start.12 = (f32[160,768]{1,0:T(8,128)S(1)}, f32[160,768]{1,0:T(8,128)}, u32[]{:S(2)}) copy-start(f32[160,768]{1,0:T(8,128)} %copy-done.11) | copy-start | bytes 1474564
  181.9 2.1 copy-start.2
  186.3 9.9 %copy-start.9 = (bf16[128,2560]{1,0:T(8,128)(2,1)S(1)}, bf16[128,2560]{1,0:T(8,128)(2,1)}, u32[]{:S(2)}) copy-start(bf16[128,2560]{1,0:T(8,128)(2,1)} %param.9) | copy-start | bytes 1966084
  188.7 25.7 %all-to-all-start.2 = ((bf16[32,5,2560]{2,1,0:T(8,128)(2,1)}), bf16[32,5,2560]{2,1,0:T(8,128)(2,1)}, u32[]{:S(2)}, u32[]{:S(2)}) async-start(bf16[32,5,2560]{2,1,0:T(8,128)(2,1)} %reshape.43), calls=%async_computation.2 | async-start | bytes 2621440 | tf_op jit(solution)/shard_map/all_to_all | solution.py:74
  196.2 3.7 %copy-start.6 = (bf16[16,1,160,768]{3,2,1,0:T(8,128)(2,1)S(1)}, bf16[16,1,160,768]{3,2,1,0:T(8,128)(2,1)}, u32[]{:S(2)}) copy-start(bf16[16,1,160,768]{3,2,1,0:T(8,128)(2,1)} %copy-done.4) | copy-start | bytes 11796484
  199.9 2.2 copy-start.3
Sparse Core Ops, SparseCore 0:
  10.7 144.5 all-gather.2
  170.3 77.9 reduce-scatter.1

commit v6 on v3

--- a/solution.py
+++ b/solution.py
@@ -63,13 +63,10 @@
     upstream = cotangent.astype(jnp.float32)
     q_home = (upstream * share_home[:, None]).astype(jnp.bfloat16)
     q_away = (upstream * share_away[:, None]).astype(jnp.bfloat16)
-    gate_full, up_full = (
-        lax.all_gather(w_gate, "replica", axis=1, tiled=True),
-        lax.all_gather(w_up, "replica", axis=1, tiled=True),
-    )
+    pair = lax.all_gather(jnp.stack([w_gate[0], w_up[0]]), "replica", axis=0, tiled=False)
     down_full = ring_gather(w_down[0], "replica")
-    gate_w = gate_full.reshape(gate_full.shape[1], gate_full.shape[2])
-    up_w = up_full.reshape(up_full.shape[1], up_full.shape[2])
+    gate_w = pair[:, 0].reshape(-1, w_gate.shape[2])
+    up_w = pair[:, 1].reshape(-1, w_up.shape[2])
     down_w = down_full.reshape(-1, down_full.shape[2])
     target = partner[:, 0]
     onehot_rows = (target[:, None] == jnp.arange(expert_count, dtype=jnp.int32)[None, :]).astype(

time: 277 us -> 250 us (0.903)
  waiting for transfers between devices: 102 us -> 81 us
  matrix products: 27 us -> 21 us
    all_gather x2 -> x1, waiting for transfers between devices: 31.7 us -> 0.01 us  [local(): lax.all_gather(jnp.stack([w_gate[0], w_up[0]]), 'replica', axis=0, tiled=...]
    ppermute x7, waiting for transfers between devices: 17.3 us -> 33.3 us  [ring_gather(): l = lax.ppermute(l, axis, left)]
    unnamed x60, local copies, waits for them, and re-layouts: 21.9 us -> 17.4 us
    slice x0 -> x1, local copies, waits for them, and re-layouts: none -> 3.77 us  [local(): up_w = pair[:, 1].reshape(-1, w_up.shape[2])]
    ppermute x7, waiting for transfers between devices: 3.45 us -> 0.07 us  [ring_gather(): r = lax.ppermute(r, axis, right)]
  transfers between devices with their start and end apart: 22 -> 21, of which waited for: 10 -> 9; matrix products, arithmetic and copies ran while one was open for 20% -> 20% of each run, Pallas kernels for 0% -> 0%
where the time goes in v6:
time: 250 us; the launch traced here: 248 us
  starting transfers between devices  86.7 us (35%)
  waiting for transfers between devices  81 us (32%)
  local copies, waits for them, and re-layouts  36 us (14%)
  matrix products  21 us (8%)
  between operations  15.3 us (6%)
  other arithmetic  8.11 us (3%)
    ppermute x7, starting transfers between devices, ring_gather(): l = lax.ppermute(l, axis, left)  43.9 us
    ppermute x7, waiting for transfers between devices, ring_gather(): l = lax.ppermute(l, axis, left)  33.3 us
    reduce_scatter x1, waiting for transfers between devices, local(): lax.psum_scatter((lax.dot_general(hidden_home, q_home, contract, preferre...  23.9 us
    unnamed x60, local copies, waits for them, and re-layouts  17.4 us
    ppermute x7, starting transfers between devices, ring_gather(): r = lax.ppermute(r, axis, right)  13.4 us
    all_to_all x1, waiting for transfers between devices, local(): lax.all_to_all(grad_there.astype(jnp.bfloat16).reshape(expert_count, item...  12.9 us
    dot_general x6, matrix products, against_rows(): lax.dot_general(left, matrix, (((1,), (1,)), ((), ())), preferred_element...  11.6 us
    all_to_all x1, starting transfers between devices, local(): lax.all_to_all(send_x, 'expert', split_axis=0, concat_axis=0, tiled=True)  7.61 us
  transfers between devices with their start and end apart: 21, of which 9 were waited for; matrix products, arithmetic and copies ran while one was open for 20% of the time, Pallas kernels for 0%

profile of v6, /device:TPU:6, one launch (start us, length us, event | category | flops | bytes accessed | tf_op | source)
XLA Modules:
  0.0 248.2 jit_solution(122268542665340448)
XLA Ops:
  9.2 11.4 %collective-permute-start = (bf16[48,2560]{1,0:T(8,128)(2,1)}, bf16[48,2560]{1,0:T(8,128)(2,1)}, u32[]{:S(2)}, u32[]{:S(2)}) collective-permute-start(bf16[48,2560]{1,0:T(8,128)(2,1)} %bitcast.82), channel_id=1, source_target_pairs={{0,15},{1,0},{2,1},{3,2},{4,3},{5,4},{6,5},{7,6},{8,7},{9,8},{10,9... | collective-permute-start | bytes 737288 | tf_op jit(solution)/shard_map/ppermute | solution.py:39
  26.6 7.6 %all-to-all-start.1 = ((bf16[32,5,2560]{2,1,0:T(8,128)(2,1)}), bf16[32,5,2560]{2,1,0:T(8,128)(2,1)S(1)}, u32[]{:S(2)}, u32[]{:S(2)}) async-start(bf16[32,5,2560]{2,1,0:T(8,128)(2,1)} %reshape.128), calls=%async_computation.1 | async-start | bytes 2621440 | tf_op jit(solution)/shard_map/all_to_all | solution.py:91
  38.6 5.1 %collective-permute-start.1 = (bf16[48,2560]{1,0:T(8,128)(2,1)}, bf16[48,2560]{1,0:T(8,128)(2,1)S(1)}, u32[]{:S(2)}, u32[]{:S(2)}) collective-permute-start(bf16[48,2560]{1,0:T(8,128)(2,1)} %collective-permute-done), channel_id=1, source_target_pairs={{0,15},{1,0},{2,1},{3,2},{4,3},{5,4},{6,5},{7,6},{8,7},{9,8},{10,9... | collective-permute-start | bytes 737288 | tf_op jit(solution)/shard_map/ppermute | solution.py:39
  47.3 7.9 %collective-permute-done.1 = bf16[48,2560]{1,0:T(8,128)(2,1)S(1)} collective-permute-done((bf16[48,2560]{1,0:T(8,128)(2,1)}, bf16[48,2560]{1,0:T(8,128)(2,1)S(1)}, u32[]{:S(2)}, u32[]{:S(2)}) %collective-permute-start.1) | collective-permute-done | bytes 245792 | tf_op jit(solution)/shard_map/ppermute | solution.py:39
  55.3 5.5 %collective-permute-start.2 = (bf16[48,2560]{1,0:T(8,128)(2,1)S(1)}, bf16[48,2560]{1,0:T(8,128)(2,1)}, u32[]{:S(2)}, u32[]{:S(2)}) collective-permute-start(bf16[48,2560]{1,0:T(8,128)(2,1)S(1)} %collective-permute-done.1), channel_id=1, source_target_pairs={{0,15},{1,0},{2,1},{3,2},{4,3},{5,4},{6,5},{7,6},{8,7},{9,8},{10,9... | collective-permute-start | bytes 737288 | tf_op jit(solution)/shard_map/ppermute | solution.py:39
  62.8 7.5 %all-to-all-start = ((bf16[32,5,2560]{2,1,0:T(8,128)(2,1)}), bf16[32,5,2560]{2,1,0:T(8,128)(2,1)}, u32[]{:S(2)}, u32[]{:S(2)}) async-start(bf16[32,5,2560]{2,1,0:T(8,128)(2,1)} %reshape.126), calls=%async_computation | async-start | bytes 2621440 | tf_op jit(solution)/shard_map/all_to_all | solution.py:92
  71.9 5.7 %collective-permute-start.3 = (bf16[48,2560]{1,0:T(8,128)(2,1)}, bf16[48,2560]{1,0:T(8,128)(2,1)}, u32[]{:S(2)}, u32[]{:S(2)}) collective-permute-start(bf16[48,2560]{1,0:T(8,128)(2,1)} %collective-permute-done.2), channel_id=1, source_target_pairs={{0,15},{1,0},{2,1},{3,2},{4,3},{5,4},{6,5},{7,6},{8,7},{9,8},{10,9... | collective-permute-start | bytes 737288 | tf_op jit(solution)/shard_map/ppermute | solution.py:39
  82.7 5.7 %all-to-all-done = bf16[32,5,2560]{2,1,0:T(8,128)(2,1)} async-done(((bf16[32,5,2560]{2,1,0:T(8,128)(2,1)}), bf16[32,5,2560]{2,1,0:T(8,128)(2,1)}, u32[]{:S(2)}, u32[]{:S(2)}) %all-to-all-start) | async-done | bytes 819232 | tf_op jit(solution)/shard_map/all_to_all | solution.py:92
  89.9 5.1 %collective-permute-start.4 = (bf16[48,2560]{1,0:T(8,128)(2,1)}, bf16[48,2560]{1,0:T(8,128)(2,1)S(1)}, u32[]{:S(2)}, u32[]{:S(2)}) collective-permute-start(bf16[48,2560]{1,0:T(8,128)(2,1)} %collective-permute-done.3), channel_id=1, source_target_pairs={{0,15},{1,0},{2,1},{3,2},{4,3},{5,4},{6,5},{7,6},{8,7},{9,8},{10,9... | collective-permute-start | bytes 737288 | tf_op jit(solution)/shard_map/ppermute | solution.py:39
  98.7 7.9 %collective-permute-done.4 = bf16[48,2560]{1,0:T(8,128)(2,1)S(1)} collective-permute-done((bf16[48,2560]{1,0:T(8,128)(2,1)}, bf16[48,2560]{1,0:T(8,128)(2,1)S(1)}, u32[]{:S(2)}, u32[]{:S(2)}) %collective-permute-start.4) | collective-permute-done | bytes 245792 | tf_op jit(solution)/shard_map/ppermute | solution.py:39
  106.6 5.5 %collective-permute-start.5 = (bf16[48,2560]{1,0:T(8,128)(2,1)S(1)}, bf16[48,2560]{1,0:T(8,128)(2,1)S(1)}, u32[]{:S(2)}, u32[]{:S(2)}) collective-permute-start(bf16[48,2560]{1,0:T(8,128)(2,1)S(1)} %collective-permute-done.4), channel_id=1, source_target_pairs={{0,15},{1,0},{2,1},{3,2},{4,3},{5,4},{6,5},{7,6},{8,7},{9,8},{10,9... | collective-permute-start | bytes 737288 | tf_op jit(solution)/shard_map/ppermute | solution.py:39
  114.7 8.4 %collective-permute-done.5 = bf16[48,2560]{1,0:T(8,128)(2,1)S(1)} collective-permute-done((bf16[48,2560]{1,0:T(8,128)(2,1)S(1)}, bf16[48,2560]{1,0:T(8,128)(2,1)S(1)}, u32[]{:S(2)}, u32[]{:S(2)}) %collective-permute-start.5) | collective-permute-done | bytes 245792 | tf_op jit(solution)/shard_map/ppermute | solution.py:39
  123.1 5.6 %collective-permute-start.6 = (bf16[48,2560]{1,0:T(8,128)(2,1)S(1)}, bf16[48,2560]{1,0:T(8,128)(2,1)S(1)}, u32[]{:S(2)}, u32[]{:S(2)}) collective-permute-start(bf16[48,2560]{1,0:T(8,128)(2,1)S(1)} %collective-permute-done.5), channel_id=1, source_target_pairs={{0,15},{1,0},{2,1},{3,2},{4,3},{5,4},{6,5},{7,6},{8,7},{9,8},{10,9... | collective-permute-start | bytes 737288 | tf_op jit(solution)/shard_map/ppermute | solution.py:39
  131.4 8.2 %collective-permute-done.6 = bf16[48,2560]{1,0:T(8,128)(2,1)S(1)} collective-permute-done((bf16[48,2560]{1,0:T(8,128)(2,1)S(1)}, bf16[48,2560]{1,0:T(8,128)(2,1)S(1)}, u32[]{:S(2)}, u32[]{:S(2)}) %collective-permute-start.6) | collective-permute-done | bytes 245792 | tf_op jit(solution)/shard_map/ppermute | solution.py:39
  139.5 5.6 %collective-permute-start.15 = (bf16[48,1280]{1,0:T(8,128)(2,1)S(1)}, bf16[48,1280]{1,0:T(8,128)(2,1)S(1)}, u32[]{:S(2)}, u32[]{:S(2)}) collective-permute-start(bf16[48,1280]{1,0:T(8,128)(2,1)S(1)} %slice.29), channel_id=1, source_target_pairs={{0,15},{1,0},{2,1},{3,2},{4,3},{5,4},{6,5},{7,6},{8,7},{9,8},{10,9... | collective-permute-start | bytes 368648 | tf_op jit(solution)/shard_map/ppermute | solution.py:45
  148.0 5.2 %collective-permute-done.14 = bf16[48,1280]{1,0:T(8,128)(2,1)S(1)} collective-permute-done((bf16[48,1280]{1,0:T(8,128)(2,1)S(1)}, bf16[48,1280]{1,0:T(8,128)(2,1)S(1)}, u32[]{:S(2)}, u32[]{:S(2)}) %collective-permute-start.14) | collective-permute-done | bytes 122912 | tf_op jit(solution)/shard_map/ppermute | solution.py:44
  155.3 3.8 %fusion.36 = (bf16[16,1,160,768]{3,2,1,0:T(8,128)(2,1)S(1)}, bf16[16,1,160,768]{3,2,1,0:T(8,128)(2,1)S(1)}) fusion(bf16[16,2,160,768]{3,2,1,0:T(8,128)(2,1)} %bitcast.81), kind=kLoop, calls=%fused_computation.85 | loop fusion | bytes 15728640 | tf_op jit(solution)/shard_map/slice | solution.py:69
  164.4 3.1 %add_convert_fusion = bf16[768,2560]{1,0:T(8,128)(2,1)} fusion(f32[768,2560]{1,0:T(8,128)S(1)} %fusion.8, bf16[160,2560]{1,0:T(8,128)(2,1)S(1)} %reshape.127, f32[160,768]{1,0:T(8,128)S(1)} %fusion.38, f32[160,768]{1,0:T(8,128)S(1)} %fusion.39), kind=kOutput, calls=%fused_computation.1 | convolution fusion | flops 633815040 | bytes 13598720 | tf_op jit(solution)/shard_map/dot_general | solution.py:120
  173.1 4.8 %gather_fusion = bf16[16,48,2560]{2,1,0:T(8,128)(2,1)} fusion(bf16[16,48,2560]{2,1,0:T(8,128)(2,1)} %bitcast_dynamic-update-slice_fusion, s32[1024]{0:T(1024)S(1)} %pad_clamp_fusion), kind=kCustom, calls=%fused_computation | custom fusion | bytes 7864384 | tf_op jit(solution)/shard_map/jit(_take)/gather | solution.py:49
  177.9 2.5 %bitcast_select_fusion = bf16[768,2560]{1,0:T(8,128)(2,1)S(1)} fusion(bf16[16,48,2560]{2,1,0:T(8,128)(2,1)} %gather_fusion, pred[768]{0:T(1024)(128)(4,1)S(1)} %broadcast_in_dim.33), kind=kLoop, calls=%fused_computation.2 | loop fusion | flops 1966080 | bytes 7865088 | tf_op jit(solution)/shard_map/jit(_take)/select_n | solution.py:49
  190.2 6.5 %all-to-all-start.2 = ((bf16[32,5,2560]{2,1,0:T(8,128)(2,1)}), bf16[32,5,2560]{2,1,0:T(8,128)(2,1)}, u32[]{:S(2)}, u32[]{:S(2)}) async-start(bf16[32,5,2560]{2,1,0:T(8,128)(2,1)} %reshape.130), calls=%async_computation.2 | async-start | bytes 2621440 | tf_op jit(solution)/shard_map/all_to_all | solution.py:97
  196.7 3.7 %fusion.15 = f32[128,2560]{1,0:T(8,128)S(1)} fusion(bf16[2560,768]{1,0:T(8,128)(2,1)} %bitcast.78, f32[128,768]{1,0:T(8,128)S(1)} %convolution_bitcast_fusion, f32[128,768]{1,0:T(8,128)S(1)} %copy-done.14, f32[128,768]{1,0:T(8,128)S(1)} %copy-done.13), kind=kOutput, calls=%fused_computation.49 | convolution fusion | flops 504299520 | bytes 6422528 | tf_op jit(solution)/shard_map/dot_general | solution.py:8
  201.9 12.9 %all-to-all-done.2 = bf16[32,5,2560]{2,1,0:T(8,128)(2,1)} async-done(((bf16[32,5,2560]{2,1,0:T(8,128)(2,1)}), bf16[32,5,2560]{2,1,0:T(8,128)(2,1)}, u32[]{:S(2)}, u32[]{:S(2)}) %all-to-all-start.2) | async-done | bytes 819232 | tf_op jit(solution)/shard_map/all_to_all | solution.py:97
  217.5 23.9 %reduce-scatter.2.cloned.1.call-done = bf16[48,2560]{1,0:T(8,128)(2,1)} async-done(((bf16[768,2560]{1,0:T(8,128)(2,1)}), bf16[48,2560]{1,0:T(8,128)(2,1)}) %reduce-scatter.2.cloned.1.call-update) | async-done | bytes 245776 | tf_op jit(solution)/shard_map/reduce_scatter | solution.py:117
  (121 shorter events, 63.8 us)
Async XLA Ops:
  7.2 148.1 %all-gather.3.cloned.1.call-start = ((), (), s32[]{:S(2)}) async-start(), calls=%async_computation.5 | async-start | bytes 8355840 | tf_op jit(solution)/shard_map/all_gather | solution.py:66
  9.2 29.4 %collective-permute-start = (bf16[48,2560]{1,0:T(8,128)(2,1)}, bf16[48,2560]{1,0:T(8,128)(2,1)}, u32[]{:S(2)}, u32[]{:S(2)}) collective-permute-start(bf16[48,2560]{1,0:T(8,128)(2,1)} %bitcast.82), channel_id=1, source_target_pairs={{0,15},{1,0},{2,1},{3,2},{4,3},{5,4},{6,5},{7,6},{8,7},{9,8},{10,9... | collective-permute-start | bytes 737288 | tf_op jit(solution)/shard_map/ppermute | solution.py:39
  20.7 23.1 %collective-permute-start.7 = (bf16[48,2560]{1,0:T(8,128)(2,1)}, bf16[48,2560]{1,0:T(8,128)(2,1)}, u32[]{:S(2)}, u32[]{:S(2)}) collective-permute-start(bf16[48,2560]{1,0:T(8,128)(2,1)} %bitcast.83), channel_id=1, source_target_pairs={{0,1},{1,2},{2,3},{3,4},{4,5},{5,6},{6,7},{7,8},{8,9},{9,10},{10,1... | collective-permute-start | bytes 737288 | tf_op jit(solution)/shard_map/ppermute | solution.py:38
  26.6 36.1 %all-to-all-start.1 = ((bf16[32,5,2560]{2,1,0:T(8,128)(2,1)}), bf16[32,5,2560]{2,1,0:T(8,128)(2,1)S(1)}, u32[]{:S(2)}, u32[]{:S(2)}) async-start(bf16[32,5,2560]{2,1,0:T(8,128)(2,1)} %reshape.128), calls=%async_computation.1 | async-start | bytes 2621440 | tf_op jit(solution)/shard_map/all_to_all | solution.py:91
  38.6 16.7 %collective-permute-start.1 = (bf16[48,2560]{1,0:T(8,128)(2,1)}, bf16[48,2560]{1,0:T(8,128)(2,1)S(1)}, u32[]{:S(2)}, u32[]{:S(2)}) collective-permute-start(bf16[48,2560]{1,0:T(8,128)(2,1)} %collective-permute-done), channel_id=1, source_target_pairs={{0,15},{1,0},{2,1},{3,2},{4,3},{5,4},{6,5},{7,6},{8,7},{9,8},{10,9... | collective-permute-start | bytes 737288 | tf_op jit(solution)/shard_map/ppermute | solution.py:39
  43.8 17.1 %collective-permute-start.8 = (bf16[48,2560]{1,0:T(8,128)(2,1)}, bf16[48,2560]{1,0:T(8,128)(2,1)S(1)}, u32[]{:S(2)}, u32[]{:S(2)}) collective-permute-start(bf16[48,2560]{1,0:T(8,128)(2,1)} %collective-permute-done.7), channel_id=1, source_target_pairs={{0,1},{1,2},{2,3},{3,4},{4,5},{5,6},{6,7},{7,8},{8,9},{9,10},{10,1... | collective-permute-start | bytes 737288 | tf_op jit(solution)/shard_map/ppermute | solution.py:38
  55.3 16.6 %collective-permute-start.2 = (bf16[48,2560]{1,0:T(8,128)(2,1)S(1)}, bf16[48,2560]{1,0:T(8,128)(2,1)}, u32[]{:S(2)}, u32[]{:S(2)}) collective-permute-start(bf16[48,2560]{1,0:T(8,128)(2,1)S(1)} %collective-permute-done.1), channel_id=1, source_target_pairs={{0,15},{1,0},{2,1},{3,2},{4,3},{5,4},{6,5},{7,6},{8,7},{9,8},{10,9... | collective-permute-start | bytes 737288 | tf_op jit(solution)/shard_map/ppermute | solution.py:39
  60.8 16.8 %collective-permute-start.9 = (bf16[48,2560]{1,0:T(8,128)(2,1)S(1)}, bf16[48,2560]{1,0:T(8,128)(2,1)S(1)}, u32[]{:S(2)}, u32[]{:S(2)}) collective-permute-start(bf16[48,2560]{1,0:T(8,128)(2,1)S(1)} %collective-permute-done.8), channel_id=1, source_target_pairs={{0,1},{1,2},{2,3},{3,4},{4,5},{5,6},{6,7},{7,8},{8,9},{9,10},{10,1... | collective-permute-start | bytes 737288 | tf_op jit(solution)/shard_map/ppermute | solution.py:38
  62.8 25.6 %all-to-all-start = ((bf16[32,5,2560]{2,1,0:T(8,128)(2,1)}), bf16[32,5,2560]{2,1,0:T(8,128)(2,1)}, u32[]{:S(2)}, u32[]{:S(2)}) async-start(bf16[32,5,2560]{2,1,0:T(8,128)(2,1)} %reshape.126), calls=%async_computation | async-start | bytes 2621440 | tf_op jit(solution)/shard_map/all_to_all | solution.py:92
  70.2 171.1 %reduce-scatter.2.cloned.1.call-start = ((), (), s32[]{:S(2)}) async-start(), calls=%async_computation.4 | async-start | bytes 4177920 | tf_op jit(solution)/shard_map/reduce_scatter | solution.py:117
  71.9 18.0 %collective-permute-start.3 = (bf16[48,2560]{1,0:T(8,128)(2,1)}, bf16[48,2560]{1,0:T(8,128)(2,1)}, u32[]{:S(2)}, u32[]{:S(2)}) collective-permute-start(bf16[48,2560]{1,0:T(8,128)(2,1)} %collective-permute-done.2), channel_id=1, source_target_pairs={{0,15},{1,0},{2,1},{3,2},{4,3},{5,4},{6,5},{7,6},{8,7},{9,8},{10,9... | collective-permute-start | bytes 737288 | tf_op jit(solution)/shard_map/ppermute | solution.py:39
  77.6 77.0 %copy-start.17 = (bf16[48,2560]{1,0:T(8,128)(2,1)}, bf16[48,2560]{1,0:T(8,128)(2,1)S(1)}, u32[]{:S(2)}) copy-start(bf16[48,2560]{1,0:T(8,128)(2,1)S(1)} %collective-permute-done.9) | copy-start | bytes 737284
  77.6 17.4 %collective-permute-start.10 = (bf16[48,2560]{1,0:T(8,128)(2,1)S(1)}, bf16[48,2560]{1,0:T(8,128)(2,1)S(1)}, u32[]{:S(2)}, u32[]{:S(2)}) collective-permute-start(bf16[48,2560]{1,0:T(8,128)(2,1)S(1)} %collective-permute-done.9), channel_id=1, source_target_pairs={{0,1},{1,2},{2,3},{3,4},{4,5},{5,6},{6,7},{7,8},{8,9},{9,10},{10,1... | collective-permute-start | bytes 737288 | tf_op jit(solution)/shard_map/ppermute | solution.py:38
  89.9 16.7 %collective-permute-start.4 = (bf16[48,2560]{1,0:T(8,128)(2,1)}, bf16[48,2560]{1,0:T(8,128)(2,1)S(1)}, u32[]{:S(2)}, u32[]{:S(2)}) collective-permute-start(bf16[48,2560]{1,0:T(8,128)(2,1)} %collective-permute-done.3), channel_id=1, source_target_pairs={{0,15},{1,0},{2,1},{3,2},{4,3},{5,4},{6,5},{7,6},{8,7},{9,8},{10,9... | collective-permute-start | bytes 737288 | tf_op jit(solution)/shard_map/ppermute | solution.py:39
  95.1 64.0 %copy-start.19 = (bf16[48,2560]{1,0:T(8,128)(2,1)}, bf16[48,2560]{1,0:T(8,128)(2,1)S(1)}, u32[]{:S(2)}) copy-start(bf16[48,2560]{1,0:T(8,128)(2,1)S(1)} %collective-permute-done.10) | copy-start | bytes 737284
  95.1 17.0 %collective-permute-start.11 = (bf16[48,2560]{1,0:T(8,128)(2,1)S(1)}, bf16[48,2560]{1,0:T(8,128)(2,1)S(1)}, u32[]{:S(2)}, u32[]{:S(2)}) collective-permute-start(bf16[48,2560]{1,0:T(8,128)(2,1)S(1)} %collective-permute-done.10), channel_id=1, source_target_pairs={{0,1},{1,2},{2,3},{3,4},{4,5},{5,6},{6,7},{7,8},{8,9},{9,10},{10,1... | collective-permute-start | bytes 737288 | tf_op jit(solution)/shard_map/ppermute | solution.py:38
  106.6 16.5 %collective-permute-start.5 = (bf16[48,2560]{1,0:T(8,128)(2,1)S(1)}, bf16[48,2560]{1,0:T(8,128)(2,1)S(1)}, u32[]{:S(2)}, u32[]{:S(2)}) collective-permute-start(bf16[48,2560]{1,0:T(8,128)(2,1)S(1)} %collective-permute-done.4), channel_id=1, source_target_pairs={{0,15},{1,0},{2,1},{3,2},{4,3},{5,4},{6,5},{7,6},{8,7},{9,8},{10,9... | collective-permute-start | bytes 737288 | tf_op jit(solution)/shard_map/ppermute | solution.py:39
  112.1 16.6 %collective-permute-start.12 = (bf16[48,2560]{1,0:T(8,128)(2,1)S(1)}, bf16[48,2560]{1,0:T(8,128)(2,1)S(1)}, u32[]{:S(2)}, u32[]{:S(2)}) collective-permute-start(bf16[48,2560]{1,0:T(8,128)(2,1)S(1)} %collective-permute-done.11), channel_id=1, source_target_pairs={{0,1},{1,2},{2,3},{3,4},{4,5},{5,6},{6,7},{7,8},{8,9},{9,10},{10,1... | collective-permute-start | bytes 737288 | tf_op jit(solution)/shard_map/ppermute | solution.py:38
  123.1 16.4 %collective-permute-start.6 = (bf16[48,2560]{1,0:T(8,128)(2,1)S(1)}, bf16[48,2560]{1,0:T(8,128)(2,1)S(1)}, u32[]{:S(2)}, u32[]{:S(2)}) collective-permute-start(bf16[48,2560]{1,0:T(8,128)(2,1)S(1)} %collective-permute-done.5), channel_id=1, source_target_pairs={{0,15},{1,0},{2,1},{3,2},{4,3},{5,4},{6,5},{7,6},{8,7},{9,8},{10,9... | collective-permute-start | bytes 737288 | tf_op jit(solution)/shard_map/ppermute | solution.py:39
  128.7 16.4 %collective-permute-start.13 = (bf16[48,2560]{1,0:T(8,128)(2,1)S(1)}, bf16[48,2560]{1,0:T(8,128)(2,1)S(1)}, u32[]{:S(2)}, u32[]{:S(2)}) collective-permute-start(bf16[48,2560]{1,0:T(8,128)(2,1)S(1)} %collective-permute-done.12), channel_id=1, source_target_pairs={{0,1},{1,2},{2,3},{3,4},{4,5},{5,6},{6,7},{7,8},{8,9},{9,10},{10,1... | collective-permute-start | bytes 737288 | tf_op jit(solution)/shard_map/ppermute | solution.py:38
  139.5 8.5 %collective-permute-start.15 = (bf16[48,1280]{1,0:T(8,128)(2,1)S(1)}, bf16[48,1280]{1,0:T(8,128)(2,1)S(1)}, u32[]{:S(2)}, u32[]{:S(2)}) collective-permute-start(bf16[48,1280]{1,0:T(8,128)(2,1)S(1)} %slice.29), channel_id=1, source_target_pairs={{0,15},{1,0},{2,1},{3,2},{4,3},{5,4},{6,5},{7,6},{8,7},{9,8},{10,9... | collective-permute-start | bytes 368648 | tf_op jit(solution)/shard_map/ppermute | solution.py:45
  145.2 8.0 %collective-permute-start.14 = (bf16[48,1280]{1,0:T(8,128)(2,1)S(1)}, bf16[48,1280]{1,0:T(8,128)(2,1)S(1)}, u32[]{:S(2)}, u32[]{:S(2)}) collective-permute-start(bf16[48,1280]{1,0:T(8,128)(2,1)S(1)} %slice.28), channel_id=1, source_target_pairs={{0,1},{1,2},{2,3},{3,4},{4,5},{5,6},{6,7},{7,8},{8,9},{9,10},{10,1... | collective-permute-start | bytes 368648 | tf_op jit(solution)/shard_map/ppermute | solution.py:44
  190.2 24.6 %all-to-all-start.2 = ((bf16[32,5,2560]{2,1,0:T(8,128)(2,1)}), bf16[32,5,2560]{2,1,0:T(8,128)(2,1)}, u32[]{:S(2)}, u32[]{:S(2)}) async-start(bf16[32,5,2560]{2,1,0:T(8,128)(2,1)} %reshape.130), calls=%async_computation.2 | async-start | bytes 2621440 | tf_op jit(solution)/shard_map/all_to_all | solution.py:97
  200.4 40.9 %copy-start.1 = (bf16[128,2560]{1,0:T(8,128)(2,1)S(1)}, bf16[128,2560]{1,0:T(8,128)(2,1)}, u32[]{:S(2)}) copy-start(bf16[128,2560]{1,0:T(8,128)(2,1)} %param.8) | copy-start | bytes 1966084
  (20 other events, 187.9 us)
Sparse Core Ops, SparseCore 0:
  10.7 136.6 all-gather.2
  167.6 73.6 reduce-scatter.1

commit v7 on v6

--- a/solution.py
+++ b/solution.py
@@ -26,8 +26,8 @@
 
 
 def ring_gather(piece, axis):
-    n = lax.axis_size(axis)
-    idx = lax.axis_index(axis)
+    n = lax.axis_size(axis[0]) * lax.axis_size(axis[1])
+    idx = lax.axis_index(axis[0]) * lax.axis_size(axis[1]) + lax.axis_index(axis[1])
     right = [(i, (i + 1) % n) for i in range(n)]
     left = [(i, (i - 1) % n) for i in range(n)]
     ahead = {0: piece}
@@ -49,6 +49,9 @@
     return jnp.take(stacked, order, axis=0)
 
 
+REPLICA = ("zhi", "zlo")
+
+
 def local(tokens, cotangent, partner, combine, counts, w_gate, w_up, w_down):
     tok_rows = tokens.shape[0]
     width = tokens.shape[1]
@@ -63,8 +66,8 @@
     upstream = cotangent.astype(jnp.float32)
     q_home = (upstream * share_home[:, None]).astype(jnp.bfloat16)
     q_away = (upstream * share_away[:, None]).astype(jnp.bfloat16)
-    pair = lax.all_gather(jnp.stack([w_gate[0], w_up[0]]), "replica", axis=0, tiled=False)
-    down_full = ring_gather(w_down[0], "replica")
+    pair = lax.all_gather(jnp.stack([w_gate[0], w_up[0]]), REPLICA, axis=0, tiled=False)
+    down_full = ring_gather(w_down[0], REPLICA)
     gate_w = pair[:, 0].reshape(-1, w_gate.shape[2])
     up_w = pair[:, 1].reshape(-1, w_up.shape[2])
     down_w = down_full.reshape(-1, down_full.shape[2])
@@ -114,33 +117,34 @@
     token_grad = (grad_home + grad_away).astype(jnp.bfloat16)
     flat_hidden = hidden_away.reshape(expert_count * capacity, -1)
     flat_q = q_there.reshape(expert_count * capacity, width)
-    grad_down = lax.psum_scatter(
-        (
-            lax.dot_general(hidden_home, q_home, contract, preferred_element_type=jnp.float32)
-            + lax.dot_general(flat_hidden, flat_q, contract, preferred_element_type=jnp.float32)
-        ).astype(jnp.bfloat16),
-        "replica",
-        scatter_dimension=0,
-        tiled=True,
-    )
+    n_hi, n_lo = lax.axis_size(REPLICA[0]), lax.axis_size(REPLICA[1])
+
+    def lo_major(h):
+        rows = h.shape[0]
+        return h.reshape(rows, n_hi, n_lo, -1).transpose(0, 2, 1, 3).reshape(rows, -1)
+
+    partial = (
+        lax.dot_general(lo_major(hidden_home), q_home, contract, preferred_element_type=jnp.float32)
+        + lax.dot_general(lo_major(flat_hidden), flat_q, contract, preferred_element_type=jnp.float32)
+    ).astype(jnp.bfloat16)
+    grad_down = lax.psum_scatter(partial, REPLICA[1], scatter_dimension=0, tiled=True)
+    grad_down = lax.psum_scatter(grad_down, REPLICA[0], scatter_dimension=0, tiled=True)
     return (token_grad, grad_down[None])
 
 
 def solution(mesh):
-    placed = (
-        P(("expert", "replica"), None),
-        P(("expert", "replica"), None),
-        P(("expert", "replica"), None),
-        P(("expert", "replica"), None),
-        P(("expert", "replica")),
-        P("expert", "replica", None),
-        P("expert", "replica", None),
-        P("expert", "replica", None),
+    n_rep = mesh.shape["replica"]
+    n_lo = 4 if n_rep % 4 == 0 else 1
+    grid = jax.sharding.Mesh(
+        mesh.devices.reshape(mesh.shape["expert"], n_rep // n_lo, n_lo), ("expert",) + REPLICA
     )
+    rows = P(("expert",) + REPLICA, None)
+    weight = P("expert", REPLICA, None)
+    placed = (rows, rows, rows, rows, P(("expert",) + REPLICA), weight, weight, weight)
     return jax.shard_map(
         local,
-        mesh=mesh,
+        mesh=grid,
         in_specs=placed,
-        out_specs=(P(("expert", "replica"), None), P("expert", "replica", None)),
+        out_specs=(rows, weight),
         check_vma=False,
     )

time: 250 us -> 318 us (1.27)
  waiting for transfers between devices: 81 us -> 136 us
  local copies, waits for them, and re-layouts: 36 us -> 41.4 us
  other arithmetic: 8.11 us -> 11.3 us
    reduce_scatter x1 -> x2, waiting for transfers between devices: 23.9 us -> 83.9 us  [the longest x1 57.7 us: local(): lax.psum_scatter(partial, REPLICA[1], scatter_dimension=0, tiled=True)]
    ppermute x1, waiting for transfers between devices: 5.16 us -> 0.01 us  [ring_gather(): rh = lax.ppermute(r[..., :cut], axis, right)]
    unnamed x60 -> x62, local copies, waits for them, and re-layouts: 17.4 us -> 20.5 us
  transfers between devices with their start and end apart: 21 -> 22, of which waited for: 9 -> 10; matrix products, arithmetic and copies ran while one was open for 20% -> 22% of each run, Pallas kernels for 0% -> 0%
where the time goes in v7:
time: 318 us; the launch traced here: 316 us
  waiting for transfers between devices  136 us (43%)
  starting transfers between devices  87.7 us (28%)
  local copies, waits for them, and re-layouts  41.4 us (13%)
  matrix products  24 us (8%)
  between operations  15 us (5%)
  other arithmetic  11.3 us (4%)
    reduce_scatter x1, waiting for transfers between devices, local(): lax.psum_scatter(partial, REPLICA[1], scatter_dimension=0, tiled=True)  57.7 us
    ppermute x7, starting transfers between devices, ring_gather(): l = lax.ppermute(l, axis, left)  43.9 us
    ppermute x7, waiting for transfers between devices, ring_gather(): l = lax.ppermute(l, axis, left)  33.3 us
    reduce_scatter x1, waiting for transfers between devices, local(): lax.psum_scatter(grad_down, REPLICA[0], scatter_dimension=0, tiled=True)  26.2 us
    unnamed x62, local copies, waits for them, and re-layouts  20.5 us
    ppermute x7, starting transfers between devices, ring_gather(): r = lax.ppermute(r, axis, right)  13.4 us
    all_to_all x1, waiting for transfers between devices, local(): lax.all_to_all(grad_there.astype(jnp.bfloat16).reshape(expert_count, item...  13 us
    dot_general x6, matrix products, against_rows(): lax.dot_general(left, matrix, (((1,), (1,)), ((), ())), preferred_element...  13 us
  transfers between devices with their start and end apart: 22, of which 10 were waited for; matrix products, arithmetic and copies ran while one was open for 22% of the time, Pallas kernels for 0%

profile of v7, /device:TPU:6, one launch (start us, length us, event | category | flops | bytes accessed | tf_op | source)
XLA Modules:
  0.0 315.9 jit_solution(10011575921280382657)
XLA Ops:
  9.2 11.4 %collective-permute-start = (bf16[48,2560]{1,0:T(8,128)(2,1)}, bf16[48,2560]{1,0:T(8,128)(2,1)}, u32[]{:S(2)}, u32[]{:S(2)}) collective-permute-start(bf16[48,2560]{1,0:T(8,128)(2,1)} %bitcast.96), channel_id=1, source_target_pairs={{0,15},{1,0},{2,1},{3,2},{4,3},{5,4},{6,5},{7,6},{8,7},{9,8},{10,9... | collective-permute-start | bytes 737288 | tf_op jit(solution)/shard_map/ppermute | solution.py:39
  26.6 7.6 %all-to-all-start.1 = ((bf16[32,5,2560]{2,1,0:T(8,128)(2,1)}), bf16[32,5,2560]{2,1,0:T(8,128)(2,1)S(1)}, u32[]{:S(2)}, u32[]{:S(2)}) async-start(bf16[32,5,2560]{2,1,0:T(8,128)(2,1)} %reshape.137), calls=%async_computation.1 | async-start | bytes 2621440 | tf_op jit(solution)/shard_map/all_to_all | solution.py:94
  38.6 5.1 %collective-permute-start.1 = (bf16[48,2560]{1,0:T(8,128)(2,1)}, bf16[48,2560]{1,0:T(8,128)(2,1)S(1)}, u32[]{:S(2)}, u32[]{:S(2)}) collective-permute-start(bf16[48,2560]{1,0:T(8,128)(2,1)} %collective-permute-done), channel_id=1, source_target_pairs={{0,15},{1,0},{2,1},{3,2},{4,3},{5,4},{6,5},{7,6},{8,7},{9,8},{10,9... | collective-permute-start | bytes 737288 | tf_op jit(solution)/shard_map/ppermute | solution.py:39
  47.3 7.9 %collective-permute-done.1 = bf16[48,2560]{1,0:T(8,128)(2,1)S(1)} collective-permute-done((bf16[48,2560]{1,0:T(8,128)(2,1)}, bf16[48,2560]{1,0:T(8,128)(2,1)S(1)}, u32[]{:S(2)}, u32[]{:S(2)}) %collective-permute-start.1) | collective-permute-done | bytes 245792 | tf_op jit(solution)/shard_map/ppermute | solution.py:39
  55.3 5.5 %collective-permute-start.2 = (bf16[48,2560]{1,0:T(8,128)(2,1)S(1)}, bf16[48,2560]{1,0:T(8,128)(2,1)}, u32[]{:S(2)}, u32[]{:S(2)}) collective-permute-start(bf16[48,2560]{1,0:T(8,128)(2,1)S(1)} %collective-permute-done.1), channel_id=1, source_target_pairs={{0,15},{1,0},{2,1},{3,2},{4,3},{5,4},{6,5},{7,6},{8,7},{9,8},{10,9... | collective-permute-start | bytes 737288 | tf_op jit(solution)/shard_map/ppermute | solution.py:39
  62.7 7.5 %all-to-all-start = ((bf16[32,5,2560]{2,1,0:T(8,128)(2,1)}), bf16[32,5,2560]{2,1,0:T(8,128)(2,1)}, u32[]{:S(2)}, u32[]{:S(2)}) async-start(bf16[32,5,2560]{2,1,0:T(8,128)(2,1)} %reshape.135), calls=%async_computation | async-start | bytes 2621440 | tf_op jit(solution)/shard_map/all_to_all | solution.py:95
  71.9 5.7 %collective-permute-start.3 = (bf16[48,2560]{1,0:T(8,128)(2,1)}, bf16[48,2560]{1,0:T(8,128)(2,1)}, u32[]{:S(2)}, u32[]{:S(2)}) collective-permute-start(bf16[48,2560]{1,0:T(8,128)(2,1)} %collective-permute-done.2), channel_id=1, source_target_pairs={{0,15},{1,0},{2,1},{3,2},{4,3},{5,4},{6,5},{7,6},{8,7},{9,8},{10,9... | collective-permute-start | bytes 737288 | tf_op jit(solution)/shard_map/ppermute | solution.py:39
  82.3 6.1 %all-to-all-done = bf16[32,5,2560]{2,1,0:T(8,128)(2,1)} async-done(((bf16[32,5,2560]{2,1,0:T(8,128)(2,1)}), bf16[32,5,2560]{2,1,0:T(8,128)(2,1)}, u32[]{:S(2)}, u32[]{:S(2)}) %all-to-all-start) | async-done | bytes 819232 | tf_op jit(solution)/shard_map/all_to_all | solution.py:95
  89.9 5.1 %collective-permute-start.4 = (bf16[48,2560]{1,0:T(8,128)(2,1)}, bf16[48,2560]{1,0:T(8,128)(2,1)S(1)}, u32[]{:S(2)}, u32[]{:S(2)}) collective-permute-start(bf16[48,2560]{1,0:T(8,128)(2,1)} %collective-permute-done.3), channel_id=1, source_target_pairs={{0,15},{1,0},{2,1},{3,2},{4,3},{5,4},{6,5},{7,6},{8,7},{9,8},{10,9... | collective-permute-start | bytes 737288 | tf_op jit(solution)/shard_map/ppermute | solution.py:39
  98.6 8.0 %collective-permute-done.4 = bf16[48,2560]{1,0:T(8,128)(2,1)S(1)} collective-permute-done((bf16[48,2560]{1,0:T(8,128)(2,1)}, bf16[48,2560]{1,0:T(8,128)(2,1)S(1)}, u32[]{:S(2)}, u32[]{:S(2)}) %collective-permute-start.4) | collective-permute-done | bytes 245792 | tf_op jit(solution)/shard_map/ppermute | solution.py:39
  106.6 5.5 %collective-permute-start.5 = (bf16[48,2560]{1,0:T(8,128)(2,1)S(1)}, bf16[48,2560]{1,0:T(8,128)(2,1)S(1)}, u32[]{:S(2)}, u32[]{:S(2)}) collective-permute-start(bf16[48,2560]{1,0:T(8,128)(2,1)S(1)} %collective-permute-done.4), channel_id=1, source_target_pairs={{0,15},{1,0},{2,1},{3,2},{4,3},{5,4},{6,5},{7,6},{8,7},{9,8},{10,9... | collective-permute-start | bytes 737288 | tf_op jit(solution)/shard_map/ppermute | solution.py:39
  114.7 8.4 %collective-permute-done.5 = bf16[48,2560]{1,0:T(8,128)(2,1)S(1)} collective-permute-done((bf16[48,2560]{1,0:T(8,128)(2,1)S(1)}, bf16[48,2560]{1,0:T(8,128)(2,1)S(1)}, u32[]{:S(2)}, u32[]{:S(2)}) %collective-permute-start.5) | collective-permute-done | bytes 245792 | tf_op jit(solution)/shard_map/ppermute | solution.py:39
  123.1 5.6 %collective-permute-start.6 = (bf16[48,2560]{1,0:T(8,128)(2,1)S(1)}, bf16[48,2560]{1,0:T(8,128)(2,1)S(1)}, u32[]{:S(2)}, u32[]{:S(2)}) collective-permute-start(bf16[48,2560]{1,0:T(8,128)(2,1)S(1)} %collective-permute-done.5), channel_id=1, source_target_pairs={{0,15},{1,0},{2,1},{3,2},{4,3},{5,4},{6,5},{7,6},{8,7},{9,8},{10,9... | collective-permute-start | bytes 737288 | tf_op jit(solution)/shard_map/ppermute | solution.py:39
  131.4 8.1 %collective-permute-done.6 = bf16[48,2560]{1,0:T(8,128)(2,1)S(1)} collective-permute-done((bf16[48,2560]{1,0:T(8,128)(2,1)S(1)}, bf16[48,2560]{1,0:T(8,128)(2,1)S(1)}, u32[]{:S(2)}, u32[]{:S(2)}) %collective-permute-start.6) | collective-permute-done | bytes 245792 | tf_op jit(solution)/shard_map/ppermute | solution.py:39
  140.2 5.6 %collective-permute-start.15 = (bf16[48,1280]{1,0:T(8,128)(2,1)}, bf16[48,1280]{1,0:T(8,128)(2,1)}, u32[]{:S(2)}, u32[]{:S(2)}) collective-permute-start(bf16[48,1280]{1,0:T(8,128)(2,1)} %slice.29), channel_id=1, source_target_pairs={{0,15},{1,0},{2,1},{3,2},{4,3},{5,4},{6,5},{7,6},{8,7},{9,8},{10,9... | collective-permute-start | bytes 368648 | tf_op jit(solution)/shard_map/ppermute | solution.py:45
  149.1 3.8 %fusion.32 = (bf16[16,1,160,768]{3,2,1,0:T(8,128)(2,1)S(1)}, bf16[16,1,160,768]{3,2,1,0:T(8,128)(2,1)S(1)}) fusion(bf16[16,2,160,768]{3,2,1,0:T(8,128)(2,1)} %bitcast.91), kind=kLoop, calls=%fused_computation.83 | loop fusion | bytes 15728640 | tf_op jit(solution)/shard_map/slice | solution.py:72
  161.3 3.1 add_convert_fusion
  176.5 4.8 %gather_fusion = bf16[16,48,2560]{2,1,0:T(8,128)(2,1)} fusion(bf16[16,48,2560]{2,1,0:T(8,128)(2,1)} %bitcast_dynamic-update-slice_fusion, s32[1024]{0:T(1024)S(1)} %pad_clamp_fusion), kind=kCustom, calls=%fused_computation | custom fusion | bytes 7864384 | tf_op jit(solution)/shard_map/jit(_take)/gather | solution.py:49
  188.6 57.7 %reduce-scatter.3.cloned.1.call-done = bf16[192,2560]{1,0:T(8,128)(2,1)} async-done(((bf16[768,2560]{1,0:T(8,128)(2,1)}), bf16[192,2560]{1,0:T(8,128)(2,1)}) %reduce-scatter.3.cloned.1.call-update) | async-done | bytes 983056 | tf_op jit(solution)/shard_map/reduce_scatter | solution.py:130
  246.3 3.7 %fusion.10 = f32[128,768]{1,0:T(8,128)S(1)} fusion(bf16[768,2560]{1,0:T(8,128)(2,1)} %bitcast_select_fusion, bf16[128,2560]{1,0:T(8,128)(2,1)S(1)} %copy-done.8, f32[128]{0:T(128)S(1)} %get-tuple-element.5), kind=kOutput, calls=%fused_computation.30 | convolution fusion | flops 504299520 | bytes 4981248 | tf_op jit(solution)/shard_map/dot_general | solution.py:8
  254.8 7.5 %all-to-all-start.2 = ((bf16[32,5,2560]{2,1,0:T(8,128)(2,1)}), bf16[32,5,2560]{2,1,0:T(8,128)(2,1)}, u32[]{:S(2)}, u32[]{:S(2)}) async-start(bf16[32,5,2560]{2,1,0:T(8,128)(2,1)} %reshape.139), calls=%async_computation.2 | async-start | bytes 2621440 | tf_op jit(solution)/shard_map/all_to_all | solution.py:100
  262.3 3.6 %fusion.15 = f32[128,2560]{1,0:T(8,128)S(1)} fusion(bf16[2560,768]{1,0:T(8,128)(2,1)} %bitcast.84, f32[128,768]{1,0:T(8,128)S(1)} %convolution_bitcast_fusion, f32[128,768]{1,0:T(8,128)S(1)} %fusion.10, f32[128,768]{1,0:T(8,128)S(1)} %copy-done.15), kind=kOutput, calls=%fused_computation.49 | convolution fusion | flops 504299520 | bytes 6422528 | tf_op jit(solution)/shard_map/dot_general | solution.py:8
  267.4 13.0 %all-to-all-done.2 = bf16[32,5,2560]{2,1,0:T(8,128)(2,1)} async-done(((bf16[32,5,2560]{2,1,0:T(8,128)(2,1)}), bf16[32,5,2560]{2,1,0:T(8,128)(2,1)}, u32[]{:S(2)}, u32[]{:S(2)}) %all-to-all-start.2) | async-done | bytes 819232 | tf_op jit(solution)/shard_map/all_to_all | solution.py:100
  283.2 26.2 %reduce-scatter.5.cloned.1.call-done = bf16[48,2560]{1,0:T(8,128)(2,1)} async-done(((bf16[192,2560]{1,0:T(8,128)(2,1)}), bf16[48,2560]{1,0:T(8,128)(2,1)}) %reduce-scatter.5.cloned.1.call-update) | async-done | bytes 245776 | tf_op jit(solution)/shard_map/reduce_scatter | solution.py:131
  (130 shorter events, 74.4 us)
Async XLA Ops:
  7.2 141.9 %all-gather.3.cloned.1.call-start = ((), (), s32[]{:S(2)}) async-start(), calls=%async_computation.7 | async-start | bytes 8355840 | tf_op jit(solution)/shard_map/all_gather | solution.py:69
  9.2 29.3 %collective-permute-start = (bf16[48,2560]{1,0:T(8,128)(2,1)}, bf16[48,2560]{1,0:T(8,128)(2,1)}, u32[]{:S(2)}, u32[]{:S(2)}) collective-permute-start(bf16[48,2560]{1,0:T(8,128)(2,1)} %bitcast.96), channel_id=1, source_target_pairs={{0,15},{1,0},{2,1},{3,2},{4,3},{5,4},{6,5},{7,6},{8,7},{9,8},{10,9... | collective-permute-start | bytes 737288 | tf_op jit(solution)/shard_map/ppermute | solution.py:39
  20.7 23.1 %collective-permute-start.7 = (bf16[48,2560]{1,0:T(8,128)(2,1)}, bf16[48,2560]{1,0:T(8,128)(2,1)}, u32[]{:S(2)}, u32[]{:S(2)}) collective-permute-start(bf16[48,2560]{1,0:T(8,128)(2,1)} %bitcast.97), channel_id=1, source_target_pairs={{0,1},{1,2},{2,3},{3,4},{4,5},{5,6},{6,7},{7,8},{8,9},{9,10},{10,1... | collective-permute-start | bytes 737288 | tf_op jit(solution)/shard_map/ppermute | solution.py:38
  26.6 36.1 %all-to-all-start.1 = ((bf16[32,5,2560]{2,1,0:T(8,128)(2,1)}), bf16[32,5,2560]{2,1,0:T(8,128)(2,1)S(1)}, u32[]{:S(2)}, u32[]{:S(2)}) async-start(bf16[32,5,2560]{2,1,0:T(8,128)(2,1)} %reshape.137), calls=%async_computation.1 | async-start | bytes 2621440 | tf_op jit(solution)/shard_map/all_to_all | solution.py:94
  38.6 16.7 %collective-permute-start.1 = (bf16[48,2560]{1,0:T(8,128)(2,1)}, bf16[48,2560]{1,0:T(8,128)(2,1)S(1)}, u32[]{:S(2)}, u32[]{:S(2)}) collective-permute-start(bf16[48,2560]{1,0:T(8,128)(2,1)} %collective-permute-done), channel_id=1, source_target_pairs={{0,15},{1,0},{2,1},{3,2},{4,3},{5,4},{6,5},{7,6},{8,7},{9,8},{10,9... | collective-permute-start | bytes 737288 | tf_op jit(solution)/shard_map/ppermute | solution.py:39
  43.7 17.1 %collective-permute-start.8 = (bf16[48,2560]{1,0:T(8,128)(2,1)}, bf16[48,2560]{1,0:T(8,128)(2,1)S(1)}, u32[]{:S(2)}, u32[]{:S(2)}) collective-permute-start(bf16[48,2560]{1,0:T(8,128)(2,1)} %collective-permute-done.7), channel_id=1, source_target_pairs={{0,1},{1,2},{2,3},{3,4},{4,5},{5,6},{6,7},{7,8},{8,9},{9,10},{10,1... | collective-permute-start | bytes 737288 | tf_op jit(solution)/shard_map/ppermute | solution.py:38
  55.3 16.6 %collective-permute-start.2 = (bf16[48,2560]{1,0:T(8,128)(2,1)S(1)}, bf16[48,2560]{1,0:T(8,128)(2,1)}, u32[]{:S(2)}, u32[]{:S(2)}) collective-permute-start(bf16[48,2560]{1,0:T(8,128)(2,1)S(1)} %collective-permute-done.1), channel_id=1, source_target_pairs={{0,15},{1,0},{2,1},{3,2},{4,3},{5,4},{6,5},{7,6},{8,7},{9,8},{10,9... | collective-permute-start | bytes 737288 | tf_op jit(solution)/shard_map/ppermute | solution.py:39
  60.8 16.8 %collective-permute-start.9 = (bf16[48,2560]{1,0:T(8,128)(2,1)S(1)}, bf16[48,2560]{1,0:T(8,128)(2,1)S(1)}, u32[]{:S(2)}, u32[]{:S(2)}) collective-permute-start(bf16[48,2560]{1,0:T(8,128)(2,1)S(1)} %collective-permute-done.8), channel_id=1, source_target_pairs={{0,1},{1,2},{2,3},{3,4},{4,5},{5,6},{6,7},{7,8},{8,9},{9,10},{10,1... | collective-permute-start | bytes 737288 | tf_op jit(solution)/shard_map/ppermute | solution.py:38
  62.7 25.6 %all-to-all-start = ((bf16[32,5,2560]{2,1,0:T(8,128)(2,1)}), bf16[32,5,2560]{2,1,0:T(8,128)(2,1)}, u32[]{:S(2)}, u32[]{:S(2)}) async-start(bf16[32,5,2560]{2,1,0:T(8,128)(2,1)} %reshape.135), calls=%async_computation | async-start | bytes 2621440 | tf_op jit(solution)/shard_map/all_to_all | solution.py:95
  70.2 176.1 %reduce-scatter.3.cloned.1.call-start = ((), (), s32[]{:S(2)}) async-start(), calls=%async_computation.5 | async-start | bytes 4915200 | tf_op jit(solution)/shard_map/reduce_scatter | solution.py:130
  71.9 18.0 %collective-permute-start.3 = (bf16[48,2560]{1,0:T(8,128)(2,1)}, bf16[48,2560]{1,0:T(8,128)(2,1)}, u32[]{:S(2)}, u32[]{:S(2)}) collective-permute-start(bf16[48,2560]{1,0:T(8,128)(2,1)} %collective-permute-done.2), channel_id=1, source_target_pairs={{0,15},{1,0},{2,1},{3,2},{4,3},{5,4},{6,5},{7,6},{8,7},{9,8},{10,9... | collective-permute-start | bytes 737288 | tf_op jit(solution)/shard_map/ppermute | solution.py:39
  77.6 75.3 %copy-start.18 = (bf16[48,2560]{1,0:T(8,128)(2,1)}, bf16[48,2560]{1,0:T(8,128)(2,1)S(1)}, u32[]{:S(2)}) copy-start(bf16[48,2560]{1,0:T(8,128)(2,1)S(1)} %collective-permute-done.9) | copy-start | bytes 737284
  77.6 17.4 %collective-permute-start.10 = (bf16[48,2560]{1,0:T(8,128)(2,1)S(1)}, bf16[48,2560]{1,0:T(8,128)(2,1)S(1)}, u32[]{:S(2)}, u32[]{:S(2)}) collective-permute-start(bf16[48,2560]{1,0:T(8,128)(2,1)S(1)} %collective-permute-done.9), channel_id=1, source_target_pairs={{0,1},{1,2},{2,3},{3,4},{4,5},{5,6},{6,7},{7,8},{8,9},{9,10},{10,1... | collective-permute-start | bytes 737288 | tf_op jit(solution)/shard_map/ppermute | solution.py:38
  89.9 16.7 %collective-permute-start.4 = (bf16[48,2560]{1,0:T(8,128)(2,1)}, bf16[48,2560]{1,0:T(8,128)(2,1)S(1)}, u32[]{:S(2)}, u32[]{:S(2)}) collective-permute-start(bf16[48,2560]{1,0:T(8,128)(2,1)} %collective-permute-done.3), channel_id=1, source_target_pairs={{0,15},{1,0},{2,1},{3,2},{4,3},{5,4},{6,5},{7,6},{8,7},{9,8},{10,9... | collective-permute-start | bytes 737288 | tf_op jit(solution)/shard_map/ppermute | solution.py:39
  95.0 17.0 %collective-permute-start.11 = (bf16[48,2560]{1,0:T(8,128)(2,1)S(1)}, bf16[48,2560]{1,0:T(8,128)(2,1)S(1)}, u32[]{:S(2)}, u32[]{:S(2)}) collective-permute-start(bf16[48,2560]{1,0:T(8,128)(2,1)S(1)} %collective-permute-done.10), channel_id=1, source_target_pairs={{0,1},{1,2},{2,3},{3,4},{4,5},{5,6},{6,7},{7,8},{8,9},{9,10},{10,1... | collective-permute-start | bytes 737288 | tf_op jit(solution)/shard_map/ppermute | solution.py:38
  106.6 16.5 %collective-permute-start.5 = (bf16[48,2560]{1,0:T(8,128)(2,1)S(1)}, bf16[48,2560]{1,0:T(8,128)(2,1)S(1)}, u32[]{:S(2)}, u32[]{:S(2)}) collective-permute-start(bf16[48,2560]{1,0:T(8,128)(2,1)S(1)} %collective-permute-done.4), channel_id=1, source_target_pairs={{0,15},{1,0},{2,1},{3,2},{4,3},{5,4},{6,5},{7,6},{8,7},{9,8},{10,9... | collective-permute-start | bytes 737288 | tf_op jit(solution)/shard_map/ppermute | solution.py:39
  112.1 16.6 %collective-permute-start.12 = (bf16[48,2560]{1,0:T(8,128)(2,1)S(1)}, bf16[48,2560]{1,0:T(8,128)(2,1)S(1)}, u32[]{:S(2)}, u32[]{:S(2)}) collective-permute-start(bf16[48,2560]{1,0:T(8,128)(2,1)S(1)} %collective-permute-done.11), channel_id=1, source_target_pairs={{0,1},{1,2},{2,3},{3,4},{4,5},{5,6},{6,7},{7,8},{8,9},{9,10},{10,1... | collective-permute-start | bytes 737288 | tf_op jit(solution)/shard_map/ppermute | solution.py:38
  123.1 16.4 %collective-permute-start.6 = (bf16[48,2560]{1,0:T(8,128)(2,1)S(1)}, bf16[48,2560]{1,0:T(8,128)(2,1)S(1)}, u32[]{:S(2)}, u32[]{:S(2)}) collective-permute-start(bf16[48,2560]{1,0:T(8,128)(2,1)S(1)} %collective-permute-done.5), channel_id=1, source_target_pairs={{0,15},{1,0},{2,1},{3,2},{4,3},{5,4},{6,5},{7,6},{8,7},{9,8},{10,9... | collective-permute-start | bytes 737288 | tf_op jit(solution)/shard_map/ppermute | solution.py:39
  128.7 17.1 %collective-permute-start.13 = (bf16[48,2560]{1,0:T(8,128)(2,1)S(1)}, bf16[48,2560]{1,0:T(8,128)(2,1)S(1)}, u32[]{:S(2)}, u32[]{:S(2)}) collective-permute-start(bf16[48,2560]{1,0:T(8,128)(2,1)S(1)} %collective-permute-done.12), channel_id=1, source_target_pairs={{0,1},{1,2},{2,3},{3,4},{4,5},{5,6},{6,7},{7,8},{8,9},{9,10},{10,1... | collective-permute-start | bytes 737288 | tf_op jit(solution)/shard_map/ppermute | solution.py:38
  140.2 25.8 %collective-permute-start.15 = (bf16[48,1280]{1,0:T(8,128)(2,1)}, bf16[48,1280]{1,0:T(8,128)(2,1)}, u32[]{:S(2)}, u32[]{:S(2)}) collective-permute-start(bf16[48,1280]{1,0:T(8,128)(2,1)} %slice.29), channel_id=1, source_target_pairs={{0,15},{1,0},{2,1},{3,2},{4,3},{5,4},{6,5},{7,6},{8,7},{9,8},{10,9... | collective-permute-start | bytes 368648 | tf_op jit(solution)/shard_map/ppermute | solution.py:45
  147.2 18.8 %collective-permute-start.14 = (bf16[48,1280]{1,0:T(8,128)(2,1)}, bf16[48,1280]{1,0:T(8,128)(2,1)}, u32[]{:S(2)}, u32[]{:S(2)}) collective-permute-start(bf16[48,1280]{1,0:T(8,128)(2,1)} %slice.28), channel_id=1, source_target_pairs={{0,1},{1,2},{2,3},{3,4},{4,5},{5,6},{6,7},{7,8},{8,9},{9,10},{10,1... | collective-permute-start | bytes 368648 | tf_op jit(solution)/shard_map/ppermute | solution.py:44
  164.4 145.0 %reduce-scatter.5.cloned.1.call-start = ((), (), s32[]{:S(2)}) async-start(), calls=%async_computation.6 | async-start | bytes 1228800 | tf_op jit(solution)/shard_map/reduce_scatter | solution.py:131
  188.6 61.4 %copy-start.14 = (f32[160,768]{1,0:T(8,128)S(1)}, f32[160,768]{1,0:T(8,128)}, u32[]{:S(2)}) copy-start(f32[160,768]{1,0:T(8,128)} %get-tuple-element.9) | copy-start | bytes 1474564
  254.8 25.7 %all-to-all-start.2 = ((bf16[32,5,2560]{2,1,0:T(8,128)(2,1)}), bf16[32,5,2560]{2,1,0:T(8,128)(2,1)}, u32[]{:S(2)}, u32[]{:S(2)}) async-start(bf16[32,5,2560]{2,1,0:T(8,128)(2,1)} %reshape.139), calls=%async_computation.2 | async-start | bytes 2621440 | tf_op jit(solution)/shard_map/all_to_all | solution.py:100
  (22 other events, 303.9 us)
Sparse Core Ops, SparseCore 0:
  10.7 136.6 all-gather.2
  164.5 81.7 reduce-scatter.2
  249.7 59.5 reduce-scatter.4

commit v8 on v6

--- a/solution.py
+++ b/solution.py
@@ -87,13 +87,14 @@
         .astype(jnp.bfloat16)
         .reshape(expert_count, capacity, width)
     )
-    hidden_home, grad_home = expert_backward(tokens, q_home, gate_w, up_w, down_w)
     x_there = lax.all_to_all(send_x, "expert", split_axis=0, concat_axis=0, tiled=True)
     q_there = lax.all_to_all(send_q, "expert", split_axis=0, concat_axis=0, tiled=True)
     item_count = x_there.shape[1]
-    hidden_there, grad_there = expert_backward(
-        x_there.reshape(-1, width), q_there.reshape(-1, width), gate_w, up_w, down_w
-    )
+    rows_in = jnp.concatenate([tokens, x_there.reshape(-1, width)], axis=0)
+    q_in = jnp.concatenate([q_home, q_there.reshape(-1, width)], axis=0)
+    hidden_all, grad_all = expert_backward(rows_in, q_in, gate_w, up_w, down_w)
+    grad_home = grad_all[:tok_rows]
+    grad_there = grad_all[tok_rows:]
     returned = lax.all_to_all(
         grad_there.astype(jnp.bfloat16).reshape(expert_count, item_count, width),
         "expert",
@@ -101,24 +102,16 @@
         concat_axis=0,
         tiled=True,
     )
-    returned, hidden_away, q_there = (
-        returned,
-        hidden_there.reshape(expert_count, item_count, -1),
-        q_there,
-    )
     contract = (((0,), (0,)), ((), ()))
     flat_returned = returned.reshape(expert_count * capacity, width)
     grad_away = lax.dot_general(
         placing, flat_returned, contract, preferred_element_type=jnp.float32
     )
     token_grad = (grad_home + grad_away).astype(jnp.bfloat16)
-    flat_hidden = hidden_away.reshape(expert_count * capacity, -1)
-    flat_q = q_there.reshape(expert_count * capacity, width)
     grad_down = lax.psum_scatter(
-        (
-            lax.dot_general(hidden_home, q_home, contract, preferred_element_type=jnp.float32)
-            + lax.dot_general(flat_hidden, flat_q, contract, preferred_element_type=jnp.float32)
-        ).astype(jnp.bfloat16),
+        lax.dot_general(hidden_all, q_in, contract, preferred_element_type=jnp.float32).astype(
+            jnp.bfloat16
+        ),
         "replica",
         scatter_dimension=0,
         tiled=True,

time: 250 us -> 256 us (1.024)
  blocking collectives: 0 us -> 25.7 us
  waiting for transfers between devices: 81 us -> 66.9 us
  starting transfers between devices: 86.7 us -> 79.7 us
  local copies, waits for them, and re-layouts: 36 us -> 41.3 us
  matrix products: 21 us -> 16.5 us
    all_to_all x0 -> x1, blocking collectives: none -> 25.7 us  [local(): lax.all_to_all(grad_there.astype(jnp.bfloat16).reshape(expert_count, item...]
    all_to_all x1 -> x0, waiting for transfers between devices: 12.9 us -> none  [local(): lax.all_to_all(grad_there.astype(jnp.bfloat16).reshape(expert_count, item...]
    ppermute x7, waiting for transfers between devices: 0.07 us -> 11.1 us  [ring_gather(): r = lax.ppermute(r, axis, right)]
    ppermute x7, waiting for transfers between devices: 33.3 us -> 25.2 us  [ring_gather(): l = lax.ppermute(l, axis, left)]
    all_to_all x1, waiting for transfers between devices: 0.01 us -> 6.72 us  [local(): lax.all_to_all(send_x, 'expert', split_axis=0, concat_axis=0, tiled=True)]
    all_to_all x1 -> x0, starting transfers between devices: 6.53 us -> none  [local(): lax.all_to_all(grad_there.astype(jnp.bfloat16).reshape(expert_count, item...]
    dot_general x6 -> x3, matrix products: 11.6 us -> 5.42 us  [against_rows(): lax.dot_general(left, matrix, (((1,), (1,)), ((), ())), preferred_element...]
    all_to_all x1, waiting for transfers between devices: 5.68 us -> 0.01 us  [local(): lax.all_to_all(send_q, 'expert', split_axis=0, concat_axis=0, tiled=True)]
  transfers between devices with their start and end apart: 21 -> 20, of which waited for: 9 -> 9; matrix products, arithmetic and copies ran while one was open for 20% -> 20% of each run, Pallas kernels for 0% -> 0%
where the time goes in v8:
time: 256 us; the launch traced here: 255 us
  starting transfers between devices  79.7 us (31%)
  waiting for transfers between devices  66.9 us (26%)
  local copies, waits for them, and re-layouts  41.3 us (16%)
  blocking collectives  25.7 us (10%)
  matrix products  16.5 us (6%)
  between operations  15.1 us (6%)
  other arithmetic  9.39 us (4%)
    ppermute x7, starting transfers between devices, ring_gather(): l = lax.ppermute(l, axis, left)  43.9 us
    all_to_all x1, blocking collectives, local(): lax.all_to_all(grad_there.astype(jnp.bfloat16).reshape(expert_count, item...  25.7 us
    ppermute x7, waiting for transfers between devices, ring_gather(): l = lax.ppermute(l, axis, left)  25.2 us
    reduce_scatter x1, waiting for transfers between devices, local(): lax.psum_scatter(lax.dot_general(hidden_all, q_in, contract, preferred_el...  22.3 us
    unnamed x41, local copies, waits for them, and re-layouts  21 us
    ppermute x7, starting transfers between devices, ring_gather(): r = lax.ppermute(r, axis, right)  13.4 us
    ppermute x7, waiting for transfers between devices, ring_gather(): r = lax.ppermute(r, axis, right)  11.1 us
    all_to_all x1, starting transfers between devices, local(): lax.all_to_all(send_q, 'expert', split_axis=0, concat_axis=0, tiled=True)  7.6 us
  transfers between devices with their start and end apart: 20, of which 9 were waited for; matrix products, arithmetic and copies ran while one was open for 20% of the time, Pallas kernels for 0%

profile of v8, /device:TPU:6, one launch (start us, length us, event | category | flops | bytes accessed | tf_op | source)
XLA Modules:
  0.0 254.5 jit_solution(1668883318485534148)
XLA Ops:
  9.2 11.4 %collective-permute-start = (bf16[48,2560]{1,0:T(8,128)(2,1)}, bf16[48,2560]{1,0:T(8,128)(2,1)}, u32[]{:S(2)}, u32[]{:S(2)}) collective-permute-start(bf16[48,2560]{1,0:T(8,128)(2,1)} %bitcast.63), channel_id=1, source_target_pairs={{0,15},{1,0},{2,1},{3,2},{4,3},{5,4},{6,5},{7,6},{8,7},{9,8},{10,9... | collective-permute-start | bytes 737288 | tf_op jit(solution)/shard_map/ppermute | solution.py:39
  29.2 7.6 %all-to-all-start = ((bf16[32,5,2560]{2,1,0:T(8,128)(2,1)}), bf16[32,5,2560]{2,1,0:T(8,128)(2,1)S(1)}, u32[]{:S(2)}, u32[]{:S(2)}) async-start(bf16[32,5,2560]{2,1,0:T(8,128)(2,1)} %reshape.95), calls=%async_computation | async-start | bytes 2621440 | tf_op jit(solution)/shard_map/all_to_all | solution.py:91
  42.3 5.1 %collective-permute-start.1 = (bf16[48,2560]{1,0:T(8,128)(2,1)}, bf16[48,2560]{1,0:T(8,128)(2,1)S(1)}, u32[]{:S(2)}, u32[]{:S(2)}) collective-permute-start(bf16[48,2560]{1,0:T(8,128)(2,1)} %collective-permute-done), channel_id=1, source_target_pairs={{0,15},{1,0},{2,1},{3,2},{4,3},{5,4},{6,5},{7,6},{8,7},{9,8},{10,9... | collective-permute-start | bytes 737288 | tf_op jit(solution)/shard_map/ppermute | solution.py:39
  51.1 7.9 %collective-permute-done.1 = bf16[48,2560]{1,0:T(8,128)(2,1)S(1)} collective-permute-done((bf16[48,2560]{1,0:T(8,128)(2,1)}, bf16[48,2560]{1,0:T(8,128)(2,1)S(1)}, u32[]{:S(2)}, u32[]{:S(2)}) %collective-permute-start.1) | collective-permute-done | bytes 245792 | tf_op jit(solution)/shard_map/ppermute | solution.py:39
  59.0 5.5 %collective-permute-start.2 = (bf16[48,2560]{1,0:T(8,128)(2,1)S(1)}, bf16[48,2560]{1,0:T(8,128)(2,1)}, u32[]{:S(2)}, u32[]{:S(2)}) collective-permute-start(bf16[48,2560]{1,0:T(8,128)(2,1)S(1)} %collective-permute-done.1), channel_id=1, source_target_pairs={{0,15},{1,0},{2,1},{3,2},{4,3},{5,4},{6,5},{7,6},{8,7},{9,8},{10,9... | collective-permute-start | bytes 737288 | tf_op jit(solution)/shard_map/ppermute | solution.py:39
  66.5 7.4 %all-to-all-start.1 = ((bf16[32,5,2560]{2,1,0:T(8,128)(2,1)}), bf16[32,5,2560]{2,1,0:T(8,128)(2,1)S(1)}, u32[]{:S(2)}, u32[]{:S(2)}) async-start(bf16[32,5,2560]{2,1,0:T(8,128)(2,1)} %reshape.97), calls=%async_computation.1 | async-start | bytes 2621440 | tf_op jit(solution)/shard_map/all_to_all | solution.py:90
  75.5 5.7 %collective-permute-start.3 = (bf16[48,2560]{1,0:T(8,128)(2,1)}, bf16[48,2560]{1,0:T(8,128)(2,1)}, u32[]{:S(2)}, u32[]{:S(2)}) collective-permute-start(bf16[48,2560]{1,0:T(8,128)(2,1)} %collective-permute-done.2), channel_id=1, source_target_pairs={{0,15},{1,0},{2,1},{3,2},{4,3},{5,4},{6,5},{7,6},{8,7},{9,8},{10,9... | collective-permute-start | bytes 737288 | tf_op jit(solution)/shard_map/ppermute | solution.py:39
  85.2 6.7 %all-to-all-done.1 = bf16[32,5,2560]{2,1,0:T(8,128)(2,1)S(1)} async-done(((bf16[32,5,2560]{2,1,0:T(8,128)(2,1)}), bf16[32,5,2560]{2,1,0:T(8,128)(2,1)S(1)}, u32[]{:S(2)}, u32[]{:S(2)}) %all-to-all-start.1) | async-done | bytes 819232 | tf_op jit(solution)/shard_map/all_to_all | solution.py:90
  93.3 5.1 %collective-permute-start.4 = (bf16[48,2560]{1,0:T(8,128)(2,1)}, bf16[48,2560]{1,0:T(8,128)(2,1)S(1)}, u32[]{:S(2)}, u32[]{:S(2)}) collective-permute-start(bf16[48,2560]{1,0:T(8,128)(2,1)} %collective-permute-done.3), channel_id=1, source_target_pairs={{0,15},{1,0},{2,1},{3,2},{4,3},{5,4},{6,5},{7,6},{8,7},{9,8},{10,9... | collective-permute-start | bytes 737288 | tf_op jit(solution)/shard_map/ppermute | solution.py:39
  102.0 8.0 %collective-permute-done.4 = bf16[48,2560]{1,0:T(8,128)(2,1)S(1)} collective-permute-done((bf16[48,2560]{1,0:T(8,128)(2,1)}, bf16[48,2560]{1,0:T(8,128)(2,1)S(1)}, u32[]{:S(2)}, u32[]{:S(2)}) %collective-permute-start.4) | collective-permute-done | bytes 245792 | tf_op jit(solution)/shard_map/ppermute | solution.py:39
  110.0 5.5 %collective-permute-start.5 = (bf16[48,2560]{1,0:T(8,128)(2,1)S(1)}, bf16[48,2560]{1,0:T(8,128)(2,1)S(1)}, u32[]{:S(2)}, u32[]{:S(2)}) collective-permute-start(bf16[48,2560]{1,0:T(8,128)(2,1)S(1)} %collective-permute-done.4), channel_id=1, source_target_pairs={{0,15},{1,0},{2,1},{3,2},{4,3},{5,4},{6,5},{7,6},{8,7},{9,8},{10,9... | collective-permute-start | bytes 737288 | tf_op jit(solution)/shard_map/ppermute | solution.py:39
  118.1 8.4 %collective-permute-done.5 = bf16[48,2560]{1,0:T(8,128)(2,1)S(1)} collective-permute-done((bf16[48,2560]{1,0:T(8,128)(2,1)S(1)}, bf16[48,2560]{1,0:T(8,128)(2,1)S(1)}, u32[]{:S(2)}, u32[]{:S(2)}) %collective-permute-start.5) | collective-permute-done | bytes 245792 | tf_op jit(solution)/shard_map/ppermute | solution.py:39
  126.5 5.6 %collective-permute-start.6 = (bf16[48,2560]{1,0:T(8,128)(2,1)S(1)}, bf16[48,2560]{1,0:T(8,128)(2,1)S(1)}, u32[]{:S(2)}, u32[]{:S(2)}) collective-permute-start(bf16[48,2560]{1,0:T(8,128)(2,1)S(1)} %collective-permute-done.5), channel_id=1, source_target_pairs={{0,15},{1,0},{2,1},{3,2},{4,3},{5,4},{6,5},{7,6},{8,7},{9,8},{10,9... | collective-permute-start | bytes 737288 | tf_op jit(solution)/shard_map/ppermute | solution.py:39
  134.8 11.0 %collective-permute-done.13 = bf16[48,2560]{1,0:T(8,128)(2,1)S(1)} collective-permute-done((bf16[48,2560]{1,0:T(8,128)(2,1)S(1)}, bf16[48,2560]{1,0:T(8,128)(2,1)S(1)}, u32[]{:S(2)}, u32[]{:S(2)}) %collective-permute-start.13) | collective-permute-done | bytes 245792 | tf_op jit(solution)/shard_map/ppermute | solution.py:38
  147.8 5.3 %collective-permute-start.15 = (bf16[48,1280]{1,0:T(8,128)(2,1)S(1)}, bf16[48,1280]{1,0:T(8,128)(2,1)S(1)}, u32[]{:S(2)}, u32[]{:S(2)}) collective-permute-start(bf16[48,1280]{1,0:T(8,128)(2,1)S(1)} %slice.38), channel_id=1, source_target_pairs={{0,15},{1,0},{2,1},{3,2},{4,3},{5,4},{6,5},{7,6},{8,7},{9,8},{10,9... | collective-permute-start | bytes 368648 | tf_op jit(solution)/shard_map/ppermute | solution.py:45
  156.0 3.9 %fusion.26 = (bf16[16,1,160,768]{3,2,1,0:T(8,128)(2,1)S(1)}, bf16[16,1,160,768]{3,2,1,0:T(8,128)(2,1)S(1)}) fusion(bf16[16,2,160,768]{3,2,1,0:T(8,128)(2,1)} %bitcast.60), kind=kLoop, calls=%fused_computation.75 | loop fusion | bytes 15728640 | tf_op jit(solution)/shard_map/slice | solution.py:69
  165.3 4.2 %convolution_convert_fusion = bf16[768,2560]{1,0:T(8,128)(2,1)} fusion(bf16[160,2560]{1,0:T(8,128)(2,1)S(1)} %reshape.96, bf16[128,2560]{1,0:T(8,128)(2,1)S(1)} %copy-done.7, f32[288,768]{1,0:T(8,128)S(1)} %fusion.27, f32[288,768]{1,0:T(8,128)S(1)} %fusion.28), kind=kOutput, calls=%fused_computation.1 | convolution fusion | flops 1138704384 | bytes 7176192 | tf_op jit(solution)/shard_map/dot_general | solution.py:112
  177.3 4.8 %gather_fusion = bf16[16,48,2560]{2,1,0:T(8,128)(2,1)} fusion(bf16[16,48,2560]{2,1,0:T(8,128)(2,1)} %bitcast_dynamic-update-slice_fusion, s32[1024]{0:T(1024)S(1)} %pad_clamp_fusion), kind=kCustom, calls=%fused_computation | custom fusion | bytes 7864384 | tf_op jit(solution)/shard_map/jit(_take)/gather | solution.py:49
  182.1 2.6 %bitcast_select_fusion = bf16[768,2560]{1,0:T(8,128)(2,1)S(1)} fusion(bf16[16,48,2560]{2,1,0:T(8,128)(2,1)} %gather_fusion, pred[768]{0:T(1024)(128)(4,1)S(1)} %broadcast_in_dim.29), kind=kLoop, calls=%fused_computation.3 | loop fusion | flops 1966080 | bytes 7865088 | tf_op jit(solution)/shard_map/jit(_take)/select_n | solution.py:49
  189.2 2.6 %convolution_add_fusion = f32[288,2560]{1,0:T(8,128)S(1)} fusion(f32[288,2560]{1,0:T(8,128)S(1)} %fusion.7, bf16[2560,768]{1,0:T(8,128)(2,1)S(1)} %bitcast.59, f32[288,768]{1,0:T(8,128)S(1)} %fusion.3, f32[288,768]{1,0:T(8,128)} %copy-done.4), kind=kOutput, calls=%fused_computation.2 | convolution fusion | flops 1134526464 | bytes 11599872 | tf_op jit(solution)/shard_map/dot_general | solution.py:8
  192.7 2.3 reshape.99
  195.0 25.7 %all_to_all.15 = bf16[32,5,2560]{2,1,0:T(8,128)(2,1)} all-to-all(bf16[32,5,2560]{2,1,0:T(8,128)(2,1)} %reshape.99), channel_id=1, replica_groups=mesh['expert'=32,'replica'=16] {'expert'}, dimensions={0} | all-to-all | bytes 1638400 | tf_op jit(solution)/shard_map/all_to_all | solution.py:98
  223.0 2.4 fusion
  225.4 22.3 %reduce-scatter.2.cloned.1.call-done = bf16[48,2560]{1,0:T(8,128)(2,1)} async-done(((bf16[768,2560]{1,0:T(8,128)(2,1)}), bf16[48,2560]{1,0:T(8,128)(2,1)}) %reduce-scatter.2.cloned.1.call-update) | async-done | bytes 245776 | tf_op jit(solution)/shard_map/reduce_scatter | solution.py:111
  (97 shorter events, 62.5 us)
Async XLA Ops:
  7.2 29.6 %copy-start.5 = (bf16[128,2560]{1,0:T(8,128)(2,1)S(1)}, bf16[128,2560]{1,0:T(8,128)(2,1)}, u32[]{:S(2)}) copy-start(bf16[128,2560]{1,0:T(8,128)(2,1)} %param.8) | copy-start | bytes 1966084
  7.2 148.8 %all-gather.3.cloned.1.call-start = ((), (), s32[]{:S(2)}) async-start(), calls=%async_computation.5 | async-start | bytes 8355840 | tf_op jit(solution)/shard_map/all_gather | solution.py:66
  9.2 33.1 %collective-permute-start = (bf16[48,2560]{1,0:T(8,128)(2,1)}, bf16[48,2560]{1,0:T(8,128)(2,1)}, u32[]{:S(2)}, u32[]{:S(2)}) collective-permute-start(bf16[48,2560]{1,0:T(8,128)(2,1)} %bitcast.63), channel_id=1, source_target_pairs={{0,15},{1,0},{2,1},{3,2},{4,3},{5,4},{6,5},{7,6},{8,7},{9,8},{10,9... | collective-permute-start | bytes 737288 | tf_op jit(solution)/shard_map/ppermute | solution.py:39
  20.6 26.8 %collective-permute-start.7 = (bf16[48,2560]{1,0:T(8,128)(2,1)}, bf16[48,2560]{1,0:T(8,128)(2,1)}, u32[]{:S(2)}, u32[]{:S(2)}) collective-permute-start(bf16[48,2560]{1,0:T(8,128)(2,1)} %bitcast.64), channel_id=1, source_target_pairs={{0,1},{1,2},{2,3},{3,4},{4,5},{5,6},{6,7},{7,8},{8,9},{9,10},{10,1... | collective-permute-start | bytes 737288 | tf_op jit(solution)/shard_map/ppermute | solution.py:38
  27.9 11.9 %copy-start.6 = (bf16[128,2560]{1,0:T(8,128)(2,1)S(1)}, bf16[128,2560]{1,0:T(8,128)(2,1)}, u32[]{:S(2)}) copy-start(bf16[128,2560]{1,0:T(8,128)(2,1)} %param.9) | copy-start | bytes 1966084
  29.2 37.3 %all-to-all-start = ((bf16[32,5,2560]{2,1,0:T(8,128)(2,1)}), bf16[32,5,2560]{2,1,0:T(8,128)(2,1)S(1)}, u32[]{:S(2)}, u32[]{:S(2)}) async-start(bf16[32,5,2560]{2,1,0:T(8,128)(2,1)} %reshape.95), calls=%async_computation | async-start | bytes 2621440 | tf_op jit(solution)/shard_map/all_to_all | solution.py:91
  42.3 16.7 %collective-permute-start.1 = (bf16[48,2560]{1,0:T(8,128)(2,1)}, bf16[48,2560]{1,0:T(8,128)(2,1)S(1)}, u32[]{:S(2)}, u32[]{:S(2)}) collective-permute-start(bf16[48,2560]{1,0:T(8,128)(2,1)} %collective-permute-done), channel_id=1, source_target_pairs={{0,15},{1,0},{2,1},{3,2},{4,3},{5,4},{6,5},{7,6},{8,7},{9,8},{10,9... | collective-permute-start | bytes 737288 | tf_op jit(solution)/shard_map/ppermute | solution.py:39
  47.5 17.1 %collective-permute-start.8 = (bf16[48,2560]{1,0:T(8,128)(2,1)}, bf16[48,2560]{1,0:T(8,128)(2,1)S(1)}, u32[]{:S(2)}, u32[]{:S(2)}) collective-permute-start(bf16[48,2560]{1,0:T(8,128)(2,1)} %collective-permute-done.7), channel_id=1, source_target_pairs={{0,1},{1,2},{2,3},{3,4},{4,5},{5,6},{6,7},{7,8},{8,9},{9,10},{10,1... | collective-permute-start | bytes 737288 | tf_op jit(solution)/shard_map/ppermute | solution.py:38
  59.0 16.5 %collective-permute-start.2 = (bf16[48,2560]{1,0:T(8,128)(2,1)S(1)}, bf16[48,2560]{1,0:T(8,128)(2,1)}, u32[]{:S(2)}, u32[]{:S(2)}) collective-permute-start(bf16[48,2560]{1,0:T(8,128)(2,1)S(1)} %collective-permute-done.1), channel_id=1, source_target_pairs={{0,15},{1,0},{2,1},{3,2},{4,3},{5,4},{6,5},{7,6},{8,7},{9,8},{10,9... | collective-permute-start | bytes 737288 | tf_op jit(solution)/shard_map/ppermute | solution.py:39
  64.5 18.7 %copy-start.9 = (bf16[48,2560]{1,0:T(8,128)(2,1)}, bf16[48,2560]{1,0:T(8,128)(2,1)S(1)}, u32[]{:S(2)}) copy-start(bf16[48,2560]{1,0:T(8,128)(2,1)S(1)} %collective-permute-done.8) | copy-start | bytes 737284
  64.5 16.8 %collective-permute-start.9 = (bf16[48,2560]{1,0:T(8,128)(2,1)S(1)}, bf16[48,2560]{1,0:T(8,128)(2,1)}, u32[]{:S(2)}, u32[]{:S(2)}) collective-permute-start(bf16[48,2560]{1,0:T(8,128)(2,1)S(1)} %collective-permute-done.8), channel_id=1, source_target_pairs={{0,1},{1,2},{2,3},{3,4},{4,5},{5,6},{6,7},{7,8},{8,9},{9,10},{10,1... | collective-permute-start | bytes 737288 | tf_op jit(solution)/shard_map/ppermute | solution.py:38
  66.5 25.5 %all-to-all-start.1 = ((bf16[32,5,2560]{2,1,0:T(8,128)(2,1)}), bf16[32,5,2560]{2,1,0:T(8,128)(2,1)S(1)}, u32[]{:S(2)}, u32[]{:S(2)}) async-start(bf16[32,5,2560]{2,1,0:T(8,128)(2,1)} %reshape.97), calls=%async_computation.1 | async-start | bytes 2621440 | tf_op jit(solution)/shard_map/all_to_all | solution.py:90
  73.9 173.8 %reduce-scatter.2.cloned.1.call-start = ((), (), s32[]{:S(2)}) async-start(), calls=%async_computation.4 | async-start | bytes 4177920 | tf_op jit(solution)/shard_map/reduce_scatter | solution.py:111
  75.5 17.8 %collective-permute-start.3 = (bf16[48,2560]{1,0:T(8,128)(2,1)}, bf16[48,2560]{1,0:T(8,128)(2,1)}, u32[]{:S(2)}, u32[]{:S(2)}) collective-permute-start(bf16[48,2560]{1,0:T(8,128)(2,1)} %collective-permute-done.2), channel_id=1, source_target_pairs={{0,15},{1,0},{2,1},{3,2},{4,3},{5,4},{6,5},{7,6},{8,7},{9,8},{10,9... | collective-permute-start | bytes 737288 | tf_op jit(solution)/shard_map/ppermute | solution.py:39
  81.3 17.1 %collective-permute-start.10 = (bf16[48,2560]{1,0:T(8,128)(2,1)}, bf16[48,2560]{1,0:T(8,128)(2,1)}, u32[]{:S(2)}, u32[]{:S(2)}) collective-permute-start(bf16[48,2560]{1,0:T(8,128)(2,1)} %collective-permute-done.9), channel_id=1, source_target_pairs={{0,1},{1,2},{2,3},{3,4},{4,5},{5,6},{6,7},{7,8},{8,9},{9,10},{10,1... | collective-permute-start | bytes 737288 | tf_op jit(solution)/shard_map/ppermute | solution.py:38
  93.3 16.7 %collective-permute-start.4 = (bf16[48,2560]{1,0:T(8,128)(2,1)}, bf16[48,2560]{1,0:T(8,128)(2,1)S(1)}, u32[]{:S(2)}, u32[]{:S(2)}) collective-permute-start(bf16[48,2560]{1,0:T(8,128)(2,1)} %collective-permute-done.3), channel_id=1, source_target_pairs={{0,15},{1,0},{2,1},{3,2},{4,3},{5,4},{6,5},{7,6},{8,7},{9,8},{10,9... | collective-permute-start | bytes 737288 | tf_op jit(solution)/shard_map/ppermute | solution.py:39
  98.4 17.0 %collective-permute-start.11 = (bf16[48,2560]{1,0:T(8,128)(2,1)}, bf16[48,2560]{1,0:T(8,128)(2,1)S(1)}, u32[]{:S(2)}, u32[]{:S(2)}) collective-permute-start(bf16[48,2560]{1,0:T(8,128)(2,1)} %collective-permute-done.10), channel_id=1, source_target_pairs={{0,1},{1,2},{2,3},{3,4},{4,5},{5,6},{6,7},{7,8},{8,9},{9,10},{10,1... | collective-permute-start | bytes 737288 | tf_op jit(solution)/shard_map/ppermute | solution.py:38
  110.0 16.5 %collective-permute-start.5 = (bf16[48,2560]{1,0:T(8,128)(2,1)S(1)}, bf16[48,2560]{1,0:T(8,128)(2,1)S(1)}, u32[]{:S(2)}, u32[]{:S(2)}) collective-permute-start(bf16[48,2560]{1,0:T(8,128)(2,1)S(1)} %collective-permute-done.4), channel_id=1, source_target_pairs={{0,15},{1,0},{2,1},{3,2},{4,3},{5,4},{6,5},{7,6},{8,7},{9,8},{10,9... | collective-permute-start | bytes 737288 | tf_op jit(solution)/shard_map/ppermute | solution.py:39
  115.5 16.6 %collective-permute-start.12 = (bf16[48,2560]{1,0:T(8,128)(2,1)S(1)}, bf16[48,2560]{1,0:T(8,128)(2,1)S(1)}, u32[]{:S(2)}, u32[]{:S(2)}) collective-permute-start(bf16[48,2560]{1,0:T(8,128)(2,1)S(1)} %collective-permute-done.11), channel_id=1, source_target_pairs={{0,1},{1,2},{2,3},{3,4},{4,5},{5,6},{6,7},{7,8},{8,9},{9,10},{10,1... | collective-permute-start | bytes 737288 | tf_op jit(solution)/shard_map/ppermute | solution.py:38
  126.5 21.2 %collective-permute-start.6 = (bf16[48,2560]{1,0:T(8,128)(2,1)S(1)}, bf16[48,2560]{1,0:T(8,128)(2,1)S(1)}, u32[]{:S(2)}, u32[]{:S(2)}) collective-permute-start(bf16[48,2560]{1,0:T(8,128)(2,1)S(1)} %collective-permute-done.5), channel_id=1, source_target_pairs={{0,15},{1,0},{2,1},{3,2},{4,3},{5,4},{6,5},{7,6},{8,7},{9,8},{10,9... | collective-permute-start | bytes 737288 | tf_op jit(solution)/shard_map/ppermute | solution.py:39
  132.1 13.7 %collective-permute-start.13 = (bf16[48,2560]{1,0:T(8,128)(2,1)S(1)}, bf16[48,2560]{1,0:T(8,128)(2,1)S(1)}, u32[]{:S(2)}, u32[]{:S(2)}) collective-permute-start(bf16[48,2560]{1,0:T(8,128)(2,1)S(1)} %collective-permute-done.12), channel_id=1, source_target_pairs={{0,1},{1,2},{2,3},{3,4},{4,5},{5,6},{6,7},{7,8},{8,9},{9,10},{10,1... | collective-permute-start | bytes 737288 | tf_op jit(solution)/shard_map/ppermute | solution.py:38
  145.8 8.0 %collective-permute-start.14 = (bf16[48,1280]{1,0:T(8,128)(2,1)S(1)}, bf16[48,1280]{1,0:T(8,128)(2,1)S(1)}, u32[]{:S(2)}, u32[]{:S(2)}) collective-permute-start(bf16[48,1280]{1,0:T(8,128)(2,1)S(1)} %slice.37), channel_id=1, source_target_pairs={{0,1},{1,2},{2,3},{3,4},{4,5},{5,6},{6,7},{7,8},{8,9},{9,10},{10,1... | collective-permute-start | bytes 368648 | tf_op jit(solution)/shard_map/ppermute | solution.py:44
  147.8 7.6 %collective-permute-start.15 = (bf16[48,1280]{1,0:T(8,128)(2,1)S(1)}, bf16[48,1280]{1,0:T(8,128)(2,1)S(1)}, u32[]{:S(2)}, u32[]{:S(2)}) collective-permute-start(bf16[48,1280]{1,0:T(8,128)(2,1)S(1)} %slice.38), channel_id=1, source_target_pairs={{0,15},{1,0},{2,1},{3,2},{4,3},{5,4},{6,5},{7,6},{8,7},{9,8},{10,9... | collective-permute-start | bytes 368648 | tf_op jit(solution)/shard_map/ppermute | solution.py:45
  161.8 24.2 %copy-start.4 = (f32[288,768]{1,0:T(8,128)}, f32[288,768]{1,0:T(8,128)S(1)}, u32[]{:S(2)}) copy-start(f32[288,768]{1,0:T(8,128)S(1)} %fusion.28) | copy-start | bytes 2654212
  (9 other events, 24.1 us)
Sparse Core Ops, SparseCore 0:
  10.1 135.1 all-gather.2
  169.6 78.0 reduce-scatter.1

commit v9 on v6

--- a/solution.py
+++ b/solution.py
@@ -63,11 +63,18 @@
     upstream = cotangent.astype(jnp.float32)
     q_home = (upstream * share_home[:, None]).astype(jnp.bfloat16)
     q_away = (upstream * share_away[:, None]).astype(jnp.bfloat16)
-    pair = lax.all_gather(jnp.stack([w_gate[0], w_up[0]]), "replica", axis=0, tiled=False)
-    down_full = ring_gather(w_down[0], "replica")
-    gate_w = pair[:, 0].reshape(-1, w_gate.shape[2])
-    up_w = pair[:, 1].reshape(-1, w_up.shape[2])
-    down_w = down_full.reshape(-1, down_full.shape[2])
+    shard_rows, hidden_units = w_gate.shape[1], w_gate.shape[2]
+    down_rows, width_down = w_down.shape[1], w_down.shape[2]
+    cut = width_down // 2
+    packed = jnp.concatenate(
+        [w_gate[0], w_up[0], w_down[0, :, :cut].reshape(-1, hidden_units)], axis=0
+    )
+    full = lax.all_gather(packed, "replica", axis=0, tiled=False)
+    down_second = ring_gather(w_down[0, :, cut:], "replica")
+    gate_w = full[:, :shard_rows].reshape(-1, hidden_units)
+    up_w = full[:, shard_rows : 2 * shard_rows].reshape(-1, hidden_units)
+    down_first = full[:, 2 * shard_rows :].reshape(-1, down_rows, cut)
+    down_w = jnp.concatenate([down_first, down_second], axis=2).reshape(-1, width_down)
     target = partner[:, 0]
     onehot_rows = (target[:, None] == jnp.arange(expert_count, dtype=jnp.int32)[None, :]).astype(
         jnp.int32

time: 250 us -> 250 us (level)
  other arithmetic: 8.11 us -> 4.75 us
  matrix products: 21 us -> 23.7 us
    all_gather x1, waiting for transfers between devices: 0.01 us -> 52.8 us  [local(): full = lax.all_gather(packed, 'replica', axis=0, tiled=False)]
    ppermute x7, waiting for transfers between devices: 33.3 us -> 9.17 us  [ring_gather(): l = lax.ppermute(l, axis, left)]
    reduce_scatter x1, waiting for transfers between devices: 23.9 us -> 1.3 us  [local(): lax.psum_scatter((lax.dot_general(hidden_home, q_home, contract, preferre...]
    all_to_all x1, waiting for transfers between devices: 5.68 us -> 0.01 us  [local(): lax.all_to_all(send_q, 'expert', split_axis=0, concat_axis=0, tiled=True)]
    ppermute x1, waiting for transfers between devices: 5.16 us -> 0.58 us  [ring_gather(): rh = lax.ppermute(r[..., :cut], axis, right)]
    ppermute x7, waiting for transfers between devices: 0.07 us -> 4.11 us  [ring_gather(): r = lax.ppermute(r, axis, right)]
    dot_general x6, matrix products: 11.6 us -> 14.3 us  [against_rows(): lax.dot_general(left, matrix, (((1,), (1,)), ((), ())), preferred_element...]
    concatenate x0 -> x1, local copies, waits for them, and re-layouts: none -> 2.65 us  [local(): jnp.concatenate([down_first, down_second], axis=2).reshape(-1, width_down)]
  transfers between devices with their start and end apart: 21 -> 21, of which waited for: 9 -> 9; matrix products, arithmetic and copies ran while one was open for 20% -> 24% of each run, Pallas kernels for 0% -> 0%
where the time goes in v9:
time: 250 us; the launch traced here: 248 us
  starting transfers between devices  85.7 us (34%)
  waiting for transfers between devices  80.3 us (32%)
  local copies, waits for them, and re-layouts  37.8 us (15%)
  matrix products  23.7 us (9%)
  between operations  15.4 us (6%)
  other arithmetic  4.75 us (2%)
    all_gather x1, waiting for transfers between devices, local(): full = lax.all_gather(packed, 'replica', axis=0, tiled=False)  52.8 us
    ppermute x7, starting transfers between devices, ring_gather(): l = lax.ppermute(l, axis, left)  41.8 us
    unnamed x63, local copies, waits for them, and re-layouts  16.9 us
    dot_general x6, matrix products, against_rows(): lax.dot_general(left, matrix, (((1,), (1,)), ((), ())), preferred_element...  14.3 us
    ppermute x7, starting transfers between devices, ring_gather(): r = lax.ppermute(r, axis, right)  14.1 us
    all_to_all x1, waiting for transfers between devices, local(): lax.all_to_all(grad_there.astype(jnp.bfloat16).reshape(expert_count, item...  10.8 us
    ppermute x7, waiting for transfers between devices, ring_gather(): l = lax.ppermute(l, axis, left)  9.17 us
    all_to_all x1, starting transfers between devices, local(): lax.all_to_all(send_q, 'expert', split_axis=0, concat_axis=0, tiled=True)  7.62 us
  transfers between devices with their start and end apart: 21, of which 9 were waited for; matrix products, arithmetic and copies ran while one was open for 24% of the time, Pallas kernels for 0%

profile of v9, /device:TPU:6, one launch (start us, length us, event | category | flops | bytes accessed | tf_op | source)
XLA Modules:
  0.0 247.5 jit_solution(9395931865382826282)
XLA Ops:
  11.1 11.4 %collective-permute-start = (bf16[48,1280]{1,0:T(8,128)(2,1)S(1)}, bf16[48,1280]{1,0:T(8,128)(2,1)S(1)}, u32[]{:S(2)}, u32[]{:S(2)}) collective-permute-start(bf16[48,1280]{1,0:T(8,128)(2,1)S(1)} %get-tuple-element.4), channel_id=1, source_target_pairs={{0,15},{1,0},{2,1},{3,2},{4,3},{5,4},{6,5},{7,6},{8,7},{9,8},{10,9... | collective-permute-start | bytes 368648 | tf_op jit(solution)/shard_map/ppermute | solution.py:39
  27.3 7.6 %all-to-all-start = ((bf16[32,5,2560]{2,1,0:T(8,128)(2,1)}), bf16[32,5,2560]{2,1,0:T(8,128)(2,1)S(1)}, u32[]{:S(2)}, u32[]{:S(2)}) async-start(bf16[32,5,2560]{2,1,0:T(8,128)(2,1)} %reshape.108), calls=%async_computation | async-start | bytes 2621440 | tf_op jit(solution)/shard_map/all_to_all | solution.py:99
  36.8 5.1 %collective-permute-start.1 = (bf16[48,1280]{1,0:T(8,128)(2,1)S(1)}, bf16[48,1280]{1,0:T(8,128)(2,1)S(1)}, u32[]{:S(2)}, u32[]{:S(2)}) collective-permute-start(bf16[48,1280]{1,0:T(8,128)(2,1)S(1)} %collective-permute-done), channel_id=1, source_target_pairs={{0,15},{1,0},{2,1},{3,2},{4,3},{5,4},{6,5},{7,6},{8,7},{9,8},{10,9... | collective-permute-start | bytes 368648 | tf_op jit(solution)/shard_map/ppermute | solution.py:39
  44.5 3.4 %collective-permute-done.1 = bf16[48,1280]{1,0:T(8,128)(2,1)S(1)} collective-permute-done((bf16[48,1280]{1,0:T(8,128)(2,1)S(1)}, bf16[48,1280]{1,0:T(8,128)(2,1)S(1)}, u32[]{:S(2)}, u32[]{:S(2)}) %collective-permute-start.1) | collective-permute-done | bytes 122912 | tf_op jit(solution)/shard_map/ppermute | solution.py:39
  47.9 5.6 %collective-permute-start.2 = (bf16[48,1280]{1,0:T(8,128)(2,1)S(1)}, bf16[48,1280]{1,0:T(8,128)(2,1)}, u32[]{:S(2)}, u32[]{:S(2)}) collective-permute-start(bf16[48,1280]{1,0:T(8,128)(2,1)S(1)} %collective-permute-done.1), channel_id=1, source_target_pairs={{0,15},{1,0},{2,1},{3,2},{4,3},{5,4},{6,5},{7,6},{8,7},{9,8},{10,9... | collective-permute-start | bytes 368648 | tf_op jit(solution)/shard_map/ppermute | solution.py:39
  56.1 3.1 %collective-permute-done.2 = bf16[48,1280]{1,0:T(8,128)(2,1)} collective-permute-done((bf16[48,1280]{1,0:T(8,128)(2,1)S(1)}, bf16[48,1280]{1,0:T(8,128)(2,1)}, u32[]{:S(2)}, u32[]{:S(2)}) %collective-permute-start.2) | collective-permute-done | bytes 122912 | tf_op jit(solution)/shard_map/ppermute | solution.py:39
  59.2 5.7 %collective-permute-start.3 = (bf16[48,1280]{1,0:T(8,128)(2,1)}, bf16[48,1280]{1,0:T(8,128)(2,1)}, u32[]{:S(2)}, u32[]{:S(2)}) collective-permute-start(bf16[48,1280]{1,0:T(8,128)(2,1)} %collective-permute-done.2), channel_id=1, source_target_pairs={{0,15},{1,0},{2,1},{3,2},{4,3},{5,4},{6,5},{7,6},{8,7},{9,8},{10,9... | collective-permute-start | bytes 368648 | tf_op jit(solution)/shard_map/ppermute | solution.py:39
  66.9 7.4 %all-to-all-start.1 = ((bf16[32,5,2560]{2,1,0:T(8,128)(2,1)}), bf16[32,5,2560]{2,1,0:T(8,128)(2,1)S(1)}, u32[]{:S(2)}, u32[]{:S(2)}) async-start(bf16[32,5,2560]{2,1,0:T(8,128)(2,1)} %reshape.110), calls=%async_computation.1 | async-start | bytes 2621440 | tf_op jit(solution)/shard_map/all_to_all | solution.py:98
  75.9 5.1 %collective-permute-start.4 = (bf16[48,1280]{1,0:T(8,128)(2,1)}, bf16[48,1280]{1,0:T(8,128)(2,1)}, u32[]{:S(2)}, u32[]{:S(2)}) collective-permute-start(bf16[48,1280]{1,0:T(8,128)(2,1)} %collective-permute-done.3), channel_id=1, source_target_pairs={{0,15},{1,0},{2,1},{3,2},{4,3},{5,4},{6,5},{7,6},{8,7},{9,8},{10,9... | collective-permute-start | bytes 368648 | tf_op jit(solution)/shard_map/ppermute | solution.py:39
  84.6 2.7 %collective-permute-done.4 = bf16[48,1280]{1,0:T(8,128)(2,1)} collective-permute-done((bf16[48,1280]{1,0:T(8,128)(2,1)}, bf16[48,1280]{1,0:T(8,128)(2,1)}, u32[]{:S(2)}, u32[]{:S(2)}) %collective-permute-start.4) | collective-permute-done | bytes 122912 | tf_op jit(solution)/shard_map/ppermute | solution.py:39
  87.3 5.6 %collective-permute-start.5 = (bf16[48,1280]{1,0:T(8,128)(2,1)}, bf16[48,1280]{1,0:T(8,128)(2,1)}, u32[]{:S(2)}, u32[]{:S(2)}) collective-permute-start(bf16[48,1280]{1,0:T(8,128)(2,1)} %collective-permute-done.4), channel_id=1, source_target_pairs={{0,15},{1,0},{2,1},{3,2},{4,3},{5,4},{6,5},{7,6},{8,7},{9,8},{10,9... | collective-permute-start | bytes 368648 | tf_op jit(solution)/shard_map/ppermute | solution.py:39
  96.3 52.8 %all-gather.3.cloned.1.call-done = bf16[6400,768]{1,0:T(8,128)(2,1)} async-done(((bf16[400,768]{1,0:T(8,128)(2,1)}), bf16[6400,768]{1,0:T(8,128)(2,1)}) %all-gather.3.cloned.1.call-update) | async-done | bytes 9830416 | tf_op jit(solution)/shard_map/all_gather | solution.py:72
  149.1 3.8 %fusion.39 = (bf16[16,160,768]{2,1,0:T(8,128)(2,1)S(1)}, bf16[16,160,768]{2,1,0:T(8,128)(2,1)S(1)}) fusion(bf16[16,400,768]{2,1,0:T(8,128)(2,1)} %bitcast.80), kind=kLoop, calls=%fused_computation.89 | loop fusion | bytes 15728640 | tf_op jit(solution)/shard_map/slice | solution.py:75
  158.6 3.1 %add_convert_fusion = bf16[768,2560]{1,0:T(8,128)(2,1)} fusion(f32[768,2560]{1,0:T(8,128)S(1)} %fusion.10, bf16[160,2560]{1,0:T(8,128)(2,1)S(1)} %copy-done.11, f32[160,768]{1,0:T(8,128)S(1)} %fusion.40, f32[160,768]{1,0:T(8,128)S(1)} %fusion.41), kind=kOutput, calls=%fused_computation.1 | convolution fusion | flops 633815040 | bytes 13598720 | tf_op jit(solution)/shard_map/dot_general | solution.py:127
  163.4 3.3 %collective-permute-start.6 = (bf16[48,1280]{1,0:T(8,128)(2,1)}, bf16[48,1280]{1,0:T(8,128)(2,1)S(1)}, u32[]{:S(2)}, u32[]{:S(2)}) collective-permute-start(bf16[48,1280]{1,0:T(8,128)(2,1)} %collective-permute-done.5), channel_id=1, source_target_pairs={{0,15},{1,0},{2,1},{3,2},{4,3},{5,4},{6,5},{7,6},{8,7},{9,8},{10,9... | collective-permute-start | bytes 368648 | tf_op jit(solution)/shard_map/ppermute | solution.py:39
  166.7 2.6 %collective-permute-start.13 = (bf16[48,1280]{1,0:T(8,128)(2,1)}, bf16[48,1280]{1,0:T(8,128)(2,1)S(1)}, u32[]{:S(2)}, u32[]{:S(2)}) collective-permute-start(bf16[48,1280]{1,0:T(8,128)(2,1)} %collective-permute-done.12), channel_id=1, source_target_pairs={{0,1},{1,2},{2,3},{3,4},{4,5},{5,6},{6,7},{7,8},{8,9},{9,10},{10,1... | collective-permute-start | bytes 368648 | tf_op jit(solution)/shard_map/ppermute | solution.py:38
  170.8 4.0 %collective-permute-done.13 = bf16[48,1280]{1,0:T(8,128)(2,1)S(1)} collective-permute-done((bf16[48,1280]{1,0:T(8,128)(2,1)}, bf16[48,1280]{1,0:T(8,128)(2,1)S(1)}, u32[]{:S(2)}, u32[]{:S(2)}) %collective-permute-start.13) | collective-permute-done | bytes 122912 | tf_op jit(solution)/shard_map/ppermute | solution.py:38
  176.8 5.3 %collective-permute-start.15 = (bf16[48,640]{1,0:T(8,128)(2,1)S(1)}, bf16[48,640]{1,0:T(8,128)(2,1)S(1)}, u32[]{:S(2)}, u32[]{:S(2)}) collective-permute-start(bf16[48,640]{1,0:T(8,128)(2,1)S(1)} %slice.42), channel_id=1, source_target_pairs={{0,15},{1,0},{2,1},{3,2},{4,3},{5,4},{6,5},{7,6},{8,7},{9,8},{10,9... | collective-permute-start | bytes 184328 | tf_op jit(solution)/shard_map/ppermute | solution.py:45
  197.6 2.6 %concatenate.13 = bf16[768,1280]{1,0:T(8,128)(2,1)} reshape(bf16[16,80,768]{2,1,0:T(8,128)(2,1)S(1)} %slice.40) | data formatting | bytes 3932160 | tf_op jit(solution)/shard_map/concatenate | solution.py:77
  200.2 4.0 %fusion.2 = f32[160,768]{1,0:T(8,128)S(1)} fusion(bf16[160,2560]{1,0:T(8,128)(2,1)} %reshape.109, bf16[768,1280]{1,0:T(8,128)(2,1)} %bitcast_select_fusion, bf16[768,1280]{1,0:T(8,128)(2,1)} %concatenate.13), kind=kOutput, calls=%fused_computation.10 | convolution fusion | flops 637009920 | bytes 5242880 | tf_op jit(solution)/shard_map/dot_general | solution.py:8
  206.4 2.3 fusion
  211.0 7.5 %all-to-all-start.2 = ((bf16[32,5,2560]{2,1,0:T(8,128)(2,1)}), bf16[32,5,2560]{2,1,0:T(8,128)(2,1)}, u32[]{:S(2)}, u32[]{:S(2)}) async-start(bf16[32,5,2560]{2,1,0:T(8,128)(2,1)} %reshape.112), calls=%async_computation.2 | async-start | bytes 2621440 | tf_op jit(solution)/shard_map/all_to_all | solution.py:104
  218.6 3.7 %fusion.3 = f32[128,768]{1,0:T(8,128)S(1)} fusion(bf16[768,1280]{1,0:T(8,128)(2,1)} %bitcast_select_fusion, bf16[768,1280]{1,0:T(8,128)(2,1)} %concatenate.13, bf16[128,2560]{1,0:T(8,128)(2,1)S(1)} %copy-done.14, f32[128]{0:T(128)S(1)} %get-tuple-element.8), kind=kOutput, calls=%fused_computation.11 | convolution fusion | flops 512163840 | bytes 4981248 | tf_op jit(solution)/shard_map/dot_general | solution.py:8
  225.8 10.8 %all-to-all-done.2 = bf16[32,5,2560]{2,1,0:T(8,128)(2,1)} async-done(((bf16[32,5,2560]{2,1,0:T(8,128)(2,1)}), bf16[32,5,2560]{2,1,0:T(8,128)(2,1)}, u32[]{:S(2)}, u32[]{:S(2)}) %all-to-all-start.2) | async-done | bytes 819232 | tf_op jit(solution)/shard_map/all_to_all | solution.py:104
  (127 shorter events, 63.5 us)
Async XLA Ops:
  7.2 141.9 %all-gather.3.cloned.1.call-start = ((), (), s32[]{:S(2)}) async-start(), calls=%async_computation.5 | async-start | bytes 10444800 | tf_op jit(solution)/shard_map/all_gather | solution.py:72
  11.1 25.7 %collective-permute-start = (bf16[48,1280]{1,0:T(8,128)(2,1)S(1)}, bf16[48,1280]{1,0:T(8,128)(2,1)S(1)}, u32[]{:S(2)}, u32[]{:S(2)}) collective-permute-start(bf16[48,1280]{1,0:T(8,128)(2,1)S(1)} %get-tuple-element.4), channel_id=1, source_target_pairs={{0,15},{1,0},{2,1},{3,2},{4,3},{5,4},{6,5},{7,6},{8,7},{9,8},{10,9... | collective-permute-start | bytes 368648 | tf_op jit(solution)/shard_map/ppermute | solution.py:39
  22.5 19.4 %collective-permute-start.7 = (bf16[48,1280]{1,0:T(8,128)(2,1)S(1)}, bf16[48,1280]{1,0:T(8,128)(2,1)S(1)}, u32[]{:S(2)}, u32[]{:S(2)}) collective-permute-start(bf16[48,1280]{1,0:T(8,128)(2,1)S(1)} %get-tuple-element.4), channel_id=1, source_target_pairs={{0,1},{1,2},{2,3},{3,4},{4,5},{5,6},{6,7},{7,8},{8,9},{9,10},{10,1... | collective-permute-start | bytes 368648 | tf_op jit(solution)/shard_map/ppermute | solution.py:38
  27.3 39.6 %all-to-all-start = ((bf16[32,5,2560]{2,1,0:T(8,128)(2,1)}), bf16[32,5,2560]{2,1,0:T(8,128)(2,1)S(1)}, u32[]{:S(2)}, u32[]{:S(2)}) async-start(bf16[32,5,2560]{2,1,0:T(8,128)(2,1)} %reshape.108), calls=%async_computation | async-start | bytes 2621440 | tf_op jit(solution)/shard_map/all_to_all | solution.py:99
  36.8 11.1 %collective-permute-start.1 = (bf16[48,1280]{1,0:T(8,128)(2,1)S(1)}, bf16[48,1280]{1,0:T(8,128)(2,1)S(1)}, u32[]{:S(2)}, u32[]{:S(2)}) collective-permute-start(bf16[48,1280]{1,0:T(8,128)(2,1)S(1)} %collective-permute-done), channel_id=1, source_target_pairs={{0,15},{1,0},{2,1},{3,2},{4,3},{5,4},{6,5},{7,6},{8,7},{9,8},{10,9... | collective-permute-start | bytes 368648 | tf_op jit(solution)/shard_map/ppermute | solution.py:39
  41.9 11.6 %collective-permute-start.8 = (bf16[48,1280]{1,0:T(8,128)(2,1)S(1)}, bf16[48,1280]{1,0:T(8,128)(2,1)S(1)}, u32[]{:S(2)}, u32[]{:S(2)}) collective-permute-start(bf16[48,1280]{1,0:T(8,128)(2,1)S(1)} %collective-permute-done.7), channel_id=1, source_target_pairs={{0,1},{1,2},{2,3},{3,4},{4,5},{5,6},{6,7},{7,8},{8,9},{9,10},{10,1... | collective-permute-start | bytes 368648 | tf_op jit(solution)/shard_map/ppermute | solution.py:38
  47.9 11.4 %collective-permute-start.2 = (bf16[48,1280]{1,0:T(8,128)(2,1)S(1)}, bf16[48,1280]{1,0:T(8,128)(2,1)}, u32[]{:S(2)}, u32[]{:S(2)}) collective-permute-start(bf16[48,1280]{1,0:T(8,128)(2,1)S(1)} %collective-permute-done.1), channel_id=1, source_target_pairs={{0,15},{1,0},{2,1},{3,2},{4,3},{5,4},{6,5},{7,6},{8,7},{9,8},{10,9... | collective-permute-start | bytes 368648 | tf_op jit(solution)/shard_map/ppermute | solution.py:39
  53.5 11.4 %collective-permute-start.9 = (bf16[48,1280]{1,0:T(8,128)(2,1)S(1)}, bf16[48,1280]{1,0:T(8,128)(2,1)S(1)}, u32[]{:S(2)}, u32[]{:S(2)}) collective-permute-start(bf16[48,1280]{1,0:T(8,128)(2,1)S(1)} %collective-permute-done.8), channel_id=1, source_target_pairs={{0,1},{1,2},{2,3},{3,4},{4,5},{5,6},{6,7},{7,8},{8,9},{9,10},{10,1... | collective-permute-start | bytes 368648 | tf_op jit(solution)/shard_map/ppermute | solution.py:38
  59.2 16.7 %collective-permute-start.3 = (bf16[48,1280]{1,0:T(8,128)(2,1)}, bf16[48,1280]{1,0:T(8,128)(2,1)}, u32[]{:S(2)}, u32[]{:S(2)}) collective-permute-start(bf16[48,1280]{1,0:T(8,128)(2,1)} %collective-permute-done.2), channel_id=1, source_target_pairs={{0,15},{1,0},{2,1},{3,2},{4,3},{5,4},{6,5},{7,6},{8,7},{9,8},{10,9... | collective-permute-start | bytes 368648 | tf_op jit(solution)/shard_map/ppermute | solution.py:39
  65.0 31.0 %copy-start.19 = (bf16[48,1280]{1,0:T(8,128)(2,1)}, bf16[48,1280]{1,0:T(8,128)(2,1)S(1)}, u32[]{:S(2)}) copy-start(bf16[48,1280]{1,0:T(8,128)(2,1)S(1)} %collective-permute-done.9) | copy-start | bytes 368644
  65.0 16.1 %collective-permute-start.10 = (bf16[48,1280]{1,0:T(8,128)(2,1)S(1)}, bf16[48,1280]{1,0:T(8,128)(2,1)S(1)}, u32[]{:S(2)}, u32[]{:S(2)}) collective-permute-start(bf16[48,1280]{1,0:T(8,128)(2,1)S(1)} %collective-permute-done.9), channel_id=1, source_target_pairs={{0,1},{1,2},{2,3},{3,4},{4,5},{5,6},{6,7},{7,8},{8,9},{9,10},{10,1... | collective-permute-start | bytes 368648 | tf_op jit(solution)/shard_map/ppermute | solution.py:38
  66.9 29.0 %all-to-all-start.1 = ((bf16[32,5,2560]{2,1,0:T(8,128)(2,1)}), bf16[32,5,2560]{2,1,0:T(8,128)(2,1)S(1)}, u32[]{:S(2)}, u32[]{:S(2)}) async-start(bf16[32,5,2560]{2,1,0:T(8,128)(2,1)} %reshape.110), calls=%async_computation.1 | async-start | bytes 2621440 | tf_op jit(solution)/shard_map/all_to_all | solution.py:98
  74.3 166.4 %reduce-scatter.2.cloned.1.call-start = ((), (), s32[]{:S(2)}) async-start(), calls=%async_computation.4 | async-start | bytes 4177920 | tf_op jit(solution)/shard_map/reduce_scatter | solution.py:124
  75.9 11.3 %collective-permute-start.4 = (bf16[48,1280]{1,0:T(8,128)(2,1)}, bf16[48,1280]{1,0:T(8,128)(2,1)}, u32[]{:S(2)}, u32[]{:S(2)}) collective-permute-start(bf16[48,1280]{1,0:T(8,128)(2,1)} %collective-permute-done.3), channel_id=1, source_target_pairs={{0,15},{1,0},{2,1},{3,2},{4,3},{5,4},{6,5},{7,6},{8,7},{9,8},{10,9... | collective-permute-start | bytes 368648 | tf_op jit(solution)/shard_map/ppermute | solution.py:39
  81.1 11.8 %collective-permute-start.11 = (bf16[48,1280]{1,0:T(8,128)(2,1)S(1)}, bf16[48,1280]{1,0:T(8,128)(2,1)}, u32[]{:S(2)}, u32[]{:S(2)}) collective-permute-start(bf16[48,1280]{1,0:T(8,128)(2,1)S(1)} %collective-permute-done.10), channel_id=1, source_target_pairs={{0,1},{1,2},{2,3},{3,4},{4,5},{5,6},{6,7},{7,8},{8,9},{9,10},{10,1... | collective-permute-start | bytes 368648 | tf_op jit(solution)/shard_map/ppermute | solution.py:38
  87.3 76.2 %collective-permute-start.5 = (bf16[48,1280]{1,0:T(8,128)(2,1)}, bf16[48,1280]{1,0:T(8,128)(2,1)}, u32[]{:S(2)}, u32[]{:S(2)}) collective-permute-start(bf16[48,1280]{1,0:T(8,128)(2,1)} %collective-permute-done.4), channel_id=1, source_target_pairs={{0,15},{1,0},{2,1},{3,2},{4,3},{5,4},{6,5},{7,6},{8,7},{9,8},{10,9... | collective-permute-start | bytes 368648 | tf_op jit(solution)/shard_map/ppermute | solution.py:39
  92.9 73.8 %collective-permute-start.12 = (bf16[48,1280]{1,0:T(8,128)(2,1)}, bf16[48,1280]{1,0:T(8,128)(2,1)}, u32[]{:S(2)}, u32[]{:S(2)}) collective-permute-start(bf16[48,1280]{1,0:T(8,128)(2,1)} %collective-permute-done.11), channel_id=1, source_target_pairs={{0,1},{1,2},{2,3},{3,4},{4,5},{5,6},{6,7},{7,8},{8,9},{9,10},{10,1... | collective-permute-start | bytes 368648 | tf_op jit(solution)/shard_map/ppermute | solution.py:38
  161.8 28.8 %copy-start.18 = (bf16[48,1280]{1,0:T(8,128)(2,1)S(1)}, bf16[48,1280]{1,0:T(8,128)(2,1)}, u32[]{:S(2)}) copy-start(bf16[48,1280]{1,0:T(8,128)(2,1)} %copy-done.17) | copy-start | bytes 368644
  161.8 29.5 %copy-start.16 = (bf16[48,1280]{1,0:T(8,128)(2,1)S(1)}, bf16[48,1280]{1,0:T(8,128)(2,1)}, u32[]{:S(2)}) copy-start(bf16[48,1280]{1,0:T(8,128)(2,1)} %copy-done.15) | copy-start | bytes 368644
  163.4 13.4 %collective-permute-start.6 = (bf16[48,1280]{1,0:T(8,128)(2,1)}, bf16[48,1280]{1,0:T(8,128)(2,1)S(1)}, u32[]{:S(2)}, u32[]{:S(2)}) collective-permute-start(bf16[48,1280]{1,0:T(8,128)(2,1)} %collective-permute-done.5), channel_id=1, source_target_pairs={{0,15},{1,0},{2,1},{3,2},{4,3},{5,4},{6,5},{7,6},{8,7},{9,8},{10,9... | collective-permute-start | bytes 368648 | tf_op jit(solution)/shard_map/ppermute | solution.py:39
  166.7 8.2 %collective-permute-start.13 = (bf16[48,1280]{1,0:T(8,128)(2,1)}, bf16[48,1280]{1,0:T(8,128)(2,1)S(1)}, u32[]{:S(2)}, u32[]{:S(2)}) collective-permute-start(bf16[48,1280]{1,0:T(8,128)(2,1)} %collective-permute-done.12), channel_id=1, source_target_pairs={{0,1},{1,2},{2,3},{3,4},{4,5},{5,6},{6,7},{7,8},{8,9},{9,10},{10,1... | collective-permute-start | bytes 368648 | tf_op jit(solution)/shard_map/ppermute | solution.py:38
  174.9 8.5 %collective-permute-start.14 = (bf16[48,640]{1,0:T(8,128)(2,1)S(1)}, bf16[48,640]{1,0:T(8,128)(2,1)S(1)}, u32[]{:S(2)}, u32[]{:S(2)}) collective-permute-start(bf16[48,640]{1,0:T(8,128)(2,1)S(1)} %slice.41), channel_id=1, source_target_pairs={{0,1},{1,2},{2,3},{3,4},{4,5},{5,6},{6,7},{7,8},{8,9},{9,10},{10,1... | collective-permute-start | bytes 184328 | tf_op jit(solution)/shard_map/ppermute | solution.py:44
  176.8 8.0 %collective-permute-start.15 = (bf16[48,640]{1,0:T(8,128)(2,1)S(1)}, bf16[48,640]{1,0:T(8,128)(2,1)S(1)}, u32[]{:S(2)}, u32[]{:S(2)}) collective-permute-start(bf16[48,640]{1,0:T(8,128)(2,1)S(1)} %slice.42), channel_id=1, source_target_pairs={{0,15},{1,0},{2,1},{3,2},{4,3},{5,4},{6,5},{7,6},{8,7},{9,8},{10,9... | collective-permute-start | bytes 184328 | tf_op jit(solution)/shard_map/ppermute | solution.py:45
  211.0 25.7 %all-to-all-start.2 = ((bf16[32,5,2560]{2,1,0:T(8,128)(2,1)}), bf16[32,5,2560]{2,1,0:T(8,128)(2,1)}, u32[]{:S(2)}, u32[]{:S(2)}) async-start(bf16[32,5,2560]{2,1,0:T(8,128)(2,1)} %reshape.112), calls=%async_computation.2 | async-start | bytes 2621440 | tf_op jit(solution)/shard_map/all_to_all | solution.py:104
  (22 other events, 232.6 us)
Sparse Core Ops, SparseCore 0:
  11.2 137.9 all-gather.2
  161.9 78.7 reduce-scatter.1

commit v10 on v6

--- a/solution.py
+++ b/solution.py
@@ -63,10 +63,10 @@
     upstream = cotangent.astype(jnp.float32)
     q_home = (upstream * share_home[:, None]).astype(jnp.bfloat16)
     q_away = (upstream * share_away[:, None]).astype(jnp.bfloat16)
-    pair = lax.all_gather(jnp.stack([w_gate[0], w_up[0]]), "replica", axis=0, tiled=False)
+    pair = lax.all_gather(jnp.stack([w_gate[0], w_up[0]]), "replica", axis=1, tiled=False)
     down_full = ring_gather(w_down[0], "replica")
-    gate_w = pair[:, 0].reshape(-1, w_gate.shape[2])
-    up_w = pair[:, 1].reshape(-1, w_up.shape[2])
+    gate_w = pair[0].reshape(-1, w_gate.shape[2])
+    up_w = pair[1].reshape(-1, w_up.shape[2])
     down_w = down_full.reshape(-1, down_full.shape[2])
     target = partner[:, 0]
     onehot_rows = (target[:, None] == jnp.arange(expert_count, dtype=jnp.int32)[None, :]).astype(

time: 250 us -> 250 us (level)
  matrix products: 21 us -> 29.1 us
  local copies, waits for them, and re-layouts: 36 us -> 31.7 us
  waiting for transfers between devices: 81 us -> 78.5 us
    slice x1 -> x0, local copies, waits for them, and re-layouts: 3.77 us -> none  [local(): up_w = pair[:, 1].reshape(-1, w_up.shape[2])]
    all_to_all x1, waiting for transfers between devices: 12.9 us -> 9.8 us  [local(): lax.all_to_all(grad_there.astype(jnp.bfloat16).reshape(expert_count, item...]
    unnamed x60 -> x50, local copies, waits for them, and re-layouts: 17.4 us -> 19 us
  transfers between devices with their start and end apart: 21 -> 21, of which waited for: 9 -> 9; matrix products, arithmetic and copies ran while one was open for 20% -> 21% of each run, Pallas kernels for 0% -> 0%
where the time goes in v10:
time: 250 us; the launch traced here: 249 us
  starting transfers between devices  86.1 us (34%)
  waiting for transfers between devices  78.5 us (31%)
  local copies, waits for them, and re-layouts  31.7 us (13%)
  matrix products  29.1 us (12%)
  between operations  15.3 us (6%)
  other arithmetic  8.26 us (3%)
    ppermute x7, starting transfers between devices, ring_gather(): l = lax.ppermute(l, axis, left)  43.9 us
    ppermute x7, waiting for transfers between devices, ring_gather(): l = lax.ppermute(l, axis, left)  33.3 us
    reduce_scatter x1, waiting for transfers between devices, local(): lax.psum_scatter((lax.dot_general(hidden_home, q_home, contract, preferre...  23.4 us
    unnamed x50, local copies, waits for them, and re-layouts  19 us
    dot_general x6, matrix products, against_rows(): lax.dot_general(left, matrix, (((1,), (1,)), ((), ())), preferred_element...  13.9 us
    ppermute x7, starting transfers between devices, ring_gather(): r = lax.ppermute(r, axis, right)  13.4 us
    all_to_all x1, waiting for transfers between devices, local(): lax.all_to_all(grad_there.astype(jnp.bfloat16).reshape(expert_count, item...  9.8 us
    all_to_all x1, starting transfers between devices, local(): lax.all_to_all(send_x, 'expert', split_axis=0, concat_axis=0, tiled=True)  7.61 us
  transfers between devices with their start and end apart: 21, of which 9 were waited for; matrix products, arithmetic and copies ran while one was open for 21% of the time, Pallas kernels for 0%

profile of v10, /device:TPU:6, one launch (start us, length us, event | category | flops | bytes accessed | tf_op | source)
XLA Modules:
  0.0 248.9 jit_solution(14564975344544554799)
XLA Ops:
  9.2 11.4 %collective-permute-start = (bf16[48,2560]{1,0:T(8,128)(2,1)}, bf16[48,2560]{1,0:T(8,128)(2,1)}, u32[]{:S(2)}, u32[]{:S(2)}) collective-permute-start(bf16[48,2560]{1,0:T(8,128)(2,1)} %bitcast.78), channel_id=1, source_target_pairs={{0,15},{1,0},{2,1},{3,2},{4,3},{5,4},{6,5},{7,6},{8,7},{9,8},{10,9... | collective-permute-start | bytes 737288 | tf_op jit(solution)/shard_map/ppermute | solution.py:39
  26.6 7.6 %all-to-all-start.1 = ((bf16[32,5,2560]{2,1,0:T(8,128)(2,1)}), bf16[32,5,2560]{2,1,0:T(8,128)(2,1)S(1)}, u32[]{:S(2)}, u32[]{:S(2)}) async-start(bf16[32,5,2560]{2,1,0:T(8,128)(2,1)} %reshape.128), calls=%async_computation.1 | async-start | bytes 2621440 | tf_op jit(solution)/shard_map/all_to_all | solution.py:91
  38.6 5.1 %collective-permute-start.1 = (bf16[48,2560]{1,0:T(8,128)(2,1)}, bf16[48,2560]{1,0:T(8,128)(2,1)S(1)}, u32[]{:S(2)}, u32[]{:S(2)}) collective-permute-start(bf16[48,2560]{1,0:T(8,128)(2,1)} %collective-permute-done), channel_id=1, source_target_pairs={{0,15},{1,0},{2,1},{3,2},{4,3},{5,4},{6,5},{7,6},{8,7},{9,8},{10,9... | collective-permute-start | bytes 737288 | tf_op jit(solution)/shard_map/ppermute | solution.py:39
  47.4 7.9 %collective-permute-done.1 = bf16[48,2560]{1,0:T(8,128)(2,1)S(1)} collective-permute-done((bf16[48,2560]{1,0:T(8,128)(2,1)}, bf16[48,2560]{1,0:T(8,128)(2,1)S(1)}, u32[]{:S(2)}, u32[]{:S(2)}) %collective-permute-start.1) | collective-permute-done | bytes 245792 | tf_op jit(solution)/shard_map/ppermute | solution.py:39
  55.3 5.5 %collective-permute-start.2 = (bf16[48,2560]{1,0:T(8,128)(2,1)S(1)}, bf16[48,2560]{1,0:T(8,128)(2,1)}, u32[]{:S(2)}, u32[]{:S(2)}) collective-permute-start(bf16[48,2560]{1,0:T(8,128)(2,1)S(1)} %collective-permute-done.1), channel_id=1, source_target_pairs={{0,15},{1,0},{2,1},{3,2},{4,3},{5,4},{6,5},{7,6},{8,7},{9,8},{10,9... | collective-permute-start | bytes 737288 | tf_op jit(solution)/shard_map/ppermute | solution.py:39
  62.8 7.5 %all-to-all-start = ((bf16[32,5,2560]{2,1,0:T(8,128)(2,1)}), bf16[32,5,2560]{2,1,0:T(8,128)(2,1)}, u32[]{:S(2)}, u32[]{:S(2)}) async-start(bf16[32,5,2560]{2,1,0:T(8,128)(2,1)} %reshape.126), calls=%async_computation | async-start | bytes 2621440 | tf_op jit(solution)/shard_map/all_to_all | solution.py:92
  71.9 5.7 %collective-permute-start.3 = (bf16[48,2560]{1,0:T(8,128)(2,1)}, bf16[48,2560]{1,0:T(8,128)(2,1)}, u32[]{:S(2)}, u32[]{:S(2)}) collective-permute-start(bf16[48,2560]{1,0:T(8,128)(2,1)} %collective-permute-done.2), channel_id=1, source_target_pairs={{0,15},{1,0},{2,1},{3,2},{4,3},{5,4},{6,5},{7,6},{8,7},{9,8},{10,9... | collective-permute-start | bytes 737288 | tf_op jit(solution)/shard_map/ppermute | solution.py:39
  81.6 6.8 %all-to-all-done = bf16[32,5,2560]{2,1,0:T(8,128)(2,1)} async-done(((bf16[32,5,2560]{2,1,0:T(8,128)(2,1)}), bf16[32,5,2560]{2,1,0:T(8,128)(2,1)}, u32[]{:S(2)}, u32[]{:S(2)}) %all-to-all-start) | async-done | bytes 819232 | tf_op jit(solution)/shard_map/all_to_all | solution.py:92
  89.9 5.1 %collective-permute-start.4 = (bf16[48,2560]{1,0:T(8,128)(2,1)}, bf16[48,2560]{1,0:T(8,128)(2,1)S(1)}, u32[]{:S(2)}, u32[]{:S(2)}) collective-permute-start(bf16[48,2560]{1,0:T(8,128)(2,1)} %collective-permute-done.3), channel_id=1, source_target_pairs={{0,15},{1,0},{2,1},{3,2},{4,3},{5,4},{6,5},{7,6},{8,7},{9,8},{10,9... | collective-permute-start | bytes 737288 | tf_op jit(solution)/shard_map/ppermute | solution.py:39
  98.6 7.9 %collective-permute-done.4 = bf16[48,2560]{1,0:T(8,128)(2,1)S(1)} collective-permute-done((bf16[48,2560]{1,0:T(8,128)(2,1)}, bf16[48,2560]{1,0:T(8,128)(2,1)S(1)}, u32[]{:S(2)}, u32[]{:S(2)}) %collective-permute-start.4) | collective-permute-done | bytes 245792 | tf_op jit(solution)/shard_map/ppermute | solution.py:39
  106.6 5.5 %collective-permute-start.5 = (bf16[48,2560]{1,0:T(8,128)(2,1)S(1)}, bf16[48,2560]{1,0:T(8,128)(2,1)S(1)}, u32[]{:S(2)}, u32[]{:S(2)}) collective-permute-start(bf16[48,2560]{1,0:T(8,128)(2,1)S(1)} %collective-permute-done.4), channel_id=1, source_target_pairs={{0,15},{1,0},{2,1},{3,2},{4,3},{5,4},{6,5},{7,6},{8,7},{9,8},{10,9... | collective-permute-start | bytes 737288 | tf_op jit(solution)/shard_map/ppermute | solution.py:39
  114.7 8.4 %collective-permute-done.5 = bf16[48,2560]{1,0:T(8,128)(2,1)S(1)} collective-permute-done((bf16[48,2560]{1,0:T(8,128)(2,1)S(1)}, bf16[48,2560]{1,0:T(8,128)(2,1)S(1)}, u32[]{:S(2)}, u32[]{:S(2)}) %collective-permute-start.5) | collective-permute-done | bytes 245792 | tf_op jit(solution)/shard_map/ppermute | solution.py:39
  123.1 5.6 %collective-permute-start.6 = (bf16[48,2560]{1,0:T(8,128)(2,1)S(1)}, bf16[48,2560]{1,0:T(8,128)(2,1)S(1)}, u32[]{:S(2)}, u32[]{:S(2)}) collective-permute-start(bf16[48,2560]{1,0:T(8,128)(2,1)S(1)} %collective-permute-done.5), channel_id=1, source_target_pairs={{0,15},{1,0},{2,1},{3,2},{4,3},{5,4},{6,5},{7,6},{8,7},{9,8},{10,9... | collective-permute-start | bytes 737288 | tf_op jit(solution)/shard_map/ppermute | solution.py:39
  131.4 8.2 %collective-permute-done.6 = bf16[48,2560]{1,0:T(8,128)(2,1)S(1)} collective-permute-done((bf16[48,2560]{1,0:T(8,128)(2,1)S(1)}, bf16[48,2560]{1,0:T(8,128)(2,1)S(1)}, u32[]{:S(2)}, u32[]{:S(2)}) %collective-permute-start.6) | collective-permute-done | bytes 245792 | tf_op jit(solution)/shard_map/ppermute | solution.py:39
  139.5 5.6 %collective-permute-start.15 = (bf16[48,1280]{1,0:T(8,128)(2,1)S(1)}, bf16[48,1280]{1,0:T(8,128)(2,1)S(1)}, u32[]{:S(2)}, u32[]{:S(2)}) collective-permute-start(bf16[48,1280]{1,0:T(8,128)(2,1)S(1)} %slice.31), channel_id=1, source_target_pairs={{0,15},{1,0},{2,1},{3,2},{4,3},{5,4},{6,5},{7,6},{8,7},{9,8},{10,9... | collective-permute-start | bytes 368648 | tf_op jit(solution)/shard_map/ppermute | solution.py:45
  148.0 5.2 %collective-permute-done.14 = bf16[48,1280]{1,0:T(8,128)(2,1)S(1)} collective-permute-done((bf16[48,1280]{1,0:T(8,128)(2,1)S(1)}, bf16[48,1280]{1,0:T(8,128)(2,1)S(1)}, u32[]{:S(2)}, u32[]{:S(2)}) %collective-permute-start.14) | collective-permute-done | bytes 122912 | tf_op jit(solution)/shard_map/ppermute | solution.py:44
  158.1 3.0 %fusion.11 = f32[128,768]{1,0:T(8,128)S(1)} fusion(bf16[128,2560]{1,0:T(8,128)(2,1)S(1)} %copy-done, bf16[2,2560,768]{2,1,0:T(8,128)(2,1)} %all-gather.3.cloned.1.call-done), kind=kOutput, calls=%fused_computation.24 | convolution fusion | flops 503316480 | bytes 4980736 | tf_op jit(solution)/shard_map/dot_general | solution.py:15
  165.1 3.1 %add_convert_fusion = bf16[768,2560]{1,0:T(8,128)(2,1)} fusion(f32[768,2560]{1,0:T(8,128)S(1)} %fusion.16, bf16[160,2560]{1,0:T(8,128)(2,1)S(1)} %reshape.127, f32[160,768]{1,0:T(8,128)S(1)} %fusion.2, f32[160,768]{1,0:T(8,128)S(1)} %fusion.5), kind=kOutput, calls=%fused_computation.1 | convolution fusion | flops 633815040 | bytes 13598720 | tf_op jit(solution)/shard_map/dot_general | solution.py:120
  175.6 4.8 %gather_fusion = bf16[16,48,2560]{2,1,0:T(8,128)(2,1)} fusion(bf16[16,48,2560]{2,1,0:T(8,128)(2,1)} %bitcast_dynamic-update-slice_fusion, s32[1024]{0:T(1024)S(1)} %pad_clamp_fusion), kind=kCustom, calls=%fused_computation | custom fusion | bytes 7864384 | tf_op jit(solution)/shard_map/jit(_take)/gather | solution.py:49
  191.9 5.9 %all-to-all-start.2 = ((bf16[32,5,2560]{2,1,0:T(8,128)(2,1)}), bf16[32,5,2560]{2,1,0:T(8,128)(2,1)S(1)}, u32[]{:S(2)}, u32[]{:S(2)}) async-start(bf16[32,5,2560]{2,1,0:T(8,128)(2,1)} %reshape.130), calls=%async_computation.2 | async-start | bytes 2621440 | tf_op jit(solution)/shard_map/all_to_all | solution.py:97
  197.8 3.5 %fusion.6 = f32[128,2560]{1,0:T(8,128)S(1)} fusion(bf16[2,2560,768]{2,1,0:T(8,128)(2,1)} %all-gather.3.cloned.1.call-done, f32[128,768]{1,0:T(8,128)S(1)} %copy-done.4, f32[128,768]{1,0:T(8,128)S(1)} %fusion.18, f32[128,768]{1,0:T(8,128)S(1)} %copy-done.6), kind=kOutput, calls=%fused_computation.17 | convolution fusion | flops 504299520 | bytes 6422528 | tf_op jit(solution)/shard_map/dot_general | solution.py:8
  201.3 4.7 %convolution_add_fusion.2 = f32[128,2560]{1,0:T(8,128)} fusion(f32[128,2560]{1,0:T(8,128)S(1)} %fusion.6, bf16[2,2560,768]{2,1,0:T(8,128)(2,1)} %all-gather.3.cloned.1.call-done, f32[128,768]{1,0:T(8,128)S(1)} %fusion.18, f32[128,768]{1,0:T(8,128)S(1)} %copy-done.4), kind=kOutput, calls=%fused_computation.8 | convolution fusion | flops 504233984 | bytes 7340032 | tf_op jit(solution)/shard_map/dot_general | solution.py:8
  206.0 9.8 %all-to-all-done.2 = bf16[32,5,2560]{2,1,0:T(8,128)(2,1)S(1)} async-done(((bf16[32,5,2560]{2,1,0:T(8,128)(2,1)}), bf16[32,5,2560]{2,1,0:T(8,128)(2,1)S(1)}, u32[]{:S(2)}, u32[]{:S(2)}) %all-to-all-start.2) | async-done | bytes 819232 | tf_op jit(solution)/shard_map/all_to_all | solution.py:97
  218.7 23.4 %reduce-scatter.2.cloned.1.call-done = bf16[48,2560]{1,0:T(8,128)(2,1)} async-done(((bf16[768,2560]{1,0:T(8,128)(2,1)}), bf16[48,2560]{1,0:T(8,128)(2,1)}) %reduce-scatter.2.cloned.1.call-update) | async-done | bytes 245776 | tf_op jit(solution)/shard_map/reduce_scatter | solution.py:117
  (112 shorter events, 66.6 us)
Async XLA Ops:
  7.2 27.1 %copy-start.13 = (s32[128,2]{0,1:T(2,128)S(1)}, s32[128,2]{0,1:T(2,128)}, u32[]{:S(2)}) copy-start(s32[128,2]{0,1:T(2,128)} %param.11) | copy-start | bytes 3076
  7.2 27.7 %copy-start.2 = (bf16[128,2560]{1,0:T(8,128)(2,1)S(1)}, bf16[128,2560]{1,0:T(8,128)(2,1)}, u32[]{:S(2)}) copy-start(bf16[128,2560]{1,0:T(8,128)(2,1)} %param.9) | copy-start | bytes 1966084
  7.2 148.1 %all-gather.3.cloned.1.call-start = ((), (), s32[]{:S(2)}) async-start(), calls=%async_computation.5 | async-start | bytes 8355840 | tf_op jit(solution)/shard_map/all_gather | solution.py:66
  9.2 29.4 %collective-permute-start = (bf16[48,2560]{1,0:T(8,128)(2,1)}, bf16[48,2560]{1,0:T(8,128)(2,1)}, u32[]{:S(2)}, u32[]{:S(2)}) collective-permute-start(bf16[48,2560]{1,0:T(8,128)(2,1)} %bitcast.78), channel_id=1, source_target_pairs={{0,15},{1,0},{2,1},{3,2},{4,3},{5,4},{6,5},{7,6},{8,7},{9,8},{10,9... | collective-permute-start | bytes 737288 | tf_op jit(solution)/shard_map/ppermute | solution.py:39
  20.7 23.1 %collective-permute-start.7 = (bf16[48,2560]{1,0:T(8,128)(2,1)}, bf16[48,2560]{1,0:T(8,128)(2,1)}, u32[]{:S(2)}, u32[]{:S(2)}) collective-permute-start(bf16[48,2560]{1,0:T(8,128)(2,1)} %bitcast.79), channel_id=1, source_target_pairs={{0,1},{1,2},{2,3},{3,4},{4,5},{5,6},{6,7},{7,8},{8,9},{9,10},{10,1... | collective-permute-start | bytes 737288 | tf_op jit(solution)/shard_map/ppermute | solution.py:38
  26.6 36.2 %all-to-all-start.1 = ((bf16[32,5,2560]{2,1,0:T(8,128)(2,1)}), bf16[32,5,2560]{2,1,0:T(8,128)(2,1)S(1)}, u32[]{:S(2)}, u32[]{:S(2)}) async-start(bf16[32,5,2560]{2,1,0:T(8,128)(2,1)} %reshape.128), calls=%async_computation.1 | async-start | bytes 2621440 | tf_op jit(solution)/shard_map/all_to_all | solution.py:91
  38.6 16.7 %collective-permute-start.1 = (bf16[48,2560]{1,0:T(8,128)(2,1)}, bf16[48,2560]{1,0:T(8,128)(2,1)S(1)}, u32[]{:S(2)}, u32[]{:S(2)}) collective-permute-start(bf16[48,2560]{1,0:T(8,128)(2,1)} %collective-permute-done), channel_id=1, source_target_pairs={{0,15},{1,0},{2,1},{3,2},{4,3},{5,4},{6,5},{7,6},{8,7},{9,8},{10,9... | collective-permute-start | bytes 737288 | tf_op jit(solution)/shard_map/ppermute | solution.py:39
  43.8 17.1 %collective-permute-start.8 = (bf16[48,2560]{1,0:T(8,128)(2,1)}, bf16[48,2560]{1,0:T(8,128)(2,1)S(1)}, u32[]{:S(2)}, u32[]{:S(2)}) collective-permute-start(bf16[48,2560]{1,0:T(8,128)(2,1)} %collective-permute-done.7), channel_id=1, source_target_pairs={{0,1},{1,2},{2,3},{3,4},{4,5},{5,6},{6,7},{7,8},{8,9},{9,10},{10,1... | collective-permute-start | bytes 737288 | tf_op jit(solution)/shard_map/ppermute | solution.py:38
  55.3 16.6 %collective-permute-start.2 = (bf16[48,2560]{1,0:T(8,128)(2,1)S(1)}, bf16[48,2560]{1,0:T(8,128)(2,1)}, u32[]{:S(2)}, u32[]{:S(2)}) collective-permute-start(bf16[48,2560]{1,0:T(8,128)(2,1)S(1)} %collective-permute-done.1), channel_id=1, source_target_pairs={{0,15},{1,0},{2,1},{3,2},{4,3},{5,4},{6,5},{7,6},{8,7},{9,8},{10,9... | collective-permute-start | bytes 737288 | tf_op jit(solution)/shard_map/ppermute | solution.py:39
  60.8 18.7 %copy-start.9 = (bf16[48,2560]{1,0:T(8,128)(2,1)}, bf16[48,2560]{1,0:T(8,128)(2,1)S(1)}, u32[]{:S(2)}) copy-start(bf16[48,2560]{1,0:T(8,128)(2,1)S(1)} %collective-permute-done.8) | copy-start | bytes 737284
  60.9 16.8 %collective-permute-start.9 = (bf16[48,2560]{1,0:T(8,128)(2,1)S(1)}, bf16[48,2560]{1,0:T(8,128)(2,1)}, u32[]{:S(2)}, u32[]{:S(2)}) collective-permute-start(bf16[48,2560]{1,0:T(8,128)(2,1)S(1)} %collective-permute-done.8), channel_id=1, source_target_pairs={{0,1},{1,2},{2,3},{3,4},{4,5},{5,6},{6,7},{7,8},{8,9},{9,10},{10,1... | collective-permute-start | bytes 737288 | tf_op jit(solution)/shard_map/ppermute | solution.py:38
  62.8 25.6 %all-to-all-start = ((bf16[32,5,2560]{2,1,0:T(8,128)(2,1)}), bf16[32,5,2560]{2,1,0:T(8,128)(2,1)}, u32[]{:S(2)}, u32[]{:S(2)}) async-start(bf16[32,5,2560]{2,1,0:T(8,128)(2,1)} %reshape.126), calls=%async_computation | async-start | bytes 2621440 | tf_op jit(solution)/shard_map/all_to_all | solution.py:92
  70.2 171.8 %reduce-scatter.2.cloned.1.call-start = ((), (), s32[]{:S(2)}) async-start(), calls=%async_computation.4 | async-start | bytes 4177920 | tf_op jit(solution)/shard_map/reduce_scatter | solution.py:117
  71.9 18.0 %collective-permute-start.3 = (bf16[48,2560]{1,0:T(8,128)(2,1)}, bf16[48,2560]{1,0:T(8,128)(2,1)}, u32[]{:S(2)}, u32[]{:S(2)}) collective-permute-start(bf16[48,2560]{1,0:T(8,128)(2,1)} %collective-permute-done.2), channel_id=1, source_target_pairs={{0,15},{1,0},{2,1},{3,2},{4,3},{5,4},{6,5},{7,6},{8,7},{9,8},{10,9... | collective-permute-start | bytes 737288 | tf_op jit(solution)/shard_map/ppermute | solution.py:39
  77.6 17.4 %collective-permute-start.10 = (bf16[48,2560]{1,0:T(8,128)(2,1)}, bf16[48,2560]{1,0:T(8,128)(2,1)}, u32[]{:S(2)}, u32[]{:S(2)}) collective-permute-start(bf16[48,2560]{1,0:T(8,128)(2,1)} %collective-permute-done.9), channel_id=1, source_target_pairs={{0,1},{1,2},{2,3},{3,4},{4,5},{5,6},{6,7},{7,8},{8,9},{9,10},{10,1... | collective-permute-start | bytes 737288 | tf_op jit(solution)/shard_map/ppermute | solution.py:38
  89.9 16.7 %collective-permute-start.4 = (bf16[48,2560]{1,0:T(8,128)(2,1)}, bf16[48,2560]{1,0:T(8,128)(2,1)S(1)}, u32[]{:S(2)}, u32[]{:S(2)}) collective-permute-start(bf16[48,2560]{1,0:T(8,128)(2,1)} %collective-permute-done.3), channel_id=1, source_target_pairs={{0,15},{1,0},{2,1},{3,2},{4,3},{5,4},{6,5},{7,6},{8,7},{9,8},{10,9... | collective-permute-start | bytes 737288 | tf_op jit(solution)/shard_map/ppermute | solution.py:39
  95.0 17.0 %collective-permute-start.11 = (bf16[48,2560]{1,0:T(8,128)(2,1)}, bf16[48,2560]{1,0:T(8,128)(2,1)S(1)}, u32[]{:S(2)}, u32[]{:S(2)}) collective-permute-start(bf16[48,2560]{1,0:T(8,128)(2,1)} %collective-permute-done.10), channel_id=1, source_target_pairs={{0,1},{1,2},{2,3},{3,4},{4,5},{5,6},{6,7},{7,8},{8,9},{9,10},{10,1... | collective-permute-start | bytes 737288 | tf_op jit(solution)/shard_map/ppermute | solution.py:38
  106.6 16.5 %collective-permute-start.5 = (bf16[48,2560]{1,0:T(8,128)(2,1)S(1)}, bf16[48,2560]{1,0:T(8,128)(2,1)S(1)}, u32[]{:S(2)}, u32[]{:S(2)}) collective-permute-start(bf16[48,2560]{1,0:T(8,128)(2,1)S(1)} %collective-permute-done.4), channel_id=1, source_target_pairs={{0,15},{1,0},{2,1},{3,2},{4,3},{5,4},{6,5},{7,6},{8,7},{9,8},{10,9... | collective-permute-start | bytes 737288 | tf_op jit(solution)/shard_map/ppermute | solution.py:39
  112.1 16.6 %collective-permute-start.12 = (bf16[48,2560]{1,0:T(8,128)(2,1)S(1)}, bf16[48,2560]{1,0:T(8,128)(2,1)S(1)}, u32[]{:S(2)}, u32[]{:S(2)}) collective-permute-start(bf16[48,2560]{1,0:T(8,128)(2,1)S(1)} %collective-permute-done.11), channel_id=1, source_target_pairs={{0,1},{1,2},{2,3},{3,4},{4,5},{5,6},{6,7},{7,8},{8,9},{9,10},{10,1... | collective-permute-start | bytes 737288 | tf_op jit(solution)/shard_map/ppermute | solution.py:38
  123.1 16.4 %collective-permute-start.6 = (bf16[48,2560]{1,0:T(8,128)(2,1)S(1)}, bf16[48,2560]{1,0:T(8,128)(2,1)S(1)}, u32[]{:S(2)}, u32[]{:S(2)}) collective-permute-start(bf16[48,2560]{1,0:T(8,128)(2,1)S(1)} %collective-permute-done.5), channel_id=1, source_target_pairs={{0,15},{1,0},{2,1},{3,2},{4,3},{5,4},{6,5},{7,6},{8,7},{9,8},{10,9... | collective-permute-start | bytes 737288 | tf_op jit(solution)/shard_map/ppermute | solution.py:39
  128.7 16.4 %collective-permute-start.13 = (bf16[48,2560]{1,0:T(8,128)(2,1)S(1)}, bf16[48,2560]{1,0:T(8,128)(2,1)S(1)}, u32[]{:S(2)}, u32[]{:S(2)}) collective-permute-start(bf16[48,2560]{1,0:T(8,128)(2,1)S(1)} %collective-permute-done.12), channel_id=1, source_target_pairs={{0,1},{1,2},{2,3},{3,4},{4,5},{5,6},{6,7},{7,8},{8,9},{9,10},{10,1... | collective-permute-start | bytes 737288 | tf_op jit(solution)/shard_map/ppermute | solution.py:38
  139.5 8.5 %collective-permute-start.15 = (bf16[48,1280]{1,0:T(8,128)(2,1)S(1)}, bf16[48,1280]{1,0:T(8,128)(2,1)S(1)}, u32[]{:S(2)}, u32[]{:S(2)}) collective-permute-start(bf16[48,1280]{1,0:T(8,128)(2,1)S(1)} %slice.31), channel_id=1, source_target_pairs={{0,15},{1,0},{2,1},{3,2},{4,3},{5,4},{6,5},{7,6},{8,7},{9,8},{10,9... | collective-permute-start | bytes 368648 | tf_op jit(solution)/shard_map/ppermute | solution.py:45
  145.2 8.0 %collective-permute-start.14 = (bf16[48,1280]{1,0:T(8,128)(2,1)S(1)}, bf16[48,1280]{1,0:T(8,128)(2,1)S(1)}, u32[]{:S(2)}, u32[]{:S(2)}) collective-permute-start(bf16[48,1280]{1,0:T(8,128)(2,1)S(1)} %slice.30), channel_id=1, source_target_pairs={{0,1},{1,2},{2,3},{3,4},{4,5},{5,6},{6,7},{7,8},{8,9},{9,10},{10,1... | collective-permute-start | bytes 368648 | tf_op jit(solution)/shard_map/ppermute | solution.py:44
  191.9 23.9 %all-to-all-start.2 = ((bf16[32,5,2560]{2,1,0:T(8,128)(2,1)}), bf16[32,5,2560]{2,1,0:T(8,128)(2,1)S(1)}, u32[]{:S(2)}, u32[]{:S(2)}) async-start(bf16[32,5,2560]{2,1,0:T(8,128)(2,1)} %reshape.130), calls=%async_computation.2 | async-start | bytes 2621440 | tf_op jit(solution)/shard_map/all_to_all | solution.py:97
  (15 other events, 81.0 us)
Sparse Core Ops, SparseCore 0:
  10.7 136.6 all-gather.2
  168.4 73.6 reduce-scatter.1

commit v11 on v8

--- a/solution.py
+++ b/solution.py
@@ -63,11 +63,18 @@
     upstream = cotangent.astype(jnp.float32)
     q_home = (upstream * share_home[:, None]).astype(jnp.bfloat16)
     q_away = (upstream * share_away[:, None]).astype(jnp.bfloat16)
-    pair = lax.all_gather(jnp.stack([w_gate[0], w_up[0]]), "replica", axis=0, tiled=False)
-    down_full = ring_gather(w_down[0], "replica")
-    gate_w = pair[:, 0].reshape(-1, w_gate.shape[2])
-    up_w = pair[:, 1].reshape(-1, w_up.shape[2])
-    down_w = down_full.reshape(-1, down_full.shape[2])
+    shard_rows, hidden_units = w_gate.shape[1], w_gate.shape[2]
+    down_rows, width_down = w_down.shape[1], w_down.shape[2]
+    cut = width_down // 2
+    packed = jnp.concatenate(
+        [w_gate[0], w_up[0], w_down[0, :, :cut].reshape(-1, hidden_units)], axis=0
+    )
+    full = lax.all_gather(packed, "replica", axis=0, tiled=False)
+    down_second = ring_gather(w_down[0, :, cut:], "replica")
+    gate_w = full[:, :shard_rows].reshape(-1, hidden_units)
+    up_w = full[:, shard_rows : 2 * shard_rows].reshape(-1, hidden_units)
+    down_first = full[:, 2 * shard_rows :].reshape(-1, down_rows, cut)
+    down_w = jnp.concatenate([down_first, down_second], axis=2).reshape(-1, width_down)
     target = partner[:, 0]
     onehot_rows = (target[:, None] == jnp.arange(expert_count, dtype=jnp.int32)[None, :]).astype(
         jnp.int32

time: 256 us -> 255 us (level)
  other arithmetic: 9.39 us -> 5.77 us
    all_gather x1, waiting for transfers between devices: 0.01 us -> 50.8 us  [local(): full = lax.all_gather(packed, 'replica', axis=0, tiled=False)]
    reduce_scatter x1, waiting for transfers between devices: 22.3 us -> 0.01 us  [local(): lax.psum_scatter(lax.dot_general(hidden_all, q_in, contract, preferred_el...]
    ppermute x7, waiting for transfers between devices: 25.2 us -> 9.02 us  [ring_gather(): l = lax.ppermute(l, axis, left)]
    all_to_all x1, waiting for transfers between devices: 6.72 us -> 0.01 us  [local(): lax.all_to_all(send_x, 'expert', split_axis=0, concat_axis=0, tiled=True)]
    ppermute x7, waiting for transfers between devices: 11.1 us -> 4.54 us  [ring_gather(): r = lax.ppermute(r, axis, right)]
    unnamed x41 -> x54, local copies, waits for them, and re-layouts: 21 us -> 17.4 us
    concatenate x0 -> x1, local copies, waits for them, and re-layouts: none -> 2.65 us  [local(): jnp.concatenate([down_first, down_second], axis=2).reshape(-1, width_down)]
    gather x1, local copies, waits for them, and re-layouts: 4.8 us -> 2.24 us  [ring_gather(): return jnp.take(stacked, order, axis=0)]
  transfers between devices with their start and end apart: 20 -> 20, of which waited for: 9 -> 10; matrix products, arithmetic and copies ran while one was open for 20% -> 23% of each run, Pallas kernels for 0% -> 0%
where the time goes in v11:
time: 255 us; the launch traced here: 251 us
  starting transfers between devices  78 us (31%)
  waiting for transfers between devices  66.4 us (26%)
  local copies, waits for them, and re-layouts  41.9 us (16%)
  blocking collectives  25.7 us (10%)
  matrix products  18.1 us (7%)
  between operations  15.2 us (6%)
  other arithmetic  5.77 us (2%)
    all_gather x1, waiting for transfers between devices, local(): full = lax.all_gather(packed, 'replica', axis=0, tiled=False)  50.8 us
    ppermute x7, starting transfers between devices, ring_gather(): l = lax.ppermute(l, axis, left)  41.7 us
    all_to_all x1, blocking collectives, local(): lax.all_to_all(grad_there.astype(jnp.bfloat16).reshape(expert_count, item...  25.7 us
    unnamed x54, local copies, waits for them, and re-layouts  17.4 us
    ppermute x7, starting transfers between devices, ring_gather(): r = lax.ppermute(r, axis, right)  14.1 us
    ppermute x7, waiting for transfers between devices, ring_gather(): l = lax.ppermute(l, axis, left)  9.02 us
    dot_general x3, matrix products, against_rows(): lax.dot_general(left, matrix, (((1,), (1,)), ((), ())), preferred_element...  7.97 us
    all_to_all x1, starting transfers between devices, local(): lax.all_to_all(send_q, 'expert', split_axis=0, concat_axis=0, tiled=True)  7.61 us
  transfers between devices with their start and end apart: 20, of which 10 were waited for; matrix products, arithmetic and copies ran while one was open for 23% of the time, Pallas kernels for 0%

profile of v11, /device:TPU:6, one launch (start us, length us, event | category | flops | bytes accessed | tf_op | source)
XLA Modules:
  0.0 251.1 jit_solution(8463593617458791166)
XLA Ops:
  11.1 11.4 %collective-permute-start = (bf16[48,1280]{1,0:T(8,128)(2,1)}, bf16[48,1280]{1,0:T(8,128)(2,1)}, u32[]{:S(2)}, u32[]{:S(2)}) collective-permute-start(bf16[48,1280]{1,0:T(8,128)(2,1)} %get-tuple-element.4), channel_id=1, source_target_pairs={{0,15},{1,0},{2,1},{3,2},{4,3},{5,4},{6,5},{7,6},{8,7},{9,8},{10,9... | collective-permute-start | bytes 368648 | tf_op jit(solution)/shard_map/ppermute | solution.py:39
  27.3 7.6 %all-to-all-start = ((bf16[32,5,2560]{2,1,0:T(8,128)(2,1)}), bf16[32,5,2560]{2,1,0:T(8,128)(2,1)S(1)}, u32[]{:S(2)}, u32[]{:S(2)}) async-start(bf16[32,5,2560]{2,1,0:T(8,128)(2,1)} %reshape.105), calls=%async_computation | async-start | bytes 2621440 | tf_op jit(solution)/shard_map/all_to_all | solution.py:98
  38.7 5.1 %collective-permute-start.1 = (bf16[48,1280]{1,0:T(8,128)(2,1)}, bf16[48,1280]{1,0:T(8,128)(2,1)S(1)}, u32[]{:S(2)}, u32[]{:S(2)}) collective-permute-start(bf16[48,1280]{1,0:T(8,128)(2,1)} %collective-permute-done), channel_id=1, source_target_pairs={{0,15},{1,0},{2,1},{3,2},{4,3},{5,4},{6,5},{7,6},{8,7},{9,8},{10,9... | collective-permute-start | bytes 368648 | tf_op jit(solution)/shard_map/ppermute | solution.py:39
  47.3 2.6 %collective-permute-done.1 = bf16[48,1280]{1,0:T(8,128)(2,1)S(1)} collective-permute-done((bf16[48,1280]{1,0:T(8,128)(2,1)}, bf16[48,1280]{1,0:T(8,128)(2,1)S(1)}, u32[]{:S(2)}, u32[]{:S(2)}) %collective-permute-start.1) | collective-permute-done | bytes 122912 | tf_op jit(solution)/shard_map/ppermute | solution.py:39
  50.0 5.5 %collective-permute-start.2 = (bf16[48,1280]{1,0:T(8,128)(2,1)S(1)}, bf16[48,1280]{1,0:T(8,128)(2,1)S(1)}, u32[]{:S(2)}, u32[]{:S(2)}) collective-permute-start(bf16[48,1280]{1,0:T(8,128)(2,1)S(1)} %collective-permute-done.1), channel_id=1, source_target_pairs={{0,15},{1,0},{2,1},{3,2},{4,3},{5,4},{6,5},{7,6},{8,7},{9,8},{10,9... | collective-permute-start | bytes 368648 | tf_op jit(solution)/shard_map/ppermute | solution.py:39
  58.2 3.1 %collective-permute-done.2 = bf16[48,1280]{1,0:T(8,128)(2,1)S(1)} collective-permute-done((bf16[48,1280]{1,0:T(8,128)(2,1)S(1)}, bf16[48,1280]{1,0:T(8,128)(2,1)S(1)}, u32[]{:S(2)}, u32[]{:S(2)}) %collective-permute-start.2) | collective-permute-done | bytes 122912 | tf_op jit(solution)/shard_map/ppermute | solution.py:39
  61.3 5.6 %collective-permute-start.3 = (bf16[48,1280]{1,0:T(8,128)(2,1)S(1)}, bf16[48,1280]{1,0:T(8,128)(2,1)S(1)}, u32[]{:S(2)}, u32[]{:S(2)}) collective-permute-start(bf16[48,1280]{1,0:T(8,128)(2,1)S(1)} %collective-permute-done.2), channel_id=1, source_target_pairs={{0,15},{1,0},{2,1},{3,2},{4,3},{5,4},{6,5},{7,6},{8,7},{9,8},{10,9... | collective-permute-start | bytes 368648 | tf_op jit(solution)/shard_map/ppermute | solution.py:39
  69.0 7.4 %all-to-all-start.1 = ((bf16[32,5,2560]{2,1,0:T(8,128)(2,1)}), bf16[32,5,2560]{2,1,0:T(8,128)(2,1)S(1)}, u32[]{:S(2)}, u32[]{:S(2)}) async-start(bf16[32,5,2560]{2,1,0:T(8,128)(2,1)} %reshape.107), calls=%async_computation.1 | async-start | bytes 2621440 | tf_op jit(solution)/shard_map/all_to_all | solution.py:97
  77.1 5.1 %collective-permute-start.4 = (bf16[48,1280]{1,0:T(8,128)(2,1)S(1)}, bf16[48,1280]{1,0:T(8,128)(2,1)}, u32[]{:S(2)}, u32[]{:S(2)}) collective-permute-start(bf16[48,1280]{1,0:T(8,128)(2,1)S(1)} %collective-permute-done.3), channel_id=1, source_target_pairs={{0,15},{1,0},{2,1},{3,2},{4,3},{5,4},{6,5},{7,6},{8,7},{9,8},{10,9... | collective-permute-start | bytes 368648 | tf_op jit(solution)/shard_map/ppermute | solution.py:39
  84.8 3.3 %collective-permute-done.4 = bf16[48,1280]{1,0:T(8,128)(2,1)} collective-permute-done((bf16[48,1280]{1,0:T(8,128)(2,1)S(1)}, bf16[48,1280]{1,0:T(8,128)(2,1)}, u32[]{:S(2)}, u32[]{:S(2)}) %collective-permute-start.4) | collective-permute-done | bytes 122912 | tf_op jit(solution)/shard_map/ppermute | solution.py:39
  88.1 5.7 %collective-permute-start.5 = (bf16[48,1280]{1,0:T(8,128)(2,1)}, bf16[48,1280]{1,0:T(8,128)(2,1)}, u32[]{:S(2)}, u32[]{:S(2)}) collective-permute-start(bf16[48,1280]{1,0:T(8,128)(2,1)} %collective-permute-done.4), channel_id=1, source_target_pairs={{0,15},{1,0},{2,1},{3,2},{4,3},{5,4},{6,5},{7,6},{8,7},{9,8},{10,9... | collective-permute-start | bytes 368648 | tf_op jit(solution)/shard_map/ppermute | solution.py:39
  98.4 50.8 %all-gather.3.cloned.1.call-done = bf16[6400,768]{1,0:T(8,128)(2,1)} async-done(((bf16[400,768]{1,0:T(8,128)(2,1)}), bf16[6400,768]{1,0:T(8,128)(2,1)}) %all-gather.3.cloned.1.call-update) | async-done | bytes 9830416 | tf_op jit(solution)/shard_map/all_gather | solution.py:72
  149.1 3.9 %fusion.29 = (bf16[16,160,768]{2,1,0:T(8,128)(2,1)S(1)}, bf16[16,160,768]{2,1,0:T(8,128)(2,1)S(1)}) fusion(bf16[16,400,768]{2,1,0:T(8,128)(2,1)} %bitcast.62), kind=kLoop, calls=%fused_computation.79 | loop fusion | bytes 15728640 | tf_op jit(solution)/shard_map/slice | solution.py:75
  158.4 4.3 %convolution_convert_fusion = bf16[768,2560]{1,0:T(8,128)(2,1)} fusion(bf16[160,2560]{1,0:T(8,128)(2,1)S(1)} %copy-done.7, bf16[128,2560]{1,0:T(8,128)(2,1)S(1)} %copy-done.8, f32[288,768]{1,0:T(8,128)S(1)} %fusion.30, f32[288,768]{1,0:T(8,128)S(1)} %fusion.31), kind=kOutput, calls=%fused_computation.1 | convolution fusion | flops 1138704384 | bytes 7176192 | tf_op jit(solution)/shard_map/dot_general | solution.py:119
  164.4 3.3 %collective-permute-start.6 = (bf16[48,1280]{1,0:T(8,128)(2,1)}, bf16[48,1280]{1,0:T(8,128)(2,1)S(1)}, u32[]{:S(2)}, u32[]{:S(2)}) collective-permute-start(bf16[48,1280]{1,0:T(8,128)(2,1)} %collective-permute-done.5), channel_id=1, source_target_pairs={{0,15},{1,0},{2,1},{3,2},{4,3},{5,4},{6,5},{7,6},{8,7},{9,8},{10,9... | collective-permute-start | bytes 368648 | tf_op jit(solution)/shard_map/ppermute | solution.py:39
  167.6 2.6 %collective-permute-start.13 = (bf16[48,1280]{1,0:T(8,128)(2,1)}, bf16[48,1280]{1,0:T(8,128)(2,1)S(1)}, u32[]{:S(2)}, u32[]{:S(2)}) collective-permute-start(bf16[48,1280]{1,0:T(8,128)(2,1)} %collective-permute-done.12), channel_id=1, source_target_pairs={{0,1},{1,2},{2,3},{3,4},{4,5},{5,6},{6,7},{7,8},{8,9},{9,10},{10,1... | collective-permute-start | bytes 368648 | tf_op jit(solution)/shard_map/ppermute | solution.py:38
  171.8 4.1 %collective-permute-done.13 = bf16[48,1280]{1,0:T(8,128)(2,1)S(1)} collective-permute-done((bf16[48,1280]{1,0:T(8,128)(2,1)}, bf16[48,1280]{1,0:T(8,128)(2,1)S(1)}, u32[]{:S(2)}, u32[]{:S(2)}) %collective-permute-start.13) | collective-permute-done | bytes 122912 | tf_op jit(solution)/shard_map/ppermute | solution.py:38
  177.8 5.3 %collective-permute-start.15 = (bf16[48,640]{1,0:T(8,128)(2,1)S(1)}, bf16[48,640]{1,0:T(8,128)(2,1)S(1)}, u32[]{:S(2)}, u32[]{:S(2)}) collective-permute-start(bf16[48,640]{1,0:T(8,128)(2,1)S(1)} %slice.51), channel_id=1, source_target_pairs={{0,15},{1,0},{2,1},{3,2},{4,3},{5,4},{6,5},{7,6},{8,7},{9,8},{10,9... | collective-permute-start | bytes 184328 | tf_op jit(solution)/shard_map/ppermute | solution.py:45
  199.4 2.6 %concatenate.20 = bf16[768,1280]{1,0:T(8,128)(2,1)} reshape(bf16[16,80,768]{2,1,0:T(8,128)(2,1)S(1)} %slice.49) | data formatting | bytes 3932160 | tf_op jit(solution)/shard_map/concatenate | solution.py:77
  202.1 3.9 %fusion = f32[288,768]{1,0:T(8,128)S(1)} fusion(bf16[768,1280]{1,0:T(8,128)(2,1)} %bitcast_select_fusion, bf16[768,1280]{1,0:T(8,128)(2,1)} %concatenate.20, bf16[160,2560]{1,0:T(8,128)(2,1)} %reshape.106, bf16[128,2560]{1,0:T(8,128)(2,1)S(1)} %copy-done.8), kind=kOutput, calls=%fused_computation.3 | convolution fusion | flops 1143275520 | bytes 6291456 | tf_op jit(solution)/shard_map/dot_general | solution.py:8
  208.2 2.6 %convolution_add_fusion = f32[288,2560]{1,0:T(8,128)S(1)} fusion(f32[288,2560]{1,0:T(8,128)S(1)} %fusion.10, bf16[2560,768]{1,0:T(8,128)(2,1)S(1)} %bitcast.61, f32[288,768]{1,0:T(8,128)S(1)} %fusion, f32[288,768]{1,0:T(8,128)} %copy-done.4), kind=kOutput, calls=%fused_computation.2 | convolution fusion | flops 1134526464 | bytes 11599872 | tf_op jit(solution)/shard_map/dot_general | solution.py:8
  211.7 2.2 reshape.111
  214.0 25.7 %all_to_all.15 = bf16[32,5,2560]{2,1,0:T(8,128)(2,1)} all-to-all(bf16[32,5,2560]{2,1,0:T(8,128)(2,1)} %reshape.111), channel_id=1, replica_groups=mesh['expert'=32,'replica'=16] {'expert'}, dimensions={0} | all-to-all | bytes 1638400 | tf_op jit(solution)/shard_map/all_to_all | solution.py:105
  241.9 2.4 fusion.4
  (114 shorter events, 59.9 us)
Async XLA Ops:
  7.2 142.0 %all-gather.3.cloned.1.call-start = ((), (), s32[]{:S(2)}) async-start(), calls=%async_computation.5 | async-start | bytes 10444800 | tf_op jit(solution)/shard_map/all_gather | solution.py:72
  11.1 27.6 %collective-permute-start = (bf16[48,1280]{1,0:T(8,128)(2,1)}, bf16[48,1280]{1,0:T(8,128)(2,1)}, u32[]{:S(2)}, u32[]{:S(2)}) collective-permute-start(bf16[48,1280]{1,0:T(8,128)(2,1)} %get-tuple-element.4), channel_id=1, source_target_pairs={{0,15},{1,0},{2,1},{3,2},{4,3},{5,4},{6,5},{7,6},{8,7},{9,8},{10,9... | collective-permute-start | bytes 368648 | tf_op jit(solution)/shard_map/ppermute | solution.py:39
  22.5 21.4 %collective-permute-start.7 = (bf16[48,1280]{1,0:T(8,128)(2,1)}, bf16[48,1280]{1,0:T(8,128)(2,1)}, u32[]{:S(2)}, u32[]{:S(2)}) collective-permute-start(bf16[48,1280]{1,0:T(8,128)(2,1)} %get-tuple-element.4), channel_id=1, source_target_pairs={{0,1},{1,2},{2,3},{3,4},{4,5},{5,6},{6,7},{7,8},{8,9},{9,10},{10,1... | collective-permute-start | bytes 368648 | tf_op jit(solution)/shard_map/ppermute | solution.py:38
  27.3 41.7 %all-to-all-start = ((bf16[32,5,2560]{2,1,0:T(8,128)(2,1)}), bf16[32,5,2560]{2,1,0:T(8,128)(2,1)S(1)}, u32[]{:S(2)}, u32[]{:S(2)}) async-start(bf16[32,5,2560]{2,1,0:T(8,128)(2,1)} %reshape.105), calls=%async_computation | async-start | bytes 2621440 | tf_op jit(solution)/shard_map/all_to_all | solution.py:98
  38.7 11.3 %collective-permute-start.1 = (bf16[48,1280]{1,0:T(8,128)(2,1)}, bf16[48,1280]{1,0:T(8,128)(2,1)S(1)}, u32[]{:S(2)}, u32[]{:S(2)}) collective-permute-start(bf16[48,1280]{1,0:T(8,128)(2,1)} %collective-permute-done), channel_id=1, source_target_pairs={{0,15},{1,0},{2,1},{3,2},{4,3},{5,4},{6,5},{7,6},{8,7},{9,8},{10,9... | collective-permute-start | bytes 368648 | tf_op jit(solution)/shard_map/ppermute | solution.py:39
  43.8 11.8 %collective-permute-start.8 = (bf16[48,1280]{1,0:T(8,128)(2,1)}, bf16[48,1280]{1,0:T(8,128)(2,1)S(1)}, u32[]{:S(2)}, u32[]{:S(2)}) collective-permute-start(bf16[48,1280]{1,0:T(8,128)(2,1)} %collective-permute-done.7), channel_id=1, source_target_pairs={{0,1},{1,2},{2,3},{3,4},{4,5},{5,6},{6,7},{7,8},{8,9},{9,10},{10,1... | collective-permute-start | bytes 368648 | tf_op jit(solution)/shard_map/ppermute | solution.py:38
  50.0 11.3 %collective-permute-start.2 = (bf16[48,1280]{1,0:T(8,128)(2,1)S(1)}, bf16[48,1280]{1,0:T(8,128)(2,1)S(1)}, u32[]{:S(2)}, u32[]{:S(2)}) collective-permute-start(bf16[48,1280]{1,0:T(8,128)(2,1)S(1)} %collective-permute-done.1), channel_id=1, source_target_pairs={{0,15},{1,0},{2,1},{3,2},{4,3},{5,4},{6,5},{7,6},{8,7},{9,8},{10,9... | collective-permute-start | bytes 368648 | tf_op jit(solution)/shard_map/ppermute | solution.py:39
  55.7 11.4 %collective-permute-start.9 = (bf16[48,1280]{1,0:T(8,128)(2,1)S(1)}, bf16[48,1280]{1,0:T(8,128)(2,1)S(1)}, u32[]{:S(2)}, u32[]{:S(2)}) collective-permute-start(bf16[48,1280]{1,0:T(8,128)(2,1)S(1)} %collective-permute-done.8), channel_id=1, source_target_pairs={{0,1},{1,2},{2,3},{3,4},{4,5},{5,6},{6,7},{7,8},{8,9},{9,10},{10,1... | collective-permute-start | bytes 368648 | tf_op jit(solution)/shard_map/ppermute | solution.py:38
  61.3 15.8 %collective-permute-start.3 = (bf16[48,1280]{1,0:T(8,128)(2,1)S(1)}, bf16[48,1280]{1,0:T(8,128)(2,1)S(1)}, u32[]{:S(2)}, u32[]{:S(2)}) collective-permute-start(bf16[48,1280]{1,0:T(8,128)(2,1)S(1)} %collective-permute-done.2), channel_id=1, source_target_pairs={{0,15},{1,0},{2,1},{3,2},{4,3},{5,4},{6,5},{7,6},{8,7},{9,8},{10,9... | collective-permute-start | bytes 368648 | tf_op jit(solution)/shard_map/ppermute | solution.py:39
  67.0 30.0 %copy-start.12 = (bf16[48,1280]{1,0:T(8,128)(2,1)}, bf16[48,1280]{1,0:T(8,128)(2,1)S(1)}, u32[]{:S(2)}) copy-start(bf16[48,1280]{1,0:T(8,128)(2,1)S(1)} %collective-permute-done.9) | copy-start | bytes 368644
  67.0 15.2 %collective-permute-start.10 = (bf16[48,1280]{1,0:T(8,128)(2,1)S(1)}, bf16[48,1280]{1,0:T(8,128)(2,1)S(1)}, u32[]{:S(2)}, u32[]{:S(2)}) collective-permute-start(bf16[48,1280]{1,0:T(8,128)(2,1)S(1)} %collective-permute-done.9), channel_id=1, source_target_pairs={{0,1},{1,2},{2,3},{3,4},{4,5},{5,6},{6,7},{7,8},{8,9},{9,10},{10,1... | collective-permute-start | bytes 368648 | tf_op jit(solution)/shard_map/ppermute | solution.py:38
  69.0 28.1 %all-to-all-start.1 = ((bf16[32,5,2560]{2,1,0:T(8,128)(2,1)}), bf16[32,5,2560]{2,1,0:T(8,128)(2,1)S(1)}, u32[]{:S(2)}, u32[]{:S(2)}) async-start(bf16[32,5,2560]{2,1,0:T(8,128)(2,1)} %reshape.107), calls=%async_computation.1 | async-start | bytes 2621440 | tf_op jit(solution)/shard_map/all_to_all | solution.py:97
  76.4 167.9 %reduce-scatter.2.cloned.1.call-start = ((), (), s32[]{:S(2)}) async-start(), calls=%async_computation.4 | async-start | bytes 4177920 | tf_op jit(solution)/shard_map/reduce_scatter | solution.py:118
  77.1 11.0 %collective-permute-start.4 = (bf16[48,1280]{1,0:T(8,128)(2,1)S(1)}, bf16[48,1280]{1,0:T(8,128)(2,1)}, u32[]{:S(2)}, u32[]{:S(2)}) collective-permute-start(bf16[48,1280]{1,0:T(8,128)(2,1)S(1)} %collective-permute-done.3), channel_id=1, source_target_pairs={{0,15},{1,0},{2,1},{3,2},{4,3},{5,4},{6,5},{7,6},{8,7},{9,8},{10,9... | collective-permute-start | bytes 368648 | tf_op jit(solution)/shard_map/ppermute | solution.py:39
  82.3 11.7 %collective-permute-start.11 = (bf16[48,1280]{1,0:T(8,128)(2,1)S(1)}, bf16[48,1280]{1,0:T(8,128)(2,1)}, u32[]{:S(2)}, u32[]{:S(2)}) collective-permute-start(bf16[48,1280]{1,0:T(8,128)(2,1)S(1)} %collective-permute-done.10), channel_id=1, source_target_pairs={{0,1},{1,2},{2,3},{3,4},{4,5},{5,6},{6,7},{7,8},{8,9},{9,10},{10,1... | collective-permute-start | bytes 368648 | tf_op jit(solution)/shard_map/ppermute | solution.py:38
  88.1 76.2 %collective-permute-start.5 = (bf16[48,1280]{1,0:T(8,128)(2,1)}, bf16[48,1280]{1,0:T(8,128)(2,1)}, u32[]{:S(2)}, u32[]{:S(2)}) collective-permute-start(bf16[48,1280]{1,0:T(8,128)(2,1)} %collective-permute-done.4), channel_id=1, source_target_pairs={{0,15},{1,0},{2,1},{3,2},{4,3},{5,4},{6,5},{7,6},{8,7},{9,8},{10,9... | collective-permute-start | bytes 368648 | tf_op jit(solution)/shard_map/ppermute | solution.py:39
  94.0 73.7 %collective-permute-start.12 = (bf16[48,1280]{1,0:T(8,128)(2,1)}, bf16[48,1280]{1,0:T(8,128)(2,1)}, u32[]{:S(2)}, u32[]{:S(2)}) collective-permute-start(bf16[48,1280]{1,0:T(8,128)(2,1)} %collective-permute-done.11), channel_id=1, source_target_pairs={{0,1},{1,2},{2,3},{3,4},{4,5},{5,6},{6,7},{7,8},{8,9},{9,10},{10,1... | collective-permute-start | bytes 368648 | tf_op jit(solution)/shard_map/ppermute | solution.py:38
  154.9 51.0 %copy-start.4 = (f32[288,768]{1,0:T(8,128)}, f32[288,768]{1,0:T(8,128)S(1)}, u32[]{:S(2)}) copy-start(f32[288,768]{1,0:T(8,128)S(1)} %fusion.31) | copy-start | bytes 2654212
  162.7 28.2 %copy-start.13 = (bf16[48,1280]{1,0:T(8,128)(2,1)S(1)}, bf16[48,1280]{1,0:T(8,128)(2,1)}, u32[]{:S(2)}) copy-start(bf16[48,1280]{1,0:T(8,128)(2,1)} %copy-done.12) | copy-start | bytes 368644
  162.7 28.8 %copy-start.11 = (bf16[48,1280]{1,0:T(8,128)(2,1)S(1)}, bf16[48,1280]{1,0:T(8,128)(2,1)}, u32[]{:S(2)}) copy-start(bf16[48,1280]{1,0:T(8,128)(2,1)} %copy-done.10) | copy-start | bytes 368644
  164.4 13.4 %collective-permute-start.6 = (bf16[48,1280]{1,0:T(8,128)(2,1)}, bf16[48,1280]{1,0:T(8,128)(2,1)S(1)}, u32[]{:S(2)}, u32[]{:S(2)}) collective-permute-start(bf16[48,1280]{1,0:T(8,128)(2,1)} %collective-permute-done.5), channel_id=1, source_target_pairs={{0,15},{1,0},{2,1},{3,2},{4,3},{5,4},{6,5},{7,6},{8,7},{9,8},{10,9... | collective-permute-start | bytes 368648 | tf_op jit(solution)/shard_map/ppermute | solution.py:39
  167.6 8.2 %collective-permute-start.13 = (bf16[48,1280]{1,0:T(8,128)(2,1)}, bf16[48,1280]{1,0:T(8,128)(2,1)S(1)}, u32[]{:S(2)}, u32[]{:S(2)}) collective-permute-start(bf16[48,1280]{1,0:T(8,128)(2,1)} %collective-permute-done.12), channel_id=1, source_target_pairs={{0,1},{1,2},{2,3},{3,4},{4,5},{5,6},{6,7},{7,8},{8,9},{9,10},{10,1... | collective-permute-start | bytes 368648 | tf_op jit(solution)/shard_map/ppermute | solution.py:38
  175.8 8.5 %collective-permute-start.14 = (bf16[48,640]{1,0:T(8,128)(2,1)S(1)}, bf16[48,640]{1,0:T(8,128)(2,1)S(1)}, u32[]{:S(2)}, u32[]{:S(2)}) collective-permute-start(bf16[48,640]{1,0:T(8,128)(2,1)S(1)} %slice.50), channel_id=1, source_target_pairs={{0,1},{1,2},{2,3},{3,4},{4,5},{5,6},{6,7},{7,8},{8,9},{9,10},{10,1... | collective-permute-start | bytes 184328 | tf_op jit(solution)/shard_map/ppermute | solution.py:44
  177.8 8.0 %collective-permute-start.15 = (bf16[48,640]{1,0:T(8,128)(2,1)S(1)}, bf16[48,640]{1,0:T(8,128)(2,1)S(1)}, u32[]{:S(2)}, u32[]{:S(2)}) collective-permute-start(bf16[48,640]{1,0:T(8,128)(2,1)S(1)} %slice.51), channel_id=1, source_target_pairs={{0,15},{1,0},{2,1},{3,2},{4,3},{5,4},{6,5},{7,6},{8,7},{9,8},{10,9... | collective-permute-start | bytes 184328 | tf_op jit(solution)/shard_map/ppermute | solution.py:45
  (16 other events, 140.9 us)
Sparse Core Ops, SparseCore 0:
  11.2 137.9 all-gather.2
  162.8 78.6 reduce-scatter.1
